TPU v7x, 128 devices: a whole 4x4x4 slice. The times are simulated.
128 devices in a mesh: col: 8 (over y, z_hi), pair: 16 (over x, z_lo, core).
Axes of the slice: x: 4, y: 4, z: 4 (z_hi: 2, z_lo: 2; z = z_hi * 2 + z_lo), core: 2. Of those that a mesh axis runs over, the one named last changes fastest.
Arguments:
- integrals: bfloat16 [512, 128, 128], P('pair', 'col'), may hold values from -6 to 6
- pno_energy: float32 [512, 128], P('pair'), may hold values from 0.5 to 4
- shift: float32 [512], P('pair'), may hold values from 0.5 to 2
- intersections: bfloat16 [512, 128, 128, 128], P('pair', 'col'), may hold values from -0.09375 to 0.09375
- links: int32 [512, 128], P('pair', 'col'), may hold values from 0 to 63
- counts: int32 [512], P('pair'), may hold values from 1 to 128, as said below
- column_of: int32 [512], P('pair'), may hold values from 0 to 63
Outputs:
- amplitudes: float32 [512, 128, 128], P('pair', 'col')
- pair_energy: float32 [512], P('pair')
Inputs may be any that keep to these rules, and one draw needn't show every extreme that they name: Pair p couples through its first counts[p] slots; later slots are unused.
All inputs are finite; a program needn't handle non-finite values.
Results may differ from a plain program's by a relative error of at most 0.0012.
Values may be sent and summed in bfloat16 or wider, within the bound.
No kernel may reach another device: no remote copies, remote signals or barrier semaphores. Data moves between devices by JAX's collectives and lax.ppermute only.
A program may use at most 192 MiB of HBM per device.

v0:
```python
import jax
import jax.numpy as jnp
from jax import lax
from jax.sharding import PartitionSpec as P

COL_DEV = 8
SWEEPS = 3


def per_device(integrals, pno_energy, shift, intersections, links, counts, column_of):
    pair_dev = integrals.shape[0]
    row_count = integrals.shape[1]
    width = integrals.shape[2]
    slot_dev = intersections.shape[1]
    col_size = lax.axis_size("col")
    ncol_all = COL_DEV * col_size
    rank = lax.axis_index("col")
    row_energy = lax.dynamic_slice_in_dim(pno_energy, rank * row_count, row_count, 1)
    denom = row_energy[:, :, None] + pno_energy[:, None, :] + shift[:, None, None]
    kfloat = integrals.astype(jnp.float32)
    amplitudes = -kfloat / denom
    one_hot = (jnp.arange(ncol_all, dtype=jnp.int32)[:, None] == column_of[None, :]).astype(
        jnp.float32
    )
    own_tiles, own_links = (intersections, links)
    slot_ids = rank * slot_dev + jnp.arange(slot_dev, dtype=jnp.int32)
    own_live = (slot_ids[None, :] < counts[:, None]).astype(jnp.float32)
    for sweep in range(SWEEPS):
        contrib = jnp.dot(
            one_hot,
            amplitudes.reshape(pair_dev, row_count * width),
            precision=lax.Precision.HIGHEST,
        )
        contrib = contrib.reshape(ncol_all, row_count, width)
        totals = lax.psum(contrib, "pair")
        colamp = lax.all_gather(totals.astype(jnp.bfloat16), "col", axis=1, tiled=True)
        selected = colamp[own_links]
        left = jnp.einsum(
            "pmab,pmbc->pmac", own_tiles, selected, preferred_element_type=jnp.float32
        ).astype(jnp.bfloat16)
        right = jnp.einsum("pmac,pmdc->pmad", left, own_tiles, preferred_element_type=jnp.float32)
        partial_sum = jnp.sum(right * own_live[:, :, None, None], axis=1)
        coupled = lax.psum_scatter(partial_sum, "col", scatter_dimension=1, tiled=True)
        amplitudes = -(kfloat + coupled) / denom
    pair_energy = lax.psum(jnp.sum(kfloat * amplitudes, axis=(1, 2)), "col")
    return (amplitudes, pair_energy)


def solution(mesh):
    placed = (
        P("pair", "col", None),
        P("pair", None),
        P("pair"),
        P("pair", "col", None, None),
        P("pair", "col"),
        P("pair"),
        P("pair"),
    )
    return jax.shard_map(
        per_device,
        mesh=mesh,
        in_specs=placed,
        out_specs=(P("pair", "col", None), P("pair")),
        check_vma=False,
    )
```

profile of v0, /device:TPU:0, one launch (start us, length us, event | category | flops | bytes accessed | tf_op | source)
XLA Modules:
  0.0 745.8 jit_solution(13268401989379443307)
XLA Ops:
  8.0 1.1 fusion.18
  9.1 1.1 fusion.32
  10.3 62.5 %all-reduce.3 = bf16[64,16,128]{2,0,1:T(8,128)(2,1)} all-reduce(f32[64,16,128]{2,0,1:T(8,128)S(1)} %fusion.32), channel_id=1, replica_groups=mesh['col'=8,'pair'=16] {'pair'}, use_global_device_ids=true, to_apply=%region_0.0 | all-reduce | flops 131072 | bytes 786432 | tf_op jit(solution)/shard_map/psum | solution.py:35
  74.4 52.9 %all-gather.4.cloned.1.call-done = bf16[64,128,128]{2,0,1:T(8,128)(2,1)} async-done(((bf16[64,16,128]{2,0,1:T(8,128)(2,1)}), bf16[64,128,128]{2,0,1:T(8,128)(2,1)}) %all-gather.4.cloned.1.call-update) | async-done | bytes 2097168 | tf_op jit(solution)/shard_map/all_gather | solution.py:36
  127.3 2.9 copy.18
  130.2 13.9 %gather_fusion = bf16[512,128,128]{2,1,0:T(8,128)(2,1)} fusion(bf16[64,128,128]{2,1,0:T(8,128)(2,1)S(1)} %copy.18, s32[1024]{0:T(1024)S(1)} %pad_clamp_fusion), kind=kCustom, calls=%fused_computation | custom fusion | bytes 33556480 | tf_op jit(solution)/shard_map/gather | solution.py:37
  144.2 29.2 %multiply_reduce_fusion.2 = f32[32,128,128]{2,1,0:T(8,128)} fusion(f32[32,16]{1,0:T(8,128)S(1)} %compare_convert_fusion, bf16[32,16,128,128]{3,2,1,0:T(8,128)(2,1)} %param.10, bf16[32,16,128,128]{3,2,1,0:T(8,128)(2,1)} %bitcast.57), kind=kOutput, calls=%fused_computation.5 | convolution fusion | flops 4319608832 | bytes 35653632 | tf_op jit(solution)/shard_map/pmac,pmdc->pmad/dot_general | solution.py:41
  173.5 74.4 %reduce-scatter.4.cloned.1.call-done = f32[32,16,128]{2,1,0:T(8,128)} async-done(((f32[32,128,128]{2,1,0:T(8,128)}), f32[32,16,128]{2,1,0:T(8,128)}) %reduce-scatter.4.cloned.1.call-update) | async-done | bytes 262160 | tf_op jit(solution)/shard_map/reduce_scatter | solution.py:43
  247.9 1.1 fusion.20
  249.5 59.6 %all-reduce.4 = bf16[64,16,128]{2,0,1:T(8,128)(2,1)} all-reduce(f32[64,16,128]{2,0,1:T(8,128)S(1)} %fusion.29), channel_id=1, replica_groups=mesh['col'=8,'pair'=16] {'pair'}, use_global_device_ids=true, to_apply=%region_3.0 | all-reduce | flops 131072 | bytes 786432 | tf_op jit(solution)/shard_map/psum | solution.py:35
  309.3 51.7 %all-gather.6.cloned.1.call-done = bf16[64,128,128]{2,0,1:T(8,128)(2,1)} async-done(((bf16[64,16,128]{2,0,1:T(8,128)(2,1)}), bf16[64,128,128]{2,0,1:T(8,128)(2,1)}) %all-gather.6.cloned.1.call-update) | async-done | bytes 2097168 | tf_op jit(solution)/shard_map/all_gather | solution.py:36
  361.0 2.9 copy.22
  364.0 13.9 %gather_fusion.1 = bf16[512,128,128]{2,1,0:T(8,128)(2,1)} fusion(bf16[64,128,128]{2,1,0:T(8,128)(2,1)S(1)} %copy.22, s32[1024]{0:T(1024)S(1)} %pad_clamp_fusion), kind=kCustom, calls=%fused_computation.1 | custom fusion | bytes 33556480 | tf_op jit(solution)/shard_map/gather | solution.py:37
  377.9 29.2 %multiply_reduce_fusion.1 = f32[32,128,128]{2,1,0:T(8,128)} fusion(f32[32,16]{1,0:T(8,128)S(1)} %compare_convert_fusion, bf16[32,16,128,128]{3,2,1,0:T(8,128)(2,1)} %param.10, bf16[32,16,128,128]{3,2,1,0:T(8,128)(2,1)} %bitcast.58), kind=kOutput, calls=%fused_computation.4 | convolution fusion | flops 4319608832 | bytes 35653632 | tf_op jit(solution)/shard_map/pmac,pmdc->pmad/dot_general | solution.py:41
  407.2 74.4 %reduce-scatter.6.cloned.1.call-done = f32[32,16,128]{2,1,0:T(8,128)} async-done(((f32[32,128,128]{2,1,0:T(8,128)}), f32[32,16,128]{2,1,0:T(8,128)}) %reduce-scatter.6.cloned.1.call-update) | async-done | bytes 262160 | tf_op jit(solution)/shard_map/reduce_scatter | solution.py:43
  481.5 1.1 fusion.22
  483.2 59.6 %all-reduce.5 = bf16[64,16,128]{2,0,1:T(8,128)(2,1)} all-reduce(f32[64,16,128]{2,0,1:T(8,128)S(1)} %fusion.26), channel_id=1, replica_groups=mesh['col'=8,'pair'=16] {'pair'}, use_global_device_ids=true, to_apply=%region_6.0 | all-reduce | flops 131072 | bytes 786432 | tf_op jit(solution)/shard_map/psum | solution.py:35
  543.1 51.6 %all-gather.8.cloned.1.call-done = bf16[64,128,128]{2,0,1:T(8,128)(2,1)} async-done(((bf16[64,16,128]{2,0,1:T(8,128)(2,1)}), bf16[64,128,128]{2,0,1:T(8,128)(2,1)}) %all-gather.8.cloned.1.call-update) | async-done | bytes 2097168 | tf_op jit(solution)/shard_map/all_gather | solution.py:36
  594.7 2.9 copy.26
  597.6 13.9 %gather_fusion.2 = bf16[512,128,128]{2,1,0:T(8,128)(2,1)} fusion(bf16[64,128,128]{2,1,0:T(8,128)(2,1)S(1)} %copy.26, s32[1024]{0:T(1024)S(1)} %pad_clamp_fusion), kind=kCustom, calls=%fused_computation.2 | custom fusion | bytes 33556480 | tf_op jit(solution)/shard_map/gather | solution.py:37
  611.5 29.2 %multiply_reduce_fusion = f32[32,128,128]{2,1,0:T(8,128)} fusion(f32[32,16]{1,0:T(8,128)S(1)} %compare_convert_fusion, bf16[32,16,128,128]{3,2,1,0:T(8,128)(2,1)} %param.10, bf16[32,16,128,128]{3,2,1,0:T(8,128)(2,1)} %bitcast.56), kind=kOutput, calls=%fused_computation.3 | convolution fusion | flops 4319608832 | bytes 35653632 | tf_op jit(solution)/shard_map/pmac,pmdc->pmad/dot_general | solution.py:41
  640.8 74.5 %reduce-scatter.8.cloned.1.call-done = f32[32,16,128]{2,1,0:T(8,128)} async-done(((f32[32,128,128]{2,1,0:T(8,128)}), f32[32,16,128]{2,1,0:T(8,128)}) %reduce-scatter.8.cloned.1.call-update) | async-done | bytes 262160 | tf_op jit(solution)/shard_map/reduce_scatter | solution.py:43
  715.3 2.2 fusion.25
  717.4 21.5 %psum.31 = f32[32]{0:T(128)} all-reduce(f32[32]{0:T(128)S(1)} %get-tuple-element.2), channel_id=1, replica_groups=mesh['col'=8,'pair'=16] {'col'}, use_global_device_ids=true, to_apply=%region_10.0 | all-reduce | flops 32 | bytes 256 | tf_op jit(solution)/shard_map/psum | solution.py:45
  (29 shorter events, 4.1 us)
Async XLA Ops:
  7.2 120.1 %all-gather.4.cloned.1.call-start = ((), (), s32[]{:S(2)}) async-start(), calls=%async_computation.3 | async-start | bytes 2359296 | tf_op jit(solution)/shard_map/all_gather | solution.py:36
  72.8 175.1 %reduce-scatter.4.cloned.1.call-start = ((), (), s32[]{:S(2)}) async-start(), calls=%async_computation.4 | async-start | bytes 2359296 | tf_op jit(solution)/shard_map/reduce_scatter | solution.py:43
  144.1 103.7 %copy-start = (bf16[32,16,128]{2,1,0:T(8,128)(2,1)S(1)}, bf16[32,16,128]{2,1,0:T(8,128)(2,1)}, u32[]{:S(2)}) copy-start(bf16[32,16,128]{2,1,0:T(8,128)(2,1)} %param.7) | copy-start | bytes 393220
  144.1 103.7 %copy-start.1 = (f32[32,128]{1,0:T(8,128)S(1)}, f32[32,128]{1,0:T(8,128)}, u32[]{:S(2)}) copy-start(f32[32,128]{1,0:T(8,128)} %param.8) | copy-start | bytes 49156
  144.1 103.7 %copy-start.2 = (f32[32]{0:T(128)S(1)}, f32[32]{0:T(128)}, u32[]{:S(2)}) copy-start(f32[32]{0:T(128)} %param.9) | copy-start | bytes 388
  144.2 104.9 %copy-start.3 = (s32[32]{0:T(128)S(1)}, s32[32]{0:T(128)}, u32[]{:S(2)}) copy-start(s32[32]{0:T(128)} %param.13) | copy-start | bytes 388
  173.4 187.6 %all-gather.6.cloned.1.call-start = ((), (), s32[]{:S(2)}) async-start(), calls=%async_computation.5 | async-start | bytes 2359296 | tf_op jit(solution)/shard_map/all_gather | solution.py:36
  309.1 172.4 %reduce-scatter.6.cloned.1.call-start = ((), (), s32[]{:S(2)}) async-start(), calls=%async_computation.6 | async-start | bytes 2359296 | tf_op jit(solution)/shard_map/reduce_scatter | solution.py:43
  407.1 187.6 %all-gather.8.cloned.1.call-start = ((), (), s32[]{:S(2)}) async-start(), calls=%async_computation.7 | async-start | bytes 2359296 | tf_op jit(solution)/shard_map/all_gather | solution.py:36
  542.8 172.5 %reduce-scatter.8.cloned.1.call-start = ((), (), s32[]{:S(2)}) async-start(), calls=%async_computation.8 | async-start | bytes 2359296 | tf_op jit(solution)/shard_map/reduce_scatter | solution.py:43
Sparse Core Ops, SparseCore 0:
  72.9 54.3 all-gather.3
  173.5 74.2 reduce-scatter.3
  309.2 51.7 all-gather.5
  407.2 74.2 reduce-scatter.5
  542.9 51.7 all-gather.7
  640.9 74.3 reduce-scatter.7
where the time goes:
time: 746 us
  waiting for transfers between devices  380 us (51%)
  blocking collectives  203 us (27%)
  matrix products  89.7 us (12%)
  local copies, waits for them, and re-layouts  51.5 us (7%)
  between operations  14.2 us (2%)
    reduce_scatter x3, waiting for transfers between devices, per_device(): lax.psum_scatter(partial_sum, 'col', scatter_dimension=1, tiled=True)  223 us
    psum x3, blocking collectives, per_device(): totals = lax.psum(contrib, 'pair')  182 us
    all_gather x3, waiting for transfers between devices, per_device(): lax.all_gather(totals.astype(jnp.bfloat16), 'col', axis=1, tiled=True)  156 us
    dot_general x3, matrix products, per_device(): jnp.einsum('pmac,pmdc->pmad', left, own_tiles, preferred_element_type=jnp...  87.6 us
    gather x3, local copies, waits for them, and re-layouts, per_device(): selected = colamp[own_links]  41.7 us
    psum x1, blocking collectives, per_device(): pair_energy = lax.psum(jnp.sum(kfloat * amplitudes, axis=(1, 2)), 'col')  21.5 us
  transfers between devices with their start and end apart: 6, of which 6 were waited for; matrix products, arithmetic and copies ran while one was open for 0% of the time, Pallas kernels for 0%

commit v1 on v0

v1 whole, which is shorter than its diff:
```python
import functools

import jax
import jax.numpy as jnp
from jax import lax
from jax.experimental import pallas as pl
from jax.experimental.pallas import tpu as pltpu
from jax.sharding import PartitionSpec as P

COL_DEV = 8
SWEEPS = 3
PAIR_BLOCK = 4


def couple_kernel(slot_dev, links_ref, nlive_ref, tiles_ref, colamp_ref, out_ref):
    step = pl.program_id(0)
    width = tiles_ref.shape[-1]
    for q in range(PAIR_BLOCK):
        pair = step * PAIR_BLOCK + q
        live = nlive_ref[pair]
        acc = jnp.zeros((width, width), jnp.float32)
        for m in range(slot_dev):
            tile = tiles_ref[q, m]
            block = colamp_ref[links_ref[pair * slot_dev + m]]
            left = jnp.dot(tile, block, preferred_element_type=jnp.float32)
            left = jnp.where(m < live, left, 0.0).astype(jnp.bfloat16)
            acc = acc + lax.dot_general(
                left, tile, (((1,), (1,)), ((), ())), preferred_element_type=jnp.float32
            )
        out_ref[:, q] = acc.reshape(out_ref.shape[0], out_ref.shape[2], width)


def couple(tiles, colamp, links, nlive, col_size):
    pair_dev, slot_dev, width, _ = tiles.shape
    ncol = colamp.shape[0]
    rows = width // col_size
    grid_spec = pltpu.PrefetchScalarGridSpec(
        num_scalar_prefetch=2,
        grid=(pair_dev // PAIR_BLOCK,),
        in_specs=[
            pl.BlockSpec((PAIR_BLOCK, slot_dev, width, width), lambda i, *_: (i, 0, 0, 0)),
            pl.BlockSpec((ncol, width, width), lambda i, *_: (0, 0, 0)),
        ],
        out_specs=pl.BlockSpec(
            (col_size, PAIR_BLOCK, rows, width), lambda i, *_: (0, i, 0, 0)
        ),
    )
    flops = 4 * pair_dev * slot_dev * width**3
    return pl.pallas_call(
        functools.partial(couple_kernel, slot_dev),
        grid_spec=grid_spec,
        out_shape=jax.ShapeDtypeStruct((col_size, pair_dev, rows, width), jnp.float32),
        compiler_params=pltpu.CompilerParams(vmem_limit_bytes=48 * 1024 * 1024),
        cost_estimate=pl.CostEstimate(
            flops=flops,
            bytes_accessed=tiles.size * 2 + colamp.size * 2 + pair_dev * width * width * 4,
            transcendentals=0,
        ),
    )(links.reshape(-1), nlive, tiles, colamp)


def column_amplitudes(amplitudes, one_hot, pair_size, col_size):
    pair_dev, rows, width = amplitudes.shape
    ncol = one_hot.shape[0]
    contrib = jnp.dot(
        one_hot, amplitudes.reshape(pair_dev, rows * width), precision=lax.Precision.HIGHEST
    )
    per = ncol // pair_size
    parts = lax.all_to_all(contrib, "pair", 0, 0, tiled=True)
    mine = jnp.sum(parts.reshape(pair_size, per, rows * width), axis=0)
    mine = mine.astype(jnp.bfloat16).reshape(1, per, rows, width)
    everyone = pair_size * col_size
    sent = jnp.broadcast_to(mine, (everyone, per, rows, width))
    got = lax.all_to_all(sent, ("pair", "col"), 0, 0, tiled=True)
    got = got.reshape(pair_size, col_size, per, rows, width)
    return got.transpose(0, 2, 1, 3, 4).reshape(ncol, col_size * rows, width)


def per_device(integrals, pno_energy, shift, intersections, links, counts, column_of):
    pair_dev = integrals.shape[0]
    row_count = integrals.shape[1]
    slot_dev = intersections.shape[1]
    col_size = lax.axis_size("col")
    pair_size = lax.axis_size("pair")
    ncol_all = COL_DEV * col_size
    rank = lax.axis_index("col")
    row_energy = lax.dynamic_slice_in_dim(pno_energy, rank * row_count, row_count, 1)
    denom = row_energy[:, :, None] + pno_energy[:, None, :] + shift[:, None, None]
    kfloat = integrals.astype(jnp.float32)
    amplitudes = -kfloat / denom
    one_hot = (jnp.arange(ncol_all, dtype=jnp.int32)[:, None] == column_of[None, :]).astype(
        jnp.float32
    )
    nlive = jnp.clip(counts - rank * slot_dev, 0, slot_dev).astype(jnp.int32)
    for sweep in range(SWEEPS):
        colamp = column_amplitudes(amplitudes, one_hot, pair_size, col_size)
        partial = couple(intersections, colamp, links, nlive, col_size)
        parts = lax.all_to_all(partial, "col", 0, 0, tiled=True)
        coupled = jnp.sum(parts, axis=0)
        amplitudes = -(kfloat + coupled) / denom
    pair_energy = lax.psum(jnp.sum(kfloat * amplitudes, axis=(1, 2)), "col")
    return (amplitudes, pair_energy)


def solution(mesh):
    placed = (
        P("pair", "col", None),
        P("pair", None),
        P("pair"),
        P("pair", "col", None, None),
        P("pair", "col"),
        P("pair"),
        P("pair"),
    )
    return jax.shard_map(
        per_device,
        mesh=mesh,
        in_specs=placed,
        out_specs=(P("pair", "col", None), P("pair")),
        check_vma=False,
    )
```

time: 746 us -> 353 us (0.47)
  waiting for transfers between devices: 380 us -> 28.9 us
  matrix products: 89.7 us -> 1.9 us
  Pallas kernels: 0 us -> 72.4 us
  local copies, waits for them, and re-layouts: 51.5 us -> 7.49 us
  blocking collectives: 203 us -> 229 us
  between operations: 14.2 us -> 0.85 us
  starting transfers between devices: 0.65 us -> 8.59 us
    reduce_scatter x3 -> x0, waiting for transfers between devices: 223 us -> none  [per_device(): lax.psum_scatter(partial_sum, 'col', scatter_dimension=1, tiled=True)]
    all_to_all x0 -> x8, blocking collectives: none -> 207 us  [the longest x3 95.6 us: per_device(): parts = lax.all_to_all(partial, 'col', 0, 0, tiled=True)]
    psum x3 -> x0, blocking collectives: 182 us -> none  [per_device(): totals = lax.psum(contrib, 'pair')]
    all_gather x3 -> x0, waiting for transfers between devices: 156 us -> none  [per_device(): lax.all_gather(totals.astype(jnp.bfloat16), 'col', axis=1, tiled=True)]
    dot_general x6 -> x3, matrix products: 89.7 us -> 1.9 us  [column_amplitudes(): jnp.dot(one_hot, amplitudes.reshape(pair_dev, rows * width), precision=la...]
    pallas_call x0 -> x3, Pallas kernels: none -> 72.4 us  [couple(): pl.pallas_call(functools.partial(couple_kernel, slot_dev), grid_spec=grid...]
    gather x3 -> x0, local copies, waits for them, and re-layouts: 41.7 us -> none  [per_device(): selected = colamp[own_links]]
    all_to_all x0 -> x1, waiting for transfers between devices: none -> 28.9 us  [column_amplitudes(): got = lax.all_to_all(sent, ('pair', 'col'), 0, 0, tiled=True)]
  transfers between devices with their start and end apart: 6 -> 1, of which waited for: 6 -> 1; matrix products, arithmetic and copies ran while one was open for 0% -> 0% of each run, Pallas kernels for 0% -> 0%
where the time goes in v1:
time: 353 us; the launch traced here: 352 us
  blocking collectives  229 us (65%)
  Pallas kernels  72.4 us (21%)
  waiting for transfers between devices  28.9 us (8%)
  starting transfers between devices  8.59 us (2%)
  local copies, waits for them, and re-layouts  7.49 us (2%)
    all_to_all x3, blocking collectives, per_device(): parts = lax.all_to_all(partial, 'col', 0, 0, tiled=True)  95.6 us
    pallas_call x3, Pallas kernels, couple(): pl.pallas_call(functools.partial(couple_kernel, slot_dev), grid_spec=grid...  72.4 us
    all_to_all x2, blocking collectives, column_amplitudes(): got = lax.all_to_all(sent, ('pair', 'col'), 0, 0, tiled=True)  67.4 us
    all_to_all x3, blocking collectives, column_amplitudes(): parts = lax.all_to_all(contrib, 'pair', 0, 0, tiled=True)  44.2 us
    all_to_all x1, waiting for transfers between devices, column_amplitudes(): got = lax.all_to_all(sent, ('pair', 'col'), 0, 0, tiled=True)  28.9 us
    psum x1, blocking collectives, per_device(): pair_energy = lax.psum(jnp.sum(kfloat * amplitudes, axis=(1, 2)), 'col')  21.5 us
    all_to_all x1, starting transfers between devices, column_amplitudes(): got = lax.all_to_all(sent, ('pair', 'col'), 0, 0, tiled=True)  8.59 us
  transfers between devices with their start and end apart: 1, of which 1 were waited for; matrix products, arithmetic and copies ran while one was open for 0% of the time, Pallas kernels for 0%

profile of v1, /device:TPU:0, one launch (start us, length us, event | category | flops | bytes accessed | tf_op | source)
XLA Modules:
  0.0 352.3 jit_solution(5643719358399928666)
XLA Ops:
  0.6 0.8 constant_dynamic-slice_fusion
  1.4 1.1 fusion
  2.6 1.1 fusion.12
  4.0 16.5 %all_to_all.48 = f32[16,4,2048]{2,1,0:T(4,128)S(1)} all-to-all(f32[16,4,2048]{2,1,0:T(4,128)S(1)} %copy.14), channel_id=1, replica_groups=mesh['col'=8,'pair'=16] {'pair'}, dimensions={0} | all-to-all | bytes 1048576 | tf_op jit(solution)/shard_map/all_to_all | solution.py:69
  20.6 1.9 broadcast_in_dim.6
  22.5 8.6 %all-to-all-start.1 = ((bf16[128,4,16,128]{3,2,1,0:T(8,128)(2,1)}), bf16[128,4,16,128]{3,2,1,0:T(8,128)(2,1)S(1)}, u32[]{:S(2)}, u32[]{:S(2)}) async-start(bf16[128,4,16,128]{3,2,1,0:T(8,128)(2,1)} %broadcast_in_dim.6), calls=%async_computation.1 | async-start | bytes 4194304 | tf_op jit(solution)/shard_map/all_to_all | solution.py:74
  31.3 28.9 %all-to-all-done.1 = bf16[128,4,16,128]{3,2,1,0:T(8,128)(2,1)S(1)} async-done(((bf16[128,4,16,128]{3,2,1,0:T(8,128)(2,1)}), bf16[128,4,16,128]{3,2,1,0:T(8,128)(2,1)S(1)}, u32[]{:S(2)}, u32[]{:S(2)}) %all-to-all-start.1) | async-done | bytes 2097184 | tf_op jit(solution)/shard_map/all_to_all | solution.py:74
  60.2 0.6 copy.15
  60.8 24.1 %shard_map.86 = f32[8,32,16,128]{3,2,1,0:T(8,128)S(1)} custom-call(s32[512]{0:T(512)S(1)} %reshape.111.links_ref, s32[32]{0:T(128)S(1)} %subtract_clamp_fusion.nlive_ref, bf16[32,16,128,128]{3,2,1,0:T(8,128)(2,1)} %tiles_ref.5, bf16[64,128,128]{2,1,0:T(8,128)(2,1)S(1)} %bitcast.34), custom_call_target="tpu_custom_call" | custom-call | flops 4294967296 | bytes 20971520 | tf_op jit(solution)/shard_map/pallas_call | solution.py:49
  84.9 31.9 %all_to_all.49 = f32[8,32,16,128]{3,2,1,0:T(8,128)S(1)} all-to-all(f32[8,32,16,128]{3,2,1,0:T(8,128)S(1)} %shard_map.86), channel_id=1, replica_groups=mesh['col'=8,'pair'=16] {'col'}, dimensions={0} | all-to-all | bytes 4194304 | tf_op jit(solution)/shard_map/all_to_all | solution.py:98
  117.0 0.7 copy-done
  118.7 13.9 %all_to_all.50 = f32[16,4,2048]{2,1,0:T(4,128)S(1)} all-to-all(f32[16,4,2048]{2,1,0:T(4,128)S(1)} %copy.16), channel_id=1, replica_groups=mesh['col'=8,'pair'=16] {'pair'}, dimensions={0} | all-to-all | bytes 1048576 | tf_op jit(solution)/shard_map/all_to_all | solution.py:69
  132.7 0.5 broadcast_in_dim.7
  133.2 33.7 %all_to_all.51 = bf16[128,4,16,128]{3,2,1,0:T(8,128)(2,1)S(1)} all-to-all(bf16[128,4,16,128]{3,2,1,0:T(8,128)(2,1)S(1)} %broadcast_in_dim.7), channel_id=1, replica_groups=mesh['col'=8,'pair'=16] {'pair','col'}, dimensions={0} | all-to-all | bytes 4194304 | tf_op jit(solution)/shard_map/all_to_all | solution.py:74
  166.9 0.6 copy.17
  167.5 24.1 %shard_map.87 = f32[8,32,16,128]{3,2,1,0:T(8,128)S(1)} custom-call(s32[512]{0:T(512)S(1)} %reshape.111.links_ref, s32[32]{0:T(128)S(1)} %subtract_clamp_fusion.nlive_ref, bf16[32,16,128,128]{3,2,1,0:T(8,128)(2,1)} %tiles_ref.5, bf16[64,128,128]{2,1,0:T(8,128)(2,1)S(1)} %bitcast.35), custom_call_target="tpu_custom_call" | custom-call | flops 4294967296 | bytes 20971520 | tf_op jit(solution)/shard_map/pallas_call | solution.py:49
  191.6 31.9 %all_to_all.52 = f32[8,32,16,128]{3,2,1,0:T(8,128)S(1)} all-to-all(f32[8,32,16,128]{3,2,1,0:T(8,128)S(1)} %shard_map.87), channel_id=1, replica_groups=mesh['col'=8,'pair'=16] {'col'}, dimensions={0} | all-to-all | bytes 4194304 | tf_op jit(solution)/shard_map/all_to_all | solution.py:98
  224.6 13.9 %all_to_all.53 = f32[16,4,2048]{2,1,0:T(4,128)S(1)} all-to-all(f32[16,4,2048]{2,1,0:T(4,128)S(1)} %copy.18), channel_id=1, replica_groups=mesh['col'=8,'pair'=16] {'pair'}, dimensions={0} | all-to-all | bytes 1048576 | tf_op jit(solution)/shard_map/all_to_all | solution.py:69
  239.1 33.7 %all_to_all.54 = bf16[128,4,16,128]{3,2,1,0:T(8,128)(2,1)S(1)} all-to-all(bf16[128,4,16,128]{3,2,1,0:T(8,128)(2,1)S(1)} %broadcast_in_dim.8), channel_id=1, replica_groups=mesh['col'=8,'pair'=16] {'pair','col'}, dimensions={0} | all-to-all | bytes 4194304 | tf_op jit(solution)/shard_map/all_to_all | solution.py:74
  272.8 0.6 copy.19
  273.4 24.1 %shard_map.88 = f32[8,32,16,128]{3,2,1,0:T(8,128)S(1)} custom-call(s32[512]{0:T(512)S(1)} %reshape.111.links_ref, s32[32]{0:T(128)S(1)} %subtract_clamp_fusion.nlive_ref, bf16[32,16,128,128]{3,2,1,0:T(8,128)(2,1)} %tiles_ref.5, bf16[64,128,128]{2,1,0:T(8,128)(2,1)S(1)} %bitcast.33), custom_call_target="tpu_custom_call" | custom-call | flops 4294967296 | bytes 20971520 | tf_op jit(solution)/shard_map/pallas_call | solution.py:49
  297.5 31.9 %all_to_all.55 = f32[8,32,16,128]{3,2,1,0:T(8,128)S(1)} all-to-all(f32[8,32,16,128]{3,2,1,0:T(8,128)S(1)} %shard_map.88), channel_id=1, replica_groups=mesh['col'=8,'pair'=16] {'col'}, dimensions={0} | all-to-all | bytes 4194304 | tf_op jit(solution)/shard_map/all_to_all | solution.py:98
  329.6 1.2 fusion.7
  330.8 21.5 %psum.7 = f32[32]{0:T(128)} all-reduce(f32[32]{0:T(128)S(1)} %get-tuple-element.2), channel_id=1, replica_groups=mesh['col'=8,'pair'=16] {'col'}, use_global_device_ids=true, to_apply=%region_7.8 | all-reduce | flops 32 | bytes 256 | tf_op jit(solution)/shard_map/psum | solution.py:101
  (35 shorter events, 3.8 us)
Async XLA Ops:
  22.5 8.6 %copy-start.2 = (s32[32,16]{0,1:T(8,128)S(1)}, s32[32,16]{0,1:T(8,128)}, u32[]{:S(2)}) copy-start(s32[32,16]{0,1:T(8,128)} %param.11) | copy-start | bytes 6148
  22.5 8.8 %copy-start.5 = (s32[32]{0:T(128)S(1)}, s32[32]{0:T(128)}, u32[]{:S(2)}) copy-start(s32[32]{0:T(128)} %param.12) | copy-start | bytes 388
  22.5 37.7 %all-to-all-start.1 = ((bf16[128,4,16,128]{3,2,1,0:T(8,128)(2,1)}), bf16[128,4,16,128]{3,2,1,0:T(8,128)(2,1)S(1)}, u32[]{:S(2)}, u32[]{:S(2)}) async-start(bf16[128,4,16,128]{3,2,1,0:T(8,128)(2,1)} %broadcast_in_dim.6), calls=%async_computation.1 | async-start | bytes 4194304 | tf_op jit(solution)/shard_map/all_to_all | solution.py:74
  116.8 0.9 copy-start
  116.8 0.9 copy-start.1
  116.8 0.9 copy-start.3
  116.8 1.1 copy-start.4

commit v2 on v1

--- a/solution.py
+++ b/solution.py
@@ -9,7 +9,7 @@
 
 COL_DEV = 8
 SWEEPS = 3
-PAIR_BLOCK = 4
+PAIR_BLOCK = 8
 
 
 def couple_kernel(slot_dev, links_ref, nlive_ref, tiles_ref, colamp_ref, out_ref):
@@ -18,15 +18,16 @@
     for q in range(PAIR_BLOCK):
         pair = step * PAIR_BLOCK + q
         live = nlive_ref[pair]
-        acc = jnp.zeros((width, width), jnp.float32)
+        lefts = []
         for m in range(slot_dev):
-            tile = tiles_ref[q, m]
             block = colamp_ref[links_ref[pair * slot_dev + m]]
-            left = jnp.dot(tile, block, preferred_element_type=jnp.float32)
-            left = jnp.where(m < live, left, 0.0).astype(jnp.bfloat16)
-            acc = acc + lax.dot_general(
-                left, tile, (((1,), (1,)), ((), ())), preferred_element_type=jnp.float32
-            )
+            left = jnp.dot(tiles_ref[q, m], block, preferred_element_type=jnp.float32)
+            lefts.append(jnp.where(m < live, left, 0.0).astype(jnp.bfloat16))
+        lcat = jnp.concatenate(lefts, axis=1)
+        tcat = jnp.concatenate([tiles_ref[q, m] for m in range(slot_dev)], axis=1)
+        acc = lax.dot_general(
+            lcat, tcat, (((1,), (1,)), ((), ())), preferred_element_type=jnp.float32
+        )
         out_ref[:, q] = acc.reshape(out_ref.shape[0], out_ref.shape[2], width)
 
 

time: 353 us -> 319 us (0.904)
  Pallas kernels: 72.4 us -> 38.7 us
    pallas_call x3, Pallas kernels: 72.4 us -> 38.7 us  [couple(): pl.pallas_call(functools.partial(couple_kernel, slot_dev), grid_spec=grid...]
where the time goes in v2:
time: 319 us
  blocking collectives  229 us (72%)
  Pallas kernels  38.7 us (12%)
  waiting for transfers between devices  28.9 us (9%)
  starting transfers between devices  8.59 us (3%)
  local copies, waits for them, and re-layouts  7.49 us (2%)
  other arithmetic  3.38 us (1%)
    all_to_all x3, blocking collectives, per_device(): parts = lax.all_to_all(partial, 'col', 0, 0, tiled=True)  95.6 us
    all_to_all x2, blocking collectives, column_amplitudes(): got = lax.all_to_all(sent, ('pair', 'col'), 0, 0, tiled=True)  67.4 us
    all_to_all x3, blocking collectives, column_amplitudes(): parts = lax.all_to_all(contrib, 'pair', 0, 0, tiled=True)  44.2 us
    pallas_call x3, Pallas kernels, couple(): pl.pallas_call(functools.partial(couple_kernel, slot_dev), grid_spec=grid...  38.7 us
    all_to_all x1, waiting for transfers between devices, column_amplitudes(): got = lax.all_to_all(sent, ('pair', 'col'), 0, 0, tiled=True)  28.9 us
    psum x1, blocking collectives, per_device(): pair_energy = lax.psum(jnp.sum(kfloat * amplitudes, axis=(1, 2)), 'col')  21.5 us
    all_to_all x1, starting transfers between devices, column_amplitudes(): got = lax.all_to_all(sent, ('pair', 'col'), 0, 0, tiled=True)  8.59 us
  transfers between devices with their start and end apart: 1, of which 1 were waited for; matrix products, arithmetic and copies ran while one was open for 0% of the time, Pallas kernels for 0%

profile of v2, /device:TPU:0, one launch (start us, length us, event | category | flops | bytes accessed | tf_op | source)
XLA Modules:
  0.0 318.6 jit_solution(8410665981199982619)
XLA Ops:
  0.6 0.8 constant_dynamic-slice_fusion
  1.4 1.1 fusion
  2.6 1.1 fusion.12
  4.0 16.5 %all_to_all.48 = f32[16,4,2048]{2,1,0:T(4,128)S(1)} all-to-all(f32[16,4,2048]{2,1,0:T(4,128)S(1)} %copy.14), channel_id=1, replica_groups=mesh['col'=8,'pair'=16] {'pair'}, dimensions={0} | all-to-all | bytes 1048576 | tf_op jit(solution)/shard_map/all_to_all | solution.py:70
  20.6 1.9 broadcast_in_dim.6
  22.5 8.6 %all-to-all-start.1 = ((bf16[128,4,16,128]{3,2,1,0:T(8,128)(2,1)}), bf16[128,4,16,128]{3,2,1,0:T(8,128)(2,1)S(1)}, u32[]{:S(2)}, u32[]{:S(2)}) async-start(bf16[128,4,16,128]{3,2,1,0:T(8,128)(2,1)} %broadcast_in_dim.6), calls=%async_computation.1 | async-start | bytes 4194304 | tf_op jit(solution)/shard_map/all_to_all | solution.py:75
  31.3 28.9 %all-to-all-done.1 = bf16[128,4,16,128]{3,2,1,0:T(8,128)(2,1)S(1)} async-done(((bf16[128,4,16,128]{3,2,1,0:T(8,128)(2,1)}), bf16[128,4,16,128]{3,2,1,0:T(8,128)(2,1)S(1)}, u32[]{:S(2)}, u32[]{:S(2)}) %all-to-all-start.1) | async-done | bytes 2097184 | tf_op jit(solution)/shard_map/all_to_all | solution.py:75
  60.2 0.6 copy.15
  60.8 12.9 %shard_map.86 = f32[8,32,16,128]{3,2,1,0:T(8,128)S(1)} custom-call(s32[512]{0:T(512)S(1)} %reshape.111.links_ref, s32[32]{0:T(128)S(1)} %subtract_clamp_fusion.nlive_ref, bf16[32,16,128,128]{3,2,1,0:T(8,128)(2,1)} %tiles_ref.5, bf16[64,128,128]{2,1,0:T(8,128)(2,1)S(1)} %bitcast.34), custom_call_target="tpu_custom_call" | custom-call | flops 4294967296 | bytes 20971520 | tf_op jit(solution)/shard_map/pallas_call | solution.py:50
  73.7 31.9 %all_to_all.49 = f32[8,32,16,128]{3,2,1,0:T(8,128)S(1)} all-to-all(f32[8,32,16,128]{3,2,1,0:T(8,128)S(1)} %shard_map.86), channel_id=1, replica_groups=mesh['col'=8,'pair'=16] {'col'}, dimensions={0} | all-to-all | bytes 4194304 | tf_op jit(solution)/shard_map/all_to_all | solution.py:99
  105.7 0.7 copy-done
  107.5 13.9 %all_to_all.50 = f32[16,4,2048]{2,1,0:T(4,128)S(1)} all-to-all(f32[16,4,2048]{2,1,0:T(4,128)S(1)} %copy.16), channel_id=1, replica_groups=mesh['col'=8,'pair'=16] {'pair'}, dimensions={0} | all-to-all | bytes 1048576 | tf_op jit(solution)/shard_map/all_to_all | solution.py:70
  121.5 0.5 broadcast_in_dim.7
  122.0 33.7 %all_to_all.51 = bf16[128,4,16,128]{3,2,1,0:T(8,128)(2,1)S(1)} all-to-all(bf16[128,4,16,128]{3,2,1,0:T(8,128)(2,1)S(1)} %broadcast_in_dim.7), channel_id=1, replica_groups=mesh['col'=8,'pair'=16] {'pair','col'}, dimensions={0} | all-to-all | bytes 4194304 | tf_op jit(solution)/shard_map/all_to_all | solution.py:75
  155.7 0.6 copy.17
  156.2 12.9 %shard_map.87 = f32[8,32,16,128]{3,2,1,0:T(8,128)S(1)} custom-call(s32[512]{0:T(512)S(1)} %reshape.111.links_ref, s32[32]{0:T(128)S(1)} %subtract_clamp_fusion.nlive_ref, bf16[32,16,128,128]{3,2,1,0:T(8,128)(2,1)} %tiles_ref.5, bf16[64,128,128]{2,1,0:T(8,128)(2,1)S(1)} %bitcast.35), custom_call_target="tpu_custom_call" | custom-call | flops 4294967296 | bytes 20971520 | tf_op jit(solution)/shard_map/pallas_call | solution.py:50
  169.1 31.9 %all_to_all.52 = f32[8,32,16,128]{3,2,1,0:T(8,128)S(1)} all-to-all(f32[8,32,16,128]{3,2,1,0:T(8,128)S(1)} %shard_map.87), channel_id=1, replica_groups=mesh['col'=8,'pair'=16] {'col'}, dimensions={0} | all-to-all | bytes 4194304 | tf_op jit(solution)/shard_map/all_to_all | solution.py:99
  202.2 13.9 %all_to_all.53 = f32[16,4,2048]{2,1,0:T(4,128)S(1)} all-to-all(f32[16,4,2048]{2,1,0:T(4,128)S(1)} %copy.18), channel_id=1, replica_groups=mesh['col'=8,'pair'=16] {'pair'}, dimensions={0} | all-to-all | bytes 1048576 | tf_op jit(solution)/shard_map/all_to_all | solution.py:70
  216.7 33.7 %all_to_all.54 = bf16[128,4,16,128]{3,2,1,0:T(8,128)(2,1)S(1)} all-to-all(bf16[128,4,16,128]{3,2,1,0:T(8,128)(2,1)S(1)} %broadcast_in_dim.8), channel_id=1, replica_groups=mesh['col'=8,'pair'=16] {'pair','col'}, dimensions={0} | all-to-all | bytes 4194304 | tf_op jit(solution)/shard_map/all_to_all | solution.py:75
  250.3 0.6 copy.19
  250.9 12.9 %shard_map.88 = f32[8,32,16,128]{3,2,1,0:T(8,128)S(1)} custom-call(s32[512]{0:T(512)S(1)} %reshape.111.links_ref, s32[32]{0:T(128)S(1)} %subtract_clamp_fusion.nlive_ref, bf16[32,16,128,128]{3,2,1,0:T(8,128)(2,1)} %tiles_ref.5, bf16[64,128,128]{2,1,0:T(8,128)(2,1)S(1)} %bitcast.33), custom_call_target="tpu_custom_call" | custom-call | flops 4294967296 | bytes 20971520 | tf_op jit(solution)/shard_map/pallas_call | solution.py:50
  263.8 31.9 %all_to_all.55 = f32[8,32,16,128]{3,2,1,0:T(8,128)S(1)} all-to-all(f32[8,32,16,128]{3,2,1,0:T(8,128)S(1)} %shard_map.88), channel_id=1, replica_groups=mesh['col'=8,'pair'=16] {'col'}, dimensions={0} | all-to-all | bytes 4194304 | tf_op jit(solution)/shard_map/all_to_all | solution.py:99
  295.8 1.2 fusion.7
  297.1 21.5 %psum.7 = f32[32]{0:T(128)} all-reduce(f32[32]{0:T(128)S(1)} %get-tuple-element.2), channel_id=1, replica_groups=mesh['col'=8,'pair'=16] {'col'}, use_global_device_ids=true, to_apply=%region_7.8 | all-reduce | flops 32 | bytes 256 | tf_op jit(solution)/shard_map/psum | solution.py:102
  (35 shorter events, 3.8 us)
Async XLA Ops:
  22.5 8.6 %copy-start.2 = (s32[32,16]{0,1:T(8,128)S(1)}, s32[32,16]{0,1:T(8,128)}, u32[]{:S(2)}) copy-start(s32[32,16]{0,1:T(8,128)} %param.11) | copy-start | bytes 6148
  22.5 8.8 %copy-start.5 = (s32[32]{0:T(128)S(1)}, s32[32]{0:T(128)}, u32[]{:S(2)}) copy-start(s32[32]{0:T(128)} %param.12) | copy-start | bytes 388
  22.5 37.7 %all-to-all-start.1 = ((bf16[128,4,16,128]{3,2,1,0:T(8,128)(2,1)}), bf16[128,4,16,128]{3,2,1,0:T(8,128)(2,1)S(1)}, u32[]{:S(2)}, u32[]{:S(2)}) async-start(bf16[128,4,16,128]{3,2,1,0:T(8,128)(2,1)} %broadcast_in_dim.6), calls=%async_computation.1 | async-start | bytes 4194304 | tf_op jit(solution)/shard_map/all_to_all | solution.py:75
  105.6 0.9 copy-start
  105.6 0.9 copy-start.1
  105.6 0.9 copy-start.3
  105.6 1.1 copy-start.4

commit v3 on v2

--- a/solution.py
+++ b/solution.py
@@ -28,7 +28,7 @@
         acc = lax.dot_general(
             lcat, tcat, (((1,), (1,)), ((), ())), preferred_element_type=jnp.float32
         )
-        out_ref[:, q] = acc.reshape(out_ref.shape[0], out_ref.shape[2], width)
+        out_ref[:, q] = acc.reshape(out_ref.shape[0], out_ref.shape[2], width).astype(out_ref.dtype)
 
 
 def couple(tiles, colamp, links, nlive, col_size):
@@ -50,11 +50,11 @@
     return pl.pallas_call(
         functools.partial(couple_kernel, slot_dev),
         grid_spec=grid_spec,
-        out_shape=jax.ShapeDtypeStruct((col_size, pair_dev, rows, width), jnp.float32),
+        out_shape=jax.ShapeDtypeStruct((col_size, pair_dev, rows, width), jnp.bfloat16),
         compiler_params=pltpu.CompilerParams(vmem_limit_bytes=48 * 1024 * 1024),
         cost_estimate=pl.CostEstimate(
             flops=flops,
-            bytes_accessed=tiles.size * 2 + colamp.size * 2 + pair_dev * width * width * 4,
+            bytes_accessed=tiles.size * 2 + colamp.size * 2 + pair_dev * width * width * 2,
             transcendentals=0,
         ),
     )(links.reshape(-1), nlive, tiles, colamp)
@@ -97,7 +97,7 @@
         colamp = column_amplitudes(amplitudes, one_hot, pair_size, col_size)
         partial = couple(intersections, colamp, links, nlive, col_size)
         parts = lax.all_to_all(partial, "col", 0, 0, tiled=True)
-        coupled = jnp.sum(parts, axis=0)
+        coupled = jnp.sum(parts.astype(jnp.float32), axis=0)
         amplitudes = -(kfloat + coupled) / denom
     pair_energy = lax.psum(jnp.sum(kfloat * amplitudes, axis=(1, 2)), "col")
     return (amplitudes, pair_energy)

time: 319 us -> 285 us (0.89)
  blocking collectives: 229 us -> 195 us
    all_to_all x3, blocking collectives: 95.6 us -> 62.1 us  [per_device(): parts = lax.all_to_all(partial, 'col', 0, 0, tiled=True)]
where the time goes in v3:
time: 285 us; the launch traced here: 284 us
  blocking collectives  195 us (68%)
  Pallas kernels  38.7 us (14%)
  waiting for transfers between devices  28.9 us (10%)
  starting transfers between devices  8.59 us (3%)
  local copies, waits for them, and re-layouts  6.76 us (2%)
  other arithmetic  3.35 us (1%)
    all_to_all x2, blocking collectives, column_amplitudes(): got = lax.all_to_all(sent, ('pair', 'col'), 0, 0, tiled=True)  67.4 us
    all_to_all x3, blocking collectives, per_device(): parts = lax.all_to_all(partial, 'col', 0, 0, tiled=True)  62.1 us
    all_to_all x3, blocking collectives, column_amplitudes(): parts = lax.all_to_all(contrib, 'pair', 0, 0, tiled=True)  44.2 us
    pallas_call x3, Pallas kernels, couple(): pl.pallas_call(functools.partial(couple_kernel, slot_dev), grid_spec=grid...  38.7 us
    all_to_all x1, waiting for transfers between devices, column_amplitudes(): got = lax.all_to_all(sent, ('pair', 'col'), 0, 0, tiled=True)  28.9 us
    psum x1, blocking collectives, per_device(): pair_energy = lax.psum(jnp.sum(kfloat * amplitudes, axis=(1, 2)), 'col')  21.3 us
    all_to_all x1, starting transfers between devices, column_amplitudes(): got = lax.all_to_all(sent, ('pair', 'col'), 0, 0, tiled=True)  8.59 us
  transfers between devices with their start and end apart: 1, of which 1 were waited for; matrix products, arithmetic and copies ran while one was open for 0% of the time, Pallas kernels for 0%

profile of v3, /device:TPU:0, one launch (start us, length us, event | category | flops | bytes accessed | tf_op | source)
XLA Modules:
  0.0 284.1 jit_solution(17777013649386831760)
XLA Ops:
  0.6 0.8 constant_dynamic-slice_fusion
  1.4 1.1 fusion
  2.6 1.1 fusion.12
  4.0 16.5 %all_to_all.48 = f32[16,4,2048]{2,1,0:T(4,128)S(1)} all-to-all(f32[16,4,2048]{2,1,0:T(4,128)S(1)} %copy.14), channel_id=1, replica_groups=mesh['col'=8,'pair'=16] {'pair'}, dimensions={0} | all-to-all | bytes 1048576 | tf_op jit(solution)/shard_map/all_to_all | solution.py:70
  20.6 1.9 broadcast_in_dim.6
  22.5 8.6 %all-to-all-start.1 = ((bf16[128,4,16,128]{3,2,1,0:T(8,128)(2,1)}), bf16[128,4,16,128]{3,2,1,0:T(8,128)(2,1)S(1)}, u32[]{:S(2)}, u32[]{:S(2)}) async-start(bf16[128,4,16,128]{3,2,1,0:T(8,128)(2,1)} %broadcast_in_dim.6), calls=%async_computation.1 | async-start | bytes 4194304 | tf_op jit(solution)/shard_map/all_to_all | solution.py:75
  31.3 28.9 %all-to-all-done.1 = bf16[128,4,16,128]{3,2,1,0:T(8,128)(2,1)S(1)} async-done(((bf16[128,4,16,128]{3,2,1,0:T(8,128)(2,1)}), bf16[128,4,16,128]{3,2,1,0:T(8,128)(2,1)S(1)}, u32[]{:S(2)}, u32[]{:S(2)}) %all-to-all-start.1) | async-done | bytes 2097184 | tf_op jit(solution)/shard_map/all_to_all | solution.py:75
  60.2 0.6 copy.15
  60.8 12.9 %shard_map.86 = bf16[8,32,16,128]{3,2,1,0:T(8,128)(2,1)S(1)} custom-call(s32[512]{0:T(512)S(1)} %reshape.111.links_ref, s32[32]{0:T(128)S(1)} %subtract_clamp_fusion.nlive_ref, bf16[32,16,128,128]{3,2,1,0:T(8,128)(2,1)} %tiles_ref.5, bf16[64,128,128]{2,1,0:T(8,128)(2,1)S(1)} %bitcast.34), custom_call_target="tpu_custom_call" | custom-call | flops 4294967296 | bytes 19922944 | tf_op jit(solution)/shard_map/pallas_call | solution.py:50
  73.7 20.8 %all_to_all.49 = bf16[8,32,16,128]{3,2,1,0:T(8,128)(2,1)S(1)} all-to-all(bf16[8,32,16,128]{3,2,1,0:T(8,128)(2,1)S(1)} %shard_map.86), channel_id=1, replica_groups=mesh['col'=8,'pair'=16] {'col'}, dimensions={0} | all-to-all | bytes 2097152 | tf_op jit(solution)/shard_map/all_to_all | solution.py:99
  95.7 13.8 %all_to_all.50 = f32[16,4,2048]{2,1,0:T(4,128)S(1)} all-to-all(f32[16,4,2048]{2,1,0:T(4,128)S(1)} %copy.16), channel_id=1, replica_groups=mesh['col'=8,'pair'=16] {'pair'}, dimensions={0} | all-to-all | bytes 1048576 | tf_op jit(solution)/shard_map/all_to_all | solution.py:70
  109.6 0.5 broadcast_in_dim.7
  110.2 33.7 %all_to_all.51 = bf16[128,4,16,128]{3,2,1,0:T(8,128)(2,1)S(1)} all-to-all(bf16[128,4,16,128]{3,2,1,0:T(8,128)(2,1)S(1)} %broadcast_in_dim.7), channel_id=1, replica_groups=mesh['col'=8,'pair'=16] {'pair','col'}, dimensions={0} | all-to-all | bytes 4194304 | tf_op jit(solution)/shard_map/all_to_all | solution.py:75
  143.8 0.6 copy.17
  144.4 12.9 %shard_map.87 = bf16[8,32,16,128]{3,2,1,0:T(8,128)(2,1)S(1)} custom-call(s32[512]{0:T(512)S(1)} %reshape.111.links_ref, s32[32]{0:T(128)S(1)} %subtract_clamp_fusion.nlive_ref, bf16[32,16,128,128]{3,2,1,0:T(8,128)(2,1)} %tiles_ref.5, bf16[64,128,128]{2,1,0:T(8,128)(2,1)S(1)} %bitcast.35), custom_call_target="tpu_custom_call" | custom-call | flops 4294967296 | bytes 19922944 | tf_op jit(solution)/shard_map/pallas_call | solution.py:50
  157.3 20.6 %all_to_all.52 = bf16[8,32,16,128]{3,2,1,0:T(8,128)(2,1)S(1)} all-to-all(bf16[8,32,16,128]{3,2,1,0:T(8,128)(2,1)S(1)} %shard_map.87), channel_id=1, replica_groups=mesh['col'=8,'pair'=16] {'col'}, dimensions={0} | all-to-all | bytes 2097152 | tf_op jit(solution)/shard_map/all_to_all | solution.py:99
  179.1 13.8 %all_to_all.53 = f32[16,4,2048]{2,1,0:T(4,128)S(1)} all-to-all(f32[16,4,2048]{2,1,0:T(4,128)S(1)} %copy.18), channel_id=1, replica_groups=mesh['col'=8,'pair'=16] {'pair'}, dimensions={0} | all-to-all | bytes 1048576 | tf_op jit(solution)/shard_map/all_to_all | solution.py:70
  193.1 0.5 broadcast_in_dim.8
  193.6 33.7 %all_to_all.54 = bf16[128,4,16,128]{3,2,1,0:T(8,128)(2,1)S(1)} all-to-all(bf16[128,4,16,128]{3,2,1,0:T(8,128)(2,1)S(1)} %broadcast_in_dim.8), channel_id=1, replica_groups=mesh['col'=8,'pair'=16] {'pair','col'}, dimensions={0} | all-to-all | bytes 4194304 | tf_op jit(solution)/shard_map/all_to_all | solution.py:75
  227.3 0.6 copy.19
  227.8 12.9 %shard_map.88 = bf16[8,32,16,128]{3,2,1,0:T(8,128)(2,1)S(1)} custom-call(s32[512]{0:T(512)S(1)} %reshape.111.links_ref, s32[32]{0:T(128)S(1)} %subtract_clamp_fusion.nlive_ref, bf16[32,16,128,128]{3,2,1,0:T(8,128)(2,1)} %tiles_ref.5, bf16[64,128,128]{2,1,0:T(8,128)(2,1)S(1)} %bitcast.33), custom_call_target="tpu_custom_call" | custom-call | flops 4294967296 | bytes 19922944 | tf_op jit(solution)/shard_map/pallas_call | solution.py:50
  240.7 20.6 %all_to_all.55 = bf16[8,32,16,128]{3,2,1,0:T(8,128)(2,1)S(1)} all-to-all(bf16[8,32,16,128]{3,2,1,0:T(8,128)(2,1)S(1)} %shard_map.88), channel_id=1, replica_groups=mesh['col'=8,'pair'=16] {'col'}, dimensions={0} | all-to-all | bytes 2097152 | tf_op jit(solution)/shard_map/all_to_all | solution.py:99
  261.5 1.2 fusion.7
  262.7 21.3 %psum.7 = f32[32]{0:T(128)} all-reduce(f32[32]{0:T(128)S(1)} %get-tuple-element.2), channel_id=1, replica_groups=mesh['col'=8,'pair'=16] {'col'}, use_global_device_ids=true, to_apply=%region_7.8 | all-reduce | flops 32 | bytes 256 | tf_op jit(solution)/shard_map/psum | solution.py:102
  (35 shorter events, 3.3 us)
Async XLA Ops:
  22.5 8.6 %copy-start.2 = (s32[32,16]{0,1:T(8,128)S(1)}, s32[32,16]{0,1:T(8,128)}, u32[]{:S(2)}) copy-start(s32[32,16]{0,1:T(8,128)} %param.11) | copy-start | bytes 6148
  22.5 8.8 %copy-start.5 = (s32[32]{0:T(128)S(1)}, s32[32]{0:T(128)}, u32[]{:S(2)}) copy-start(s32[32]{0:T(128)} %param.12) | copy-start | bytes 388
  22.5 37.7 %all-to-all-start.1 = ((bf16[128,4,16,128]{3,2,1,0:T(8,128)(2,1)}), bf16[128,4,16,128]{3,2,1,0:T(8,128)(2,1)S(1)}, u32[]{:S(2)}, u32[]{:S(2)}) async-start(bf16[128,4,16,128]{3,2,1,0:T(8,128)(2,1)} %broadcast_in_dim.6), calls=%async_computation.1 | async-start | bytes 4194304 | tf_op jit(solution)/shard_map/all_to_all | solution.py:75
  73.7 21.0 %copy-start = (bf16[32,16,128]{2,1,0:T(8,128)(2,1)S(1)}, bf16[32,16,128]{2,1,0:T(8,128)(2,1)}, u32[]{:S(2)}) copy-start(bf16[32,16,128]{2,1,0:T(8,128)(2,1)} %param.7) | copy-start | bytes 393220
  73.7 21.0 %copy-start.1 = (f32[32,128]{1,0:T(8,128)S(1)}, f32[32,128]{1,0:T(8,128)}, u32[]{:S(2)}) copy-start(f32[32,128]{1,0:T(8,128)} %param.8) | copy-start | bytes 49156
  73.7 21.0 %copy-start.3 = (f32[32]{0:T(128)S(1)}, f32[32]{0:T(128)}, u32[]{:S(2)}) copy-start(f32[32]{0:T(128)} %param.9) | copy-start | bytes 388
  73.7 21.2 %copy-start.4 = (s32[32]{0:T(128)S(1)}, s32[32]{0:T(128)}, u32[]{:S(2)}) copy-start(s32[32]{0:T(128)} %param.13) | copy-start | bytes 388

commit v4 on v3

--- a/solution.py
+++ b/solution.py
@@ -93,13 +93,35 @@
         jnp.float32
     )
     nlive = jnp.clip(counts - rank * slot_dev, 0, slot_dev).astype(jnp.int32)
+    blocks = [integrals]
+    for k in range(1, col_size):
+        ring = [(i, (i + k) % col_size) for i in range(col_size)]
+        blocks.append(lax.ppermute(integrals, "col", ring))
+    owner_of = (rank - jnp.arange(col_size)) % col_size
+    k_full = jnp.take(jnp.stack(blocks), owner_of, axis=0).astype(jnp.float32)
+    full_energy = pno_energy.reshape(pair_dev, col_size, 1, row_count, 1)
+    denom_full = full_energy + pno_energy[:, None, None, None, :] + shift[:, None, None, None, None]
+    weight = k_full / jnp.swapaxes(denom_full[:, :, 0], 0, 1)
     for sweep in range(SWEEPS):
         colamp = column_amplitudes(amplitudes, one_hot, pair_size, col_size)
         partial = couple(intersections, colamp, links, nlive, col_size)
-        parts = lax.all_to_all(partial, "col", 0, 0, tiled=True)
-        coupled = jnp.sum(parts.astype(jnp.float32), axis=0)
+        if sweep < SWEEPS - 1:
+            parts = lax.all_to_all(partial, "col", 0, 0, tiled=True)
+            coupled = jnp.sum(parts.astype(jnp.float32), axis=0)
+        else:
+            share = -jnp.sum(weight * partial.astype(jnp.float32), axis=(0, 2, 3))
+            high = share.astype(jnp.bfloat16)
+            low = (share - high.astype(jnp.float32)).astype(jnp.bfloat16)
+            extra = jnp.zeros((row_count, partial.shape[-1]), jnp.bfloat16)
+            extra = extra.at[0, :pair_dev].set(high).at[1, :pair_dev].set(low)
+            extra = jnp.broadcast_to(extra, (col_size, 1) + extra.shape)
+            parts = lax.all_to_all(jnp.concatenate([partial, extra], axis=1), "col", 0, 0, tiled=True)
+            parts = parts.astype(jnp.float32)
+            coupled = jnp.sum(parts[:, :pair_dev], axis=0)
+            shares = parts[:, pair_dev, 0, :pair_dev] + parts[:, pair_dev, 1, :pair_dev]
         amplitudes = -(kfloat + coupled) / denom
-    pair_energy = lax.psum(jnp.sum(kfloat * amplitudes, axis=(1, 2)), "col")
+    base = -jnp.sum(weight * k_full, axis=(0, 2, 3))
+    pair_energy = base + jnp.sum(shares, axis=0)
     return (amplitudes, pair_energy)
 
 

time: 285 us -> 280 us (0.982)
  blocking collectives: 195 us -> 129 us
  starting transfers between devices: 8.59 us -> 36.5 us
  waiting for transfers between devices: 28.9 us -> 49.2 us
  local copies, waits for them, and re-layouts: 6.76 us -> 16.5 us
    all_to_all x2 -> x1, blocking collectives: 67.4 us -> 33.7 us  [column_amplitudes(): got = lax.all_to_all(sent, ('pair', 'col'), 0, 0, tiled=True)]
    all_to_all x0 -> x1, blocking collectives: none -> 24 us  [per_device(): lax.all_to_all(jnp.concatenate([partial, extra], axis=1), 'col', 0, 0, ti...]
    psum x1 -> x0, blocking collectives: 21.3 us -> none  [per_device(): pair_energy = lax.psum(jnp.sum(kfloat * amplitudes, axis=(1, 2)), 'col')]
    all_to_all x3 -> x2, blocking collectives: 62.1 us -> 41.4 us  [per_device(): parts = lax.all_to_all(partial, 'col', 0, 0, tiled=True)]
    ppermute x0 -> x7, waiting for transfers between devices: none -> 18.2 us  [per_device(): blocks.append(lax.ppermute(integrals, 'col', ring))]
    ppermute x0 -> x7, starting transfers between devices: none -> 16.3 us  [per_device(): blocks.append(lax.ppermute(integrals, 'col', ring))]
    all_to_all x3 -> x2, blocking collectives: 44.2 us -> 30.4 us  [column_amplitudes(): parts = lax.all_to_all(contrib, 'pair', 0, 0, tiled=True)]
    all_to_all x1 -> x2, starting transfers between devices: 8.59 us -> 16.7 us  [column_amplitudes(): got = lax.all_to_all(sent, ('pair', 'col'), 0, 0, tiled=True)]
  transfers between devices with their start and end apart: 1 -> 10, of which waited for: 1 -> 4; matrix products, arithmetic and copies ran while one was open for 0% -> 3% of each run, Pallas kernels for 0% -> 0%
where the time goes in v4:
time: 280 us; the launch traced here: 279 us
  blocking collectives  129 us (46%)
  waiting for transfers between devices  49.2 us (18%)
  Pallas kernels  39 us (14%)
  starting transfers between devices  36.5 us (13%)
  local copies, waits for them, and re-layouts  16.5 us (6%)
  other arithmetic  5.33 us (2%)
    all_to_all x2, blocking collectives, per_device(): parts = lax.all_to_all(partial, 'col', 0, 0, tiled=True)  41.4 us
    pallas_call x3, Pallas kernels, couple(): pl.pallas_call(functools.partial(couple_kernel, slot_dev), grid_spec=grid...  39 us
    all_to_all x1, blocking collectives, column_amplitudes(): got = lax.all_to_all(sent, ('pair', 'col'), 0, 0, tiled=True)  33.7 us
    all_to_all x2, blocking collectives, column_amplitudes(): parts = lax.all_to_all(contrib, 'pair', 0, 0, tiled=True)  30.4 us
    all_to_all x2, waiting for transfers between devices, column_amplitudes(): got = lax.all_to_all(sent, ('pair', 'col'), 0, 0, tiled=True)  28.9 us
    all_to_all x1, blocking collectives, per_device(): lax.all_to_all(jnp.concatenate([partial, extra], axis=1), 'col', 0, 0, ti...  24 us
    ppermute x7, waiting for transfers between devices, per_device(): blocks.append(lax.ppermute(integrals, 'col', ring))  18.2 us
    all_to_all x2, starting transfers between devices, column_amplitudes(): got = lax.all_to_all(sent, ('pair', 'col'), 0, 0, tiled=True)  16.7 us
  transfers between devices with their start and end apart: 10, of which 4 were waited for; matrix products, arithmetic and copies ran while one was open for 3% of the time, Pallas kernels for 0%

profile of v4, /device:TPU:0, one launch (start us, length us, event | category | flops | bytes accessed | tf_op | source)
XLA Modules:
  0.0 278.9 jit_solution(17510445524022541673)
XLA Ops:
  4.0 16.5 %all_to_all.48 = f32[16,4,2048]{2,1,0:T(4,128)S(1)} all-to-all(f32[16,4,2048]{2,1,0:T(4,128)S(1)} %copy.17), channel_id=1, replica_groups=mesh['col'=8,'pair'=16] {'pair'}, dimensions={0} | all-to-all | bytes 1048576 | tf_op jit(solution)/shard_map/all_to_all | solution.py:70
  20.6 1.9 broadcast_in_dim.18
  22.5 8.6 %all-to-all-start.1 = ((bf16[128,4,16,128]{3,2,1,0:T(8,128)(2,1)}), bf16[128,4,16,128]{3,2,1,0:T(8,128)(2,1)S(1)}, u32[]{:S(2)}, u32[]{:S(2)}) async-start(bf16[128,4,16,128]{3,2,1,0:T(8,128)(2,1)} %broadcast_in_dim.18), calls=%async_computation.1 | async-start | bytes 4194304 | tf_op jit(solution)/shard_map/all_to_all | solution.py:75
  31.3 28.9 %all-to-all-done.1 = bf16[128,4,16,128]{3,2,1,0:T(8,128)(2,1)S(1)} async-done(((bf16[128,4,16,128]{3,2,1,0:T(8,128)(2,1)}), bf16[128,4,16,128]{3,2,1,0:T(8,128)(2,1)S(1)}, u32[]{:S(2)}, u32[]{:S(2)}) %all-to-all-start.1) | async-done | bytes 2097184 | tf_op jit(solution)/shard_map/all_to_all | solution.py:75
  60.8 13.0 %shard_map.86 = bf16[8,32,16,128]{3,2,1,0:T(8,128)(2,1)S(1)} custom-call(s32[512]{0:T(512)S(1)} %reshape.250.links_ref, s32[32]{0:T(128)S(1)} %subtract_clamp_fusion.nlive_ref, bf16[32,16,128,128]{3,2,1,0:T(8,128)(2,1)} %tiles_ref.5, bf16[64,128,128]{2,1,0:T(8,128)(2,1)S(1)} %bitcast.62), custom_call_target="tpu_custom_call" | custom-call | flops 4294967296 | bytes 19922944 | tf_op jit(solution)/shard_map/pallas_call | solution.py:50
  73.8 20.8 %all_to_all.49 = bf16[8,32,16,128]{3,2,1,0:T(8,128)(2,1)S(1)} all-to-all(bf16[8,32,16,128]{3,2,1,0:T(8,128)(2,1)S(1)} %shard_map.86), channel_id=1, replica_groups=mesh['col'=8,'pair'=16] {'col'}, dimensions={0} | all-to-all | bytes 2097152 | tf_op jit(solution)/shard_map/all_to_all | solution.py:109
  95.8 13.9 %all_to_all.50 = f32[16,4,2048]{2,1,0:T(4,128)S(1)} all-to-all(f32[16,4,2048]{2,1,0:T(4,128)S(1)} %copy.19), channel_id=1, replica_groups=mesh['col'=8,'pair'=16] {'pair'}, dimensions={0} | all-to-all | bytes 1048576 | tf_op jit(solution)/shard_map/all_to_all | solution.py:70
  110.3 33.7 %all_to_all.51 = bf16[128,4,16,128]{3,2,1,0:T(8,128)(2,1)S(1)} all-to-all(bf16[128,4,16,128]{3,2,1,0:T(8,128)(2,1)S(1)} %broadcast_in_dim.19), channel_id=1, replica_groups=mesh['col'=8,'pair'=16] {'pair','col'}, dimensions={0} | all-to-all | bytes 4194304 | tf_op jit(solution)/shard_map/all_to_all | solution.py:75
  144.5 13.0 %shard_map.87 = bf16[8,32,16,128]{3,2,1,0:T(8,128)(2,1)S(1)} custom-call(s32[512]{0:T(512)S(1)} %reshape.250.links_ref, s32[32]{0:T(128)S(1)} %subtract_clamp_fusion.nlive_ref, bf16[32,16,128,128]{3,2,1,0:T(8,128)(2,1)} %tiles_ref.5, bf16[64,128,128]{2,1,0:T(8,128)(2,1)S(1)} %bitcast.63), custom_call_target="tpu_custom_call" | custom-call | flops 4294967296 | bytes 19922944 | tf_op jit(solution)/shard_map/pallas_call | solution.py:50
  157.5 20.6 %all_to_all.52 = bf16[8,32,16,128]{3,2,1,0:T(8,128)(2,1)S(1)} all-to-all(bf16[8,32,16,128]{3,2,1,0:T(8,128)(2,1)S(1)} %shard_map.87), channel_id=1, replica_groups=mesh['col'=8,'pair'=16] {'col'}, dimensions={0} | all-to-all | bytes 2097152 | tf_op jit(solution)/shard_map/all_to_all | solution.py:109
  180.1 3.6 %all-to-all-start.6 = ((f32[16,4,2048]{2,1,0:T(4,128)}), f32[16,4,2048]{2,1,0:T(4,128)S(1)}, u32[]{:S(2)}, u32[]{:S(2)}) async-start(f32[16,4,2048]{2,1,0:T(4,128)} %copy.21), calls=%async_computation.6 | async-start | bytes 1048576 | tf_op jit(solution)/shard_map/all_to_all | solution.py:70
  183.7 1.7 collective-permute-start
  185.9 3.0 %collective-permute-start.2 = (bf16[32,16,128]{2,1,0:T(8,128)(2,1)S(1)}, bf16[32,16,128]{2,1,0:T(8,128)(2,1)S(1)}, u32[]{:S(2)}, u32[]{:S(2)}) collective-permute-start(bf16[32,16,128]{2,1,0:T(8,128)(2,1)S(1)} %copy-done), channel_id=1, source_target_pairs={{0,48},{16,64},{32,80},{48,96},{64,112},{80,0},{96,16},{112,32},{1... | collective-permute-start | bytes 393224 | tf_op jit(solution)/shard_map/ppermute | solution.py:99
  189.0 2.3 collective-permute-start.3
  191.3 2.6 collective-permute-start.4
  193.9 2.1 all-to-all-done.6
  196.1 1.9 broadcast_in_dim.20
  198.0 8.1 %all-to-all-start.7 = ((bf16[128,4,16,128]{3,2,1,0:T(8,128)(2,1)}), bf16[128,4,16,128]{3,2,1,0:T(8,128)(2,1)S(1)}, u32[]{:S(2)}, u32[]{:S(2)}) async-start(bf16[128,4,16,128]{3,2,1,0:T(8,128)(2,1)} %broadcast_in_dim.20), calls=%async_computation.7 | async-start | bytes 4194304 | tf_op jit(solution)/shard_map/all_to_all | solution.py:75
  207.0 2.3 collective-permute-start.5
  210.0 3.7 %collective-permute-start.6 = (bf16[32,16,128]{2,1,0:T(8,128)(2,1)S(1)}, bf16[32,16,128]{2,1,0:T(8,128)(2,1)S(1)}, u32[]{:S(2)}, u32[]{:S(2)}) collective-permute-start(bf16[32,16,128]{2,1,0:T(8,128)(2,1)S(1)} %copy-done), channel_id=1, source_target_pairs={{0,112},{16,0},{32,16},{48,32},{64,48},{80,64},{96,80},{112,96},{1... | collective-permute-start | bytes 393224 | tf_op jit(solution)/shard_map/ppermute | solution.py:99
  216.3 16.8 %collective-permute-done.5 = bf16[32,16,128]{2,1,0:T(8,128)(2,1)S(1)} collective-permute-done((bf16[32,16,128]{2,1,0:T(8,128)(2,1)S(1)}, bf16[32,16,128]{2,1,0:T(8,128)(2,1)S(1)}, u32[]{:S(2)}, u32[]{:S(2)}) %collective-permute-start.5) | collective-permute-done | bytes 131104 | tf_op jit(solution)/shard_map/ppermute | solution.py:99
  235.8 2.0 gather_fusion
  238.4 13.0 %shard_map.88 = bf16[8,32,16,128]{3,2,1,0:T(8,128)(2,1)S(1)} custom-call(s32[512]{0:T(512)S(1)} %reshape.250.links_ref, s32[32]{0:T(128)S(1)} %subtract_clamp_fusion.nlive_ref, bf16[32,16,128,128]{3,2,1,0:T(8,128)(2,1)} %tiles_ref.5, bf16[64,128,128]{2,1,0:T(8,128)(2,1)S(1)} %bitcast.61), custom_call_target="tpu_custom_call" | custom-call | flops 4294967296 | bytes 19922944 | tf_op jit(solution)/shard_map/pallas_call | solution.py:50
  253.2 24.0 %all_to_all.53 = bf16[8,33,16,128]{3,2,1,0:T(8,128)(2,1)S(1)} all-to-all(bf16[8,33,16,128]{3,2,1,0:T(8,128)(2,1)S(1)} %pad_maximum_fusion), channel_id=1, replica_groups=mesh['col'=8,'pair'=16] {'col'}, dimensions={0} | all-to-all | bytes 2162688 | tf_op jit(solution)/shard_map/all_to_all | solution.py:118
  (74 shorter events, 20.0 us)
Async XLA Ops:
  22.5 8.6 %copy-start.3 = (s32[32,16]{0,1:T(8,128)S(1)}, s32[32,16]{0,1:T(8,128)}, u32[]{:S(2)}) copy-start(s32[32,16]{0,1:T(8,128)} %param.15) | copy-start | bytes 6148
  22.5 8.8 %copy-start.5 = (s32[32]{0:T(128)S(1)}, s32[32]{0:T(128)}, u32[]{:S(2)}) copy-start(s32[32]{0:T(128)} %param.16) | copy-start | bytes 388
  22.5 37.7 %all-to-all-start.1 = ((bf16[128,4,16,128]{3,2,1,0:T(8,128)(2,1)}), bf16[128,4,16,128]{3,2,1,0:T(8,128)(2,1)S(1)}, u32[]{:S(2)}, u32[]{:S(2)}) async-start(bf16[128,4,16,128]{3,2,1,0:T(8,128)(2,1)} %broadcast_in_dim.18), calls=%async_computation.1 | async-start | bytes 4194304 | tf_op jit(solution)/shard_map/all_to_all | solution.py:75
  73.8 21.0 %copy-start = (bf16[32,16,128]{2,1,0:T(8,128)(2,1)S(1)}, bf16[32,16,128]{2,1,0:T(8,128)(2,1)}, u32[]{:S(2)}) copy-start(bf16[32,16,128]{2,1,0:T(8,128)(2,1)} %param.11) | copy-start | bytes 393220
  73.8 21.0 %copy-start.1 = (f32[32,128]{1,0:T(8,128)S(1)}, f32[32,128]{1,0:T(8,128)}, u32[]{:S(2)}) copy-start(f32[32,128]{1,0:T(8,128)} %param.12) | copy-start | bytes 49156
  73.8 21.0 %copy-start.2 = (f32[32]{0:T(128)S(1)}, f32[32]{0:T(128)}, u32[]{:S(2)}) copy-start(f32[32]{0:T(128)} %param.13) | copy-start | bytes 388
  73.8 21.2 %copy-start.4 = (s32[32]{0:T(128)S(1)}, s32[32]{0:T(128)}, u32[]{:S(2)}) copy-start(s32[32]{0:T(128)} %param.17) | copy-start | bytes 388
  180.1 15.9 %all-to-all-start.6 = ((f32[16,4,2048]{2,1,0:T(4,128)}), f32[16,4,2048]{2,1,0:T(4,128)S(1)}, u32[]{:S(2)}, u32[]{:S(2)}) async-start(f32[16,4,2048]{2,1,0:T(4,128)} %copy.21), calls=%async_computation.6 | async-start | bytes 1048576 | tf_op jit(solution)/shard_map/all_to_all | solution.py:70
  183.7 23.3 %collective-permute-start = (bf16[32,16,128]{2,1,0:T(8,128)(2,1)S(1)}, bf16[32,16,128]{2,1,0:T(8,128)(2,1)S(1)}, u32[]{:S(2)}, u32[]{:S(2)}) collective-permute-start(bf16[32,16,128]{2,1,0:T(8,128)(2,1)S(1)} %copy-done), channel_id=1, source_target_pairs={{0,16},{16,32},{32,48},{48,64},{64,80},{80,96},{96,112},{112,0},{1... | collective-permute-start | bytes 393224 | tf_op jit(solution)/shard_map/ppermute | solution.py:99
  185.4 24.6 %collective-permute-start.1 = (bf16[32,16,128]{2,1,0:T(8,128)(2,1)S(1)}, bf16[32,16,128]{2,1,0:T(8,128)(2,1)S(1)}, u32[]{:S(2)}, u32[]{:S(2)}) collective-permute-start(bf16[32,16,128]{2,1,0:T(8,128)(2,1)S(1)} %copy-done), channel_id=1, source_target_pairs={{0,32},{16,48},{32,64},{48,80},{64,96},{80,112},{96,0},{112,16},{1... | collective-permute-start | bytes 393224 | tf_op jit(solution)/shard_map/ppermute | solution.py:99
  185.9 28.4 %collective-permute-start.2 = (bf16[32,16,128]{2,1,0:T(8,128)(2,1)S(1)}, bf16[32,16,128]{2,1,0:T(8,128)(2,1)S(1)}, u32[]{:S(2)}, u32[]{:S(2)}) collective-permute-start(bf16[32,16,128]{2,1,0:T(8,128)(2,1)S(1)} %copy-done), channel_id=1, source_target_pairs={{0,48},{16,64},{32,80},{48,96},{64,112},{80,0},{96,16},{112,32},{1... | collective-permute-start | bytes 393224 | tf_op jit(solution)/shard_map/ppermute | solution.py:99
  189.0 26.1 %collective-permute-start.3 = (bf16[32,16,128]{2,1,0:T(8,128)(2,1)S(1)}, bf16[32,16,128]{2,1,0:T(8,128)(2,1)S(1)}, u32[]{:S(2)}, u32[]{:S(2)}) collective-permute-start(bf16[32,16,128]{2,1,0:T(8,128)(2,1)S(1)} %copy-done), channel_id=1, source_target_pairs={{0,64},{16,80},{32,96},{48,112},{64,0},{80,16},{96,32},{112,48},{1... | collective-permute-start | bytes 393224 | tf_op jit(solution)/shard_map/ppermute | solution.py:99
  191.3 24.4 %collective-permute-start.4 = (bf16[32,16,128]{2,1,0:T(8,128)(2,1)S(1)}, bf16[32,16,128]{2,1,0:T(8,128)(2,1)S(1)}, u32[]{:S(2)}, u32[]{:S(2)}) collective-permute-start(bf16[32,16,128]{2,1,0:T(8,128)(2,1)S(1)} %copy-done), channel_id=1, source_target_pairs={{0,80},{16,96},{32,112},{48,0},{64,16},{80,32},{96,48},{112,64},{1... | collective-permute-start | bytes 393224 | tf_op jit(solution)/shard_map/ppermute | solution.py:99
  198.0 39.8 %all-to-all-start.7 = ((bf16[128,4,16,128]{3,2,1,0:T(8,128)(2,1)}), bf16[128,4,16,128]{3,2,1,0:T(8,128)(2,1)S(1)}, u32[]{:S(2)}, u32[]{:S(2)}) async-start(bf16[128,4,16,128]{3,2,1,0:T(8,128)(2,1)} %broadcast_in_dim.20), calls=%async_computation.7 | async-start | bytes 4194304 | tf_op jit(solution)/shard_map/all_to_all | solution.py:75
  207.0 26.1 %collective-permute-start.5 = (bf16[32,16,128]{2,1,0:T(8,128)(2,1)S(1)}, bf16[32,16,128]{2,1,0:T(8,128)(2,1)S(1)}, u32[]{:S(2)}, u32[]{:S(2)}) collective-permute-start(bf16[32,16,128]{2,1,0:T(8,128)(2,1)S(1)} %copy-done), channel_id=1, source_target_pairs={{0,96},{16,112},{32,0},{48,16},{64,32},{80,48},{96,64},{112,80},{1... | collective-permute-start | bytes 393224 | tf_op jit(solution)/shard_map/ppermute | solution.py:99
  210.0 25.2 %collective-permute-start.6 = (bf16[32,16,128]{2,1,0:T(8,128)(2,1)S(1)}, bf16[32,16,128]{2,1,0:T(8,128)(2,1)S(1)}, u32[]{:S(2)}, u32[]{:S(2)}) collective-permute-start(bf16[32,16,128]{2,1,0:T(8,128)(2,1)S(1)} %copy-done), channel_id=1, source_target_pairs={{0,112},{16,0},{32,16},{48,32},{64,48},{80,64},{96,80},{112,96},{1... | collective-permute-start | bytes 393224 | tf_op jit(solution)/shard_map/ppermute | solution.py:99

commit v5 on v4

--- a/solution.py
+++ b/solution.py
@@ -98,13 +98,15 @@
         ring = [(i, (i + k) % col_size) for i in range(col_size)]
         blocks.append(lax.ppermute(integrals, "col", ring))
     owner_of = (rank - jnp.arange(col_size)) % col_size
-    k_full = jnp.take(jnp.stack(blocks), owner_of, axis=0).astype(jnp.float32)
     full_energy = pno_energy.reshape(pair_dev, col_size, 1, row_count, 1)
     denom_full = full_energy + pno_energy[:, None, None, None, :] + shift[:, None, None, None, None]
-    weight = k_full / jnp.swapaxes(denom_full[:, :, 0], 0, 1)
     for sweep in range(SWEEPS):
         colamp = column_amplitudes(amplitudes, one_hot, pair_size, col_size)
         partial = couple(intersections, colamp, links, nlive, col_size)
+        if sweep == 0:
+            partial, blocks = lax.optimization_barrier((partial, blocks))
+            k_full = jnp.take(jnp.stack(blocks), owner_of, axis=0).astype(jnp.float32)
+            weight = k_full / jnp.swapaxes(denom_full[:, :, 0], 0, 1)
         if sweep < SWEEPS - 1:
             parts = lax.all_to_all(partial, "col", 0, 0, tiled=True)
             coupled = jnp.sum(parts.astype(jnp.float32), axis=0)

time: 280 us -> 276 us (0.986)
  blocking collectives: 129 us -> 141 us
  waiting for transfers between devices: 49.2 us -> 38.9 us
  starting transfers between devices: 36.5 us -> 32.4 us
    ppermute x7, waiting for transfers between devices: 18.2 us -> 1.58 us  [per_device(): blocks.append(lax.ppermute(integrals, 'col', ring))]
    all_to_all x2 -> x3, blocking collectives: 30.4 us -> 46.4 us  [column_amplitudes(): parts = lax.all_to_all(contrib, 'pair', 0, 0, tiled=True)]
    all_to_all x2, waiting for transfers between devices: 28.9 us -> 37.3 us  [column_amplitudes(): got = lax.all_to_all(sent, ('pair', 'col'), 0, 0, tiled=True)]
    all_to_all x1 -> x0, starting transfers between devices: 3.57 us -> none  [column_amplitudes(): parts = lax.all_to_all(contrib, 'pair', 0, 0, tiled=True)]
    all_to_all x2, starting transfers between devices: 16.7 us -> 13.4 us  [column_amplitudes(): got = lax.all_to_all(sent, ('pair', 'col'), 0, 0, tiled=True)]
    ppermute x7, starting transfers between devices: 16.3 us -> 19.1 us  [per_device(): blocks.append(lax.ppermute(integrals, 'col', ring))]
  transfers between devices with their start and end apart: 10 -> 9, of which waited for: 4 -> 3; matrix products, arithmetic and copies ran while one was open for 3% -> 3% of each run, Pallas kernels for 0% -> 5%
where the time goes in v5:
time: 276 us; the launch traced here: 275 us
  blocking collectives  141 us (51%)
  Pallas kernels  39 us (14%)
  waiting for transfers between devices  38.9 us (14%)
  starting transfers between devices  32.4 us (12%)
  local copies, waits for them, and re-layouts  15.7 us (6%)
  other arithmetic  5.33 us (2%)
    all_to_all x3, blocking collectives, column_amplitudes(): parts = lax.all_to_all(contrib, 'pair', 0, 0, tiled=True)  46.4 us
    all_to_all x2, blocking collectives, per_device(): parts = lax.all_to_all(partial, 'col', 0, 0, tiled=True)  39.3 us
    pallas_call x3, Pallas kernels, couple(): pl.pallas_call(functools.partial(couple_kernel, slot_dev), grid_spec=grid...  39 us
    all_to_all x2, waiting for transfers between devices, column_amplitudes(): got = lax.all_to_all(sent, ('pair', 'col'), 0, 0, tiled=True)  37.3 us
    all_to_all x1, blocking collectives, column_amplitudes(): got = lax.all_to_all(sent, ('pair', 'col'), 0, 0, tiled=True)  33.7 us
    all_to_all x1, blocking collectives, per_device(): lax.all_to_all(jnp.concatenate([partial, extra], axis=1), 'col', 0, 0, ti...  21.6 us
    ppermute x7, starting transfers between devices, per_device(): blocks.append(lax.ppermute(integrals, 'col', ring))  19.1 us
    all_to_all x2, starting transfers between devices, column_amplitudes(): got = lax.all_to_all(sent, ('pair', 'col'), 0, 0, tiled=True)  13.4 us
  transfers between devices with their start and end apart: 9, of which 3 were waited for; matrix products, arithmetic and copies ran while one was open for 3% of the time, Pallas kernels for 5%

profile of v5, /device:TPU:0, one launch (start us, length us, event | category | flops | bytes accessed | tf_op | source)
XLA Modules:
  0.0 275.2 jit_solution(7489959321239509148)
XLA Ops:
  4.0 16.5 %all_to_all.48 = f32[16,4,2048]{2,1,0:T(4,128)S(1)} all-to-all(f32[16,4,2048]{2,1,0:T(4,128)S(1)} %copy.17), channel_id=1, replica_groups=mesh['col'=8,'pair'=16] {'pair'}, dimensions={0} | all-to-all | bytes 1048576 | tf_op jit(solution)/shard_map/all_to_all | solution.py:70
  20.6 1.9 broadcast_in_dim.18
  22.5 8.6 %all-to-all-start.1 = ((bf16[128,4,16,128]{3,2,1,0:T(8,128)(2,1)}), bf16[128,4,16,128]{3,2,1,0:T(8,128)(2,1)S(1)}, u32[]{:S(2)}, u32[]{:S(2)}) async-start(bf16[128,4,16,128]{3,2,1,0:T(8,128)(2,1)} %broadcast_in_dim.18), calls=%async_computation.1 | async-start | bytes 4194304 | tf_op jit(solution)/shard_map/all_to_all | solution.py:75
  31.1 2.9 %collective-permute-start = (bf16[32,16,128]{2,1,0:T(8,128)(2,1)S(1)}, bf16[32,16,128]{2,1,0:T(8,128)(2,1)S(1)}, u32[]{:S(2)}, u32[]{:S(2)}) collective-permute-start(bf16[32,16,128]{2,1,0:T(8,128)(2,1)S(1)} %copy-done), channel_id=1, source_target_pairs={{0,16},{16,32},{32,48},{48,64},{64,80},{80,96},{96,112},{112,0},{1... | collective-permute-start | bytes 393224 | tf_op jit(solution)/shard_map/ppermute | solution.py:99
  34.0 1.5 collective-permute-start.1
  35.6 1.7 collective-permute-start.2
  37.2 2.0 collective-permute-start.3
  39.3 5.1 %collective-permute-start.4 = (bf16[32,16,128]{2,1,0:T(8,128)(2,1)S(1)}, bf16[32,16,128]{2,1,0:T(8,128)(2,1)S(1)}, u32[]{:S(2)}, u32[]{:S(2)}) collective-permute-start(bf16[32,16,128]{2,1,0:T(8,128)(2,1)S(1)} %copy-done), channel_id=1, source_target_pairs={{0,80},{16,96},{32,112},{48,0},{64,16},{80,32},{96,48},{112,64},{1... | collective-permute-start | bytes 393224 | tf_op jit(solution)/shard_map/ppermute | solution.py:99
  44.5 15.7 %all-to-all-done.1 = bf16[128,4,16,128]{3,2,1,0:T(8,128)(2,1)S(1)} async-done(((bf16[128,4,16,128]{3,2,1,0:T(8,128)(2,1)}), bf16[128,4,16,128]{3,2,1,0:T(8,128)(2,1)S(1)}, u32[]{:S(2)}, u32[]{:S(2)}) %all-to-all-start.1) | async-done | bytes 2097184 | tf_op jit(solution)/shard_map/all_to_all | solution.py:75
  60.8 1.6 collective-permute-done
  62.4 4.4 %collective-permute-start.5 = (bf16[32,16,128]{2,1,0:T(8,128)(2,1)S(1)}, bf16[32,16,128]{2,1,0:T(8,128)(2,1)S(1)}, u32[]{:S(2)}, u32[]{:S(2)}) collective-permute-start(bf16[32,16,128]{2,1,0:T(8,128)(2,1)S(1)} %copy-done), channel_id=1, source_target_pairs={{0,96},{16,112},{32,0},{48,16},{64,32},{80,48},{96,64},{112,80},{1... | collective-permute-start | bytes 393224 | tf_op jit(solution)/shard_map/ppermute | solution.py:99
  68.2 13.0 %shard_map.86 = bf16[8,32,16,128]{3,2,1,0:T(8,128)(2,1)S(1)} custom-call(s32[512]{0:T(512)S(1)} %reshape.250.links_ref, s32[32]{0:T(128)S(1)} %subtract_clamp_fusion.nlive_ref, bf16[32,16,128,128]{3,2,1,0:T(8,128)(2,1)} %tiles_ref.5, bf16[64,128,128]{2,1,0:T(8,128)(2,1)S(1)} %bitcast.61), custom_call_target="tpu_custom_call" | custom-call | flops 4294967296 | bytes 19922944 | tf_op jit(solution)/shard_map/pallas_call | solution.py:50
  81.3 18.6 %all_to_all.49 = bf16[8,32,16,128]{3,2,1,0:T(8,128)(2,1)S(1)} all-to-all(bf16[8,32,16,128]{3,2,1,0:T(8,128)(2,1)S(1)} %shard_map.86), channel_id=1, replica_groups=mesh['col'=8,'pair'=16] {'col'}, dimensions={0} | all-to-all | bytes 2097152 | tf_op jit(solution)/shard_map/all_to_all | solution.py:111
  101.1 16.0 %all_to_all.50 = f32[16,4,2048]{2,1,0:T(4,128)S(1)} all-to-all(f32[16,4,2048]{2,1,0:T(4,128)S(1)} %copy.19), channel_id=1, replica_groups=mesh['col'=8,'pair'=16] {'pair'}, dimensions={0} | all-to-all | bytes 1048576 | tf_op jit(solution)/shard_map/all_to_all | solution.py:70
  117.8 33.7 %all_to_all.51 = bf16[128,4,16,128]{3,2,1,0:T(8,128)(2,1)S(1)} all-to-all(bf16[128,4,16,128]{3,2,1,0:T(8,128)(2,1)S(1)} %broadcast_in_dim.19), channel_id=1, replica_groups=mesh['col'=8,'pair'=16] {'pair','col'}, dimensions={0} | all-to-all | bytes 4194304 | tf_op jit(solution)/shard_map/all_to_all | solution.py:75
  152.0 13.0 %shard_map.87 = bf16[8,32,16,128]{3,2,1,0:T(8,128)(2,1)S(1)} custom-call(s32[512]{0:T(512)S(1)} %reshape.250.links_ref, s32[32]{0:T(128)S(1)} %subtract_clamp_fusion.nlive_ref, bf16[32,16,128,128]{3,2,1,0:T(8,128)(2,1)} %tiles_ref.5, bf16[64,128,128]{2,1,0:T(8,128)(2,1)S(1)} %bitcast.63), custom_call_target="tpu_custom_call" | custom-call | flops 4294967296 | bytes 19922944 | tf_op jit(solution)/shard_map/pallas_call | solution.py:50
  165.0 20.6 %all_to_all.52 = bf16[8,32,16,128]{3,2,1,0:T(8,128)(2,1)S(1)} all-to-all(bf16[8,32,16,128]{3,2,1,0:T(8,128)(2,1)S(1)} %shard_map.87), channel_id=1, replica_groups=mesh['col'=8,'pair'=16] {'col'}, dimensions={0} | all-to-all | bytes 2097152 | tf_op jit(solution)/shard_map/all_to_all | solution.py:111
  186.8 13.8 %all_to_all.53 = f32[16,4,2048]{2,1,0:T(4,128)S(1)} all-to-all(f32[16,4,2048]{2,1,0:T(4,128)S(1)} %copy.21), channel_id=1, replica_groups=mesh['col'=8,'pair'=16] {'pair'}, dimensions={0} | all-to-all | bytes 1048576 | tf_op jit(solution)/shard_map/all_to_all | solution.py:70
  200.8 1.9 broadcast_in_dim.20
  202.7 4.8 %all-to-all-start.7 = ((bf16[128,4,16,128]{3,2,1,0:T(8,128)(2,1)}), bf16[128,4,16,128]{3,2,1,0:T(8,128)(2,1)S(1)}, u32[]{:S(2)}, u32[]{:S(2)}) async-start(bf16[128,4,16,128]{3,2,1,0:T(8,128)(2,1)} %broadcast_in_dim.20), calls=%async_computation.7 | async-start | bytes 4194304 | tf_op jit(solution)/shard_map/all_to_all | solution.py:75
  213.0 2.0 gather_fusion
  214.9 21.6 %all-to-all-done.7 = bf16[128,4,16,128]{3,2,1,0:T(8,128)(2,1)S(1)} async-done(((bf16[128,4,16,128]{3,2,1,0:T(8,128)(2,1)}), bf16[128,4,16,128]{3,2,1,0:T(8,128)(2,1)S(1)}, u32[]{:S(2)}, u32[]{:S(2)}) %all-to-all-start.7) | async-done | bytes 2097184 | tf_op jit(solution)/shard_map/all_to_all | solution.py:75
  237.1 13.0 %shard_map.88 = bf16[8,32,16,128]{3,2,1,0:T(8,128)(2,1)S(1)} custom-call(s32[512]{0:T(512)S(1)} %reshape.250.links_ref, s32[32]{0:T(128)S(1)} %subtract_clamp_fusion.nlive_ref, bf16[32,16,128,128]{3,2,1,0:T(8,128)(2,1)} %tiles_ref.5, bf16[64,128,128]{2,1,0:T(8,128)(2,1)S(1)} %bitcast.62), custom_call_target="tpu_custom_call" | custom-call | flops 4294967296 | bytes 19922944 | tf_op jit(solution)/shard_map/pallas_call | solution.py:50
  251.9 21.6 %all_to_all.54 = bf16[8,33,16,128]{3,2,1,0:T(8,128)(2,1)S(1)} all-to-all(bf16[8,33,16,128]{3,2,1,0:T(8,128)(2,1)S(1)} %pad_maximum_fusion), channel_id=1, replica_groups=mesh['col'=8,'pair'=16] {'col'}, dimensions={0} | all-to-all | bytes 2162688 | tf_op jit(solution)/shard_map/all_to_all | solution.py:120
  (73 shorter events, 18.7 us)
Async XLA Ops:
  22.5 8.6 %copy-start = (bf16[32,16,128]{2,1,0:T(8,128)(2,1)S(1)}, bf16[32,16,128]{2,1,0:T(8,128)(2,1)}, u32[]{:S(2)}) copy-start(bf16[32,16,128]{2,1,0:T(8,128)(2,1)} %param.11) | copy-start | bytes 393220
  22.5 21.8 %copy-start.3 = (s32[32,16]{0,1:T(8,128)S(1)}, s32[32,16]{0,1:T(8,128)}, u32[]{:S(2)}) copy-start(s32[32,16]{0,1:T(8,128)} %param.15) | copy-start | bytes 6148
  22.5 22.0 %copy-start.5 = (s32[32]{0:T(128)S(1)}, s32[32]{0:T(128)}, u32[]{:S(2)}) copy-start(s32[32]{0:T(128)} %param.16) | copy-start | bytes 388
  22.5 37.7 %all-to-all-start.1 = ((bf16[128,4,16,128]{3,2,1,0:T(8,128)(2,1)}), bf16[128,4,16,128]{3,2,1,0:T(8,128)(2,1)S(1)}, u32[]{:S(2)}, u32[]{:S(2)}) async-start(bf16[128,4,16,128]{3,2,1,0:T(8,128)(2,1)} %broadcast_in_dim.18), calls=%async_computation.1 | async-start | bytes 4194304 | tf_op jit(solution)/shard_map/all_to_all | solution.py:75
  31.1 31.2 %collective-permute-start = (bf16[32,16,128]{2,1,0:T(8,128)(2,1)S(1)}, bf16[32,16,128]{2,1,0:T(8,128)(2,1)S(1)}, u32[]{:S(2)}, u32[]{:S(2)}) collective-permute-start(bf16[32,16,128]{2,1,0:T(8,128)(2,1)S(1)} %copy-done), channel_id=1, source_target_pairs={{0,16},{16,32},{32,48},{48,64},{64,80},{80,96},{96,112},{112,0},{1... | collective-permute-start | bytes 393224 | tf_op jit(solution)/shard_map/ppermute | solution.py:99
  34.0 32.7 %collective-permute-start.1 = (bf16[32,16,128]{2,1,0:T(8,128)(2,1)S(1)}, bf16[32,16,128]{2,1,0:T(8,128)(2,1)S(1)}, u32[]{:S(2)}, u32[]{:S(2)}) collective-permute-start(bf16[32,16,128]{2,1,0:T(8,128)(2,1)S(1)} %copy-done), channel_id=1, source_target_pairs={{0,32},{16,48},{32,64},{48,80},{64,96},{80,112},{96,0},{112,16},{1... | collective-permute-start | bytes 393224 | tf_op jit(solution)/shard_map/ppermute | solution.py:99
  35.6 45.7 %collective-permute-start.2 = (bf16[32,16,128]{2,1,0:T(8,128)(2,1)S(1)}, bf16[32,16,128]{2,1,0:T(8,128)(2,1)S(1)}, u32[]{:S(2)}, u32[]{:S(2)}) collective-permute-start(bf16[32,16,128]{2,1,0:T(8,128)(2,1)S(1)} %copy-done), channel_id=1, source_target_pairs={{0,48},{16,64},{32,80},{48,96},{64,112},{80,0},{96,16},{112,32},{1... | collective-permute-start | bytes 393224 | tf_op jit(solution)/shard_map/ppermute | solution.py:99
  37.2 44.0 %collective-permute-start.3 = (bf16[32,16,128]{2,1,0:T(8,128)(2,1)S(1)}, bf16[32,16,128]{2,1,0:T(8,128)(2,1)S(1)}, u32[]{:S(2)}, u32[]{:S(2)}) collective-permute-start(bf16[32,16,128]{2,1,0:T(8,128)(2,1)S(1)} %copy-done), channel_id=1, source_target_pairs={{0,64},{16,80},{32,96},{48,112},{64,0},{80,16},{96,32},{112,48},{1... | collective-permute-start | bytes 393224 | tf_op jit(solution)/shard_map/ppermute | solution.py:99
  39.3 42.0 %collective-permute-start.4 = (bf16[32,16,128]{2,1,0:T(8,128)(2,1)S(1)}, bf16[32,16,128]{2,1,0:T(8,128)(2,1)S(1)}, u32[]{:S(2)}, u32[]{:S(2)}) collective-permute-start(bf16[32,16,128]{2,1,0:T(8,128)(2,1)S(1)} %copy-done), channel_id=1, source_target_pairs={{0,80},{16,96},{32,112},{48,0},{64,16},{80,32},{96,48},{112,64},{1... | collective-permute-start | bytes 393224 | tf_op jit(solution)/shard_map/ppermute | solution.py:99
  62.4 18.9 %collective-permute-start.5 = (bf16[32,16,128]{2,1,0:T(8,128)(2,1)S(1)}, bf16[32,16,128]{2,1,0:T(8,128)(2,1)S(1)}, u32[]{:S(2)}, u32[]{:S(2)}) collective-permute-start(bf16[32,16,128]{2,1,0:T(8,128)(2,1)S(1)} %copy-done), channel_id=1, source_target_pairs={{0,96},{16,112},{32,0},{48,16},{64,32},{80,48},{96,64},{112,80},{1... | collective-permute-start | bytes 393224 | tf_op jit(solution)/shard_map/ppermute | solution.py:99
  66.7 14.6 %collective-permute-start.6 = (bf16[32,16,128]{2,1,0:T(8,128)(2,1)S(1)}, bf16[32,16,128]{2,1,0:T(8,128)(2,1)S(1)}, u32[]{:S(2)}, u32[]{:S(2)}) collective-permute-start(bf16[32,16,128]{2,1,0:T(8,128)(2,1)S(1)} %copy-done), channel_id=1, source_target_pairs={{0,112},{16,0},{32,16},{48,32},{64,48},{80,64},{96,80},{112,96},{1... | collective-permute-start | bytes 393224 | tf_op jit(solution)/shard_map/ppermute | solution.py:99
  81.2 18.8 %copy-start.1 = (f32[32,128]{1,0:T(8,128)S(1)}, f32[32,128]{1,0:T(8,128)}, u32[]{:S(2)}) copy-start(f32[32,128]{1,0:T(8,128)} %param.12) | copy-start | bytes 49156
  81.2 18.8 %copy-start.2 = (f32[32]{0:T(128)S(1)}, f32[32]{0:T(128)}, u32[]{:S(2)}) copy-start(f32[32]{0:T(128)} %param.13) | copy-start | bytes 388
  81.2 19.1 %copy-start.4 = (s32[32]{0:T(128)S(1)}, s32[32]{0:T(128)}, u32[]{:S(2)}) copy-start(s32[32]{0:T(128)} %param.17) | copy-start | bytes 388
  202.7 33.9 %all-to-all-start.7 = ((bf16[128,4,16,128]{3,2,1,0:T(8,128)(2,1)}), bf16[128,4,16,128]{3,2,1,0:T(8,128)(2,1)S(1)}, u32[]{:S(2)}, u32[]{:S(2)}) async-start(bf16[128,4,16,128]{3,2,1,0:T(8,128)(2,1)} %broadcast_in_dim.20), calls=%async_computation.7 | async-start | bytes 4194304 | tf_op jit(solution)/shard_map/all_to_all | solution.py:75

commit v6 on v5

--- a/solution.py
+++ b/solution.py
@@ -67,14 +67,15 @@
         one_hot, amplitudes.reshape(pair_dev, rows * width), precision=lax.Precision.HIGHEST
     )
     per = ncol // pair_size
-    parts = lax.all_to_all(contrib, "pair", 0, 0, tiled=True)
+    parts = lax.all_to_all(contrib, ("core", "ph"), 0, 0, tiled=True)
     mine = jnp.sum(parts.reshape(pair_size, per, rows * width), axis=0)
     mine = mine.astype(jnp.bfloat16).reshape(1, per, rows, width)
-    everyone = pair_size * col_size
-    sent = jnp.broadcast_to(mine, (everyone, per, rows, width))
-    got = lax.all_to_all(sent, ("pair", "col"), 0, 0, tiled=True)
-    got = got.reshape(pair_size, col_size, per, rows, width)
-    return got.transpose(0, 2, 1, 3, 4).reshape(ncol, col_size * rows, width)
+    peers = pair_size // 2 * col_size
+    sent = jnp.broadcast_to(mine, (peers, per, rows, width))
+    got = lax.all_to_all(sent, ("ph", "col"), 0, 0, tiled=True)
+    other = lax.ppermute(got, "core", [(0, 1), (1, 0)])
+    both = jnp.stack([got, other]).reshape(2, pair_size // 2, col_size, per, rows, width)
+    return both.transpose(0, 1, 3, 2, 4, 5).reshape(ncol, col_size * rows, width)
 
 
 def per_device(integrals, pno_energy, shift, intersections, links, counts, column_of):
@@ -82,7 +83,7 @@
     row_count = integrals.shape[1]
     slot_dev = intersections.shape[1]
     col_size = lax.axis_size("col")
-    pair_size = lax.axis_size("pair")
+    pair_size = lax.axis_size("ph") * lax.axis_size("core")
     ncol_all = COL_DEV * col_size
     rank = lax.axis_index("col")
     row_energy = lax.dynamic_slice_in_dim(pno_energy, rank * row_count, row_count, 1)
@@ -93,6 +94,7 @@
         jnp.float32
     )
     nlive = jnp.clip(counts - rank * slot_dev, 0, slot_dev).astype(jnp.int32)
+    local_links = (links + ncol_all // 2 * lax.axis_index("core")) % ncol_all
     blocks = [integrals]
     for k in range(1, col_size):
         ring = [(i, (i + k) % col_size) for i in range(col_size)]
@@ -102,7 +104,7 @@
     denom_full = full_energy + pno_energy[:, None, None, None, :] + shift[:, None, None, None, None]
     for sweep in range(SWEEPS):
         colamp = column_amplitudes(amplitudes, one_hot, pair_size, col_size)
-        partial = couple(intersections, colamp, links, nlive, col_size)
+        partial = couple(intersections, colamp, local_links, nlive, col_size)
         if sweep == 0:
             partial, blocks = lax.optimization_barrier((partial, blocks))
             k_full = jnp.take(jnp.stack(blocks), owner_of, axis=0).astype(jnp.float32)
@@ -128,19 +130,24 @@
 
 
 def solution(mesh):
+    col_size, pair_size = mesh.devices.shape
+    split = jax.sharding.Mesh(
+        mesh.devices.reshape(col_size, pair_size // 2, 2), ("col", "ph", "core")
+    )
+    pair = ("ph", "core")
     placed = (
-        P("pair", "col", None),
-        P("pair", None),
-        P("pair"),
-        P("pair", "col", None, None),
-        P("pair", "col"),
-        P("pair"),
-        P("pair"),
+        P(pair, "col", None),
+        P(pair, None),
+        P(pair),
+        P(pair, "col", None, None),
+        P(pair, "col"),
+        P(pair),
+        P(pair),
     )
     return jax.shard_map(
         per_device,
-        mesh=mesh,
+        mesh=split,
         in_specs=placed,
-        out_specs=(P("pair", "col", None), P("pair")),
+        out_specs=(P(pair, "col", None), P(pair)),
         check_vma=False,
     )

time: 276 us -> 257 us (0.931)
  waiting for transfers between devices: 38.9 us -> 22.7 us
  blocking collectives: 141 us -> 156 us
  starting transfers between devices: 32.4 us -> 21.8 us
  local copies, waits for them, and re-layouts: 15.7 us -> 6.88 us
    all_to_all x2 -> x1, waiting for transfers between devices: 37.3 us -> 18.2 us  [column_amplitudes(): got = lax.all_to_all(sent, ('ph', 'col'), 0, 0, tiled=True)]
    all_to_all x4 -> x5, blocking collectives: 80.1 us -> 95.5 us  [the longest x2 50.9 us: column_amplitudes(): got = lax.all_to_all(sent, ('ph', 'col'), 0, 0, tiled=True)]
    all_to_all x2 -> x1, starting transfers between devices: 13.4 us -> 5.26 us  [column_amplitudes(): got = lax.all_to_all(sent, ('ph', 'col'), 0, 0, tiled=True)]
    ppermute x0 -> x3, waiting for transfers between devices: none -> 4.52 us  [column_amplitudes(): other = lax.ppermute(got, 'core', [(0, 1), (1, 0)])]
    unnamed x24 -> x51, local copies, waits for them, and re-layouts: 4.82 us -> 0.33 us
  transfers between devices with their start and end apart: 9 -> 11, of which waited for: 3 -> 3; matrix products, arithmetic and copies ran while one was open for 3% -> 1% of each run, Pallas kernels for 5% -> 5%
where the time goes in v6:
time: 257 us
  blocking collectives  156 us (61%)
  Pallas kernels  38.8 us (15%)
  waiting for transfers between devices  22.7 us (9%)
  starting transfers between devices  21.8 us (8%)
  other arithmetic  7.13 us (3%)
  local copies, waits for them, and re-layouts  6.88 us (3%)
    all_to_all x2, blocking collectives, column_amplitudes(): got = lax.all_to_all(sent, ('ph', 'col'), 0, 0, tiled=True)  50.9 us
    all_to_all x3, blocking collectives, column_amplitudes(): parts = lax.all_to_all(contrib, ('core', 'ph'), 0, 0, tiled=True)  44.6 us
    all_to_all x2, blocking collectives, per_device(): parts = lax.all_to_all(partial, 'col', 0, 0, tiled=True)  39.8 us
    pallas_call x3, Pallas kernels, couple(): pl.pallas_call(functools.partial(couple_kernel, slot_dev), grid_spec=grid...  38.8 us
    all_to_all x1, blocking collectives, per_device(): lax.all_to_all(jnp.concatenate([partial, extra], axis=1), 'col', 0, 0, ti...  20.7 us
    all_to_all x1, waiting for transfers between devices, column_amplitudes(): got = lax.all_to_all(sent, ('ph', 'col'), 0, 0, tiled=True)  18.2 us
    ppermute x7, starting transfers between devices, per_device(): blocks.append(lax.ppermute(integrals, 'col', ring))  16.5 us
    all_to_all x1, starting transfers between devices, column_amplitudes(): got = lax.all_to_all(sent, ('ph', 'col'), 0, 0, tiled=True)  5.26 us
  transfers between devices with their start and end apart: 11, of which 3 were waited for; matrix products, arithmetic and copies ran while one was open for 1% of the time, Pallas kernels for 5%

profile of v6, /device:TPU:0, one launch (start us, length us, event | category | flops | bytes accessed | tf_op | source)
XLA Modules:
  0.0 256.5 jit_solution(17290945595150380413)
XLA Ops:
  1.4 1.1 fusion.1
  4.0 16.8 %all_to_all.48 = f32[16,4,2048]{2,1,0:T(4,128)S(1)} all-to-all(f32[16,4,2048]{2,1,0:T(4,128)S(1)} %copy.17), channel_id=1, replica_groups=mesh['col'=8,'ph'=8,'core'=2] {'core','ph'}, dimensions={0} | all-to-all | bytes 1048576 | tf_op jit(solution)/shard_map/all_to_all | solution.py:70
  21.2 27.5 %all_to_all.49 = bf16[64,4,16,128]{3,2,1,0:T(8,128)(2,1)S(1)} all-to-all(bf16[64,4,16,128]{3,2,1,0:T(8,128)(2,1)S(1)} %broadcast_in_dim.18), channel_id=1, replica_groups=mesh['col'=8,'ph'=8,'core'=2] {'ph','col'}, dimensions={0} | all-to-all | bytes 2097152 | tf_op jit(solution)/shard_map/all_to_all | solution.py:75
  49.9 3.5 %collective-permute-start.3 = (bf16[32,16,128]{2,1,0:T(8,128)(2,1)S(1)}, bf16[32,16,128]{2,1,0:T(8,128)(2,1)S(1)}, u32[]{:S(2)}, u32[]{:S(2)}) collective-permute-start(bf16[32,16,128]{2,1,0:T(8,128)(2,1)S(1)} %copy-done), channel_id=1, source_target_pairs={{0,48},{16,64},{32,80},{48,96},{64,112},{80,0},{96,16},{112,32},{1... | collective-permute-start | bytes 393224 | tf_op jit(solution)/shard_map/ppermute | solution.py:101
  53.4 3.0 %collective-permute-start.4 = (bf16[32,16,128]{2,1,0:T(8,128)(2,1)S(1)}, bf16[32,16,128]{2,1,0:T(8,128)(2,1)S(1)}, u32[]{:S(2)}, u32[]{:S(2)}) collective-permute-start(bf16[32,16,128]{2,1,0:T(8,128)(2,1)S(1)} %copy-done), channel_id=1, source_target_pairs={{0,64},{16,80},{32,96},{48,112},{64,0},{80,16},{96,32},{112,48},{1... | collective-permute-start | bytes 393224 | tf_op jit(solution)/shard_map/ppermute | solution.py:101
  56.6 1.3 collective-permute-start.5
  58.7 1.7 collective-permute-start.6
  60.4 5.9 %collective-permute-start.7 = (bf16[32,16,128]{2,1,0:T(8,128)(2,1)S(1)}, bf16[32,16,128]{2,1,0:T(8,128)(2,1)S(1)}, u32[]{:S(2)}, u32[]{:S(2)}) collective-permute-start(bf16[32,16,128]{2,1,0:T(8,128)(2,1)S(1)} %copy-done), channel_id=1, source_target_pairs={{0,112},{16,0},{32,16},{48,32},{64,48},{80,64},{96,80},{112,96},{1... | collective-permute-start | bytes 393224 | tf_op jit(solution)/shard_map/ppermute | solution.py:101
  66.3 12.9 %shard_map.86 = bf16[8,32,16,128]{3,2,1,0:T(8,128)(2,1)S(1)} custom-call(s32[512]{0:T(512)S(1)} %reshape.256.links_ref, s32[32]{0:T(128)S(1)} %subtract_clamp_fusion.nlive_ref, bf16[32,16,128,128]{3,2,1,0:T(8,128)(2,1)} %tiles_ref.5, bf16[64,128,128]{2,1,0:T(8,128)(2,1)S(1)} %bitcast.64), custom_call_target="tpu_custom_call" | custom-call | flops 4294967296 | bytes 19922944 | tf_op jit(solution)/shard_map/pallas_call | solution.py:50
  79.3 20.0 %all_to_all.50 = bf16[8,32,16,128]{3,2,1,0:T(8,128)(2,1)S(1)} all-to-all(bf16[8,32,16,128]{3,2,1,0:T(8,128)(2,1)S(1)} %shard_map.86), channel_id=1, replica_groups=mesh['col'=8,'ph'=8,'core'=2] {'col'}, dimensions={0} | all-to-all | bytes 2097152 | tf_op jit(solution)/shard_map/all_to_all | solution.py:113
  100.6 13.7 %all_to_all.51 = f32[16,4,2048]{2,1,0:T(4,128)S(1)} all-to-all(f32[16,4,2048]{2,1,0:T(4,128)S(1)} %copy.19), channel_id=1, replica_groups=mesh['col'=8,'ph'=8,'core'=2] {'core','ph'}, dimensions={0} | all-to-all | bytes 1048576 | tf_op jit(solution)/shard_map/all_to_all | solution.py:70
  114.7 23.4 %all_to_all.52 = bf16[64,4,16,128]{3,2,1,0:T(8,128)(2,1)S(1)} all-to-all(bf16[64,4,16,128]{3,2,1,0:T(8,128)(2,1)S(1)} %broadcast_in_dim.19), channel_id=1, replica_groups=mesh['col'=8,'ph'=8,'core'=2] {'ph','col'}, dimensions={0} | all-to-all | bytes 2097152 | tf_op jit(solution)/shard_map/all_to_all | solution.py:75
  138.0 2.7 %collective-permute-done.8 = bf16[64,4,16,128]{3,2,1,0:T(8,128)(2,1)S(1)} collective-permute-done((bf16[64,4,16,128]{3,2,1,0:T(8,128)(2,1)S(1)}, bf16[64,4,16,128]{3,2,1,0:T(8,128)(2,1)S(1)}, u32[]{:S(2)}, u32[]{:S(2)}) %collective-permute-start.8) | collective-permute-done | bytes 1048608 | tf_op jit(solution)/shard_map/ppermute | solution.py:76
  141.5 12.9 %shard_map.87 = bf16[8,32,16,128]{3,2,1,0:T(8,128)(2,1)S(1)} custom-call(s32[512]{0:T(512)S(1)} %reshape.256.links_ref, s32[32]{0:T(128)S(1)} %subtract_clamp_fusion.nlive_ref, bf16[32,16,128,128]{3,2,1,0:T(8,128)(2,1)} %tiles_ref.5, bf16[64,128,128]{2,1,0:T(8,128)(2,1)S(1)} %bitcast.66), custom_call_target="tpu_custom_call" | custom-call | flops 4294967296 | bytes 19922944 | tf_op jit(solution)/shard_map/pallas_call | solution.py:50
  154.4 19.9 %all_to_all.53 = bf16[8,32,16,128]{3,2,1,0:T(8,128)(2,1)S(1)} all-to-all(bf16[8,32,16,128]{3,2,1,0:T(8,128)(2,1)S(1)} %shard_map.87), channel_id=1, replica_groups=mesh['col'=8,'ph'=8,'core'=2] {'col'}, dimensions={0} | all-to-all | bytes 2097152 | tf_op jit(solution)/shard_map/all_to_all | solution.py:113
  175.4 14.0 %all_to_all.54 = f32[16,4,2048]{2,1,0:T(4,128)S(1)} all-to-all(f32[16,4,2048]{2,1,0:T(4,128)S(1)} %copy.21), channel_id=1, replica_groups=mesh['col'=8,'ph'=8,'core'=2] {'core','ph'}, dimensions={0} | all-to-all | bytes 1048576 | tf_op jit(solution)/shard_map/all_to_all | solution.py:70
  189.6 1.2 broadcast_in_dim.20
  190.8 5.3 %all-to-all-start.7 = ((bf16[64,4,16,128]{3,2,1,0:T(8,128)(2,1)}), bf16[64,4,16,128]{3,2,1,0:T(8,128)(2,1)S(1)}, u32[]{:S(2)}, u32[]{:S(2)}) async-start(bf16[64,4,16,128]{3,2,1,0:T(8,128)(2,1)} %broadcast_in_dim.20), calls=%async_computation.7 | async-start | bytes 2097152 | tf_op jit(solution)/shard_map/all_to_all | solution.py:75
  196.4 18.2 %all-to-all-done.7 = bf16[64,4,16,128]{3,2,1,0:T(8,128)(2,1)S(1)} async-done(((bf16[64,4,16,128]{3,2,1,0:T(8,128)(2,1)}), bf16[64,4,16,128]{3,2,1,0:T(8,128)(2,1)S(1)}, u32[]{:S(2)}, u32[]{:S(2)}) %all-to-all-start.7) | async-done | bytes 1048608 | tf_op jit(solution)/shard_map/all_to_all | solution.py:75
  215.6 1.9 collective-permute-done.9
  217.4 1.4 maximum_bitcast_fusion.2
  219.4 12.9 %shard_map.88 = bf16[8,32,16,128]{3,2,1,0:T(8,128)(2,1)S(1)} custom-call(s32[512]{0:T(512)S(1)} %reshape.256.links_ref, s32[32]{0:T(128)S(1)} %subtract_clamp_fusion.nlive_ref, bf16[32,16,128,128]{3,2,1,0:T(8,128)(2,1)} %tiles_ref.5, bf16[64,128,128]{2,1,0:T(8,128)(2,1)S(1)} %bitcast.65), custom_call_target="tpu_custom_call" | custom-call | flops 4294967296 | bytes 19922944 | tf_op jit(solution)/shard_map/pallas_call | solution.py:50
  232.3 1.4 fusion
  234.1 20.7 %all_to_all.55 = bf16[8,33,16,128]{3,2,1,0:T(8,128)(2,1)S(1)} all-to-all(bf16[8,33,16,128]{3,2,1,0:T(8,128)(2,1)S(1)} %pad_maximum_fusion), channel_id=1, replica_groups=mesh['col'=8,'ph'=8,'core'=2] {'col'}, dimensions={0} | all-to-all | bytes 2162688 | tf_op jit(solution)/shard_map/all_to_all | solution.py:122
  (110 shorter events, 11.9 us)
Async XLA Ops:
  20.8 27.9 %copy-start = (bf16[32,16,128]{2,1,0:T(8,128)(2,1)S(1)}, bf16[32,16,128]{2,1,0:T(8,128)(2,1)}, u32[]{:S(2)}) copy-start(bf16[32,16,128]{2,1,0:T(8,128)(2,1)} %param.11) | copy-start | bytes 393220
  20.8 35.6 %copy-start.17 = (s32[32,16]{0,1:T(8,128)S(1)}, s32[32,16]{0,1:T(8,128)}, u32[]{:S(2)}) copy-start(s32[32,16]{0,1:T(8,128)} %param.15) | copy-start | bytes 6148
  20.8 35.8 %copy-start.19 = (s32[32]{0:T(128)S(1)}, s32[32]{0:T(128)}, u32[]{:S(2)}) copy-start(s32[32]{0:T(128)} %param.16) | copy-start | bytes 388
  48.7 7.9 %collective-permute-start = (bf16[64,4,16,128]{3,2,1,0:T(8,128)(2,1)S(1)}, bf16[64,4,16,128]{3,2,1,0:T(8,128)(2,1)S(1)}, u32[]{:S(2)}, u32[]{:S(2)}) collective-permute-start(bf16[64,4,16,128]{3,2,1,0:T(8,128)(2,1)S(1)} %all_to_all.49), channel_id=1, source_target_pairs={{0,1},{1,0},{2,3},{3,2},{4,5},{5,4},{6,7},{7,6},{8,9},{9,8},{10,11... | collective-permute-start | bytes 3145736 | tf_op jit(solution)/shard_map/ppermute | solution.py:76
  48.7 9.9 %collective-permute-start.1 = (bf16[32,16,128]{2,1,0:T(8,128)(2,1)S(1)}, bf16[32,16,128]{2,1,0:T(8,128)(2,1)S(1)}, u32[]{:S(2)}, u32[]{:S(2)}) collective-permute-start(bf16[32,16,128]{2,1,0:T(8,128)(2,1)S(1)} %copy-done), channel_id=1, source_target_pairs={{0,16},{16,32},{32,48},{48,64},{64,80},{80,96},{96,112},{112,0},{1... | collective-permute-start | bytes 393224 | tf_op jit(solution)/shard_map/ppermute | solution.py:101
  49.4 11.0 %collective-permute-start.2 = (bf16[32,16,128]{2,1,0:T(8,128)(2,1)S(1)}, bf16[32,16,128]{2,1,0:T(8,128)(2,1)S(1)}, u32[]{:S(2)}, u32[]{:S(2)}) collective-permute-start(bf16[32,16,128]{2,1,0:T(8,128)(2,1)S(1)} %copy-done), channel_id=1, source_target_pairs={{0,32},{16,48},{32,64},{48,80},{64,96},{80,112},{96,0},{112,16},{1... | collective-permute-start | bytes 393224 | tf_op jit(solution)/shard_map/ppermute | solution.py:101
  49.9 29.3 %collective-permute-start.3 = (bf16[32,16,128]{2,1,0:T(8,128)(2,1)S(1)}, bf16[32,16,128]{2,1,0:T(8,128)(2,1)S(1)}, u32[]{:S(2)}, u32[]{:S(2)}) collective-permute-start(bf16[32,16,128]{2,1,0:T(8,128)(2,1)S(1)} %copy-done), channel_id=1, source_target_pairs={{0,48},{16,64},{32,80},{48,96},{64,112},{80,0},{96,16},{112,32},{1... | collective-permute-start | bytes 393224 | tf_op jit(solution)/shard_map/ppermute | solution.py:101
  53.4 25.9 %collective-permute-start.4 = (bf16[32,16,128]{2,1,0:T(8,128)(2,1)S(1)}, bf16[32,16,128]{2,1,0:T(8,128)(2,1)S(1)}, u32[]{:S(2)}, u32[]{:S(2)}) collective-permute-start(bf16[32,16,128]{2,1,0:T(8,128)(2,1)S(1)} %copy-done), channel_id=1, source_target_pairs={{0,64},{16,80},{32,96},{48,112},{64,0},{80,16},{96,32},{112,48},{1... | collective-permute-start | bytes 393224 | tf_op jit(solution)/shard_map/ppermute | solution.py:101
  56.6 22.7 %collective-permute-start.5 = (bf16[32,16,128]{2,1,0:T(8,128)(2,1)S(1)}, bf16[32,16,128]{2,1,0:T(8,128)(2,1)S(1)}, u32[]{:S(2)}, u32[]{:S(2)}) collective-permute-start(bf16[32,16,128]{2,1,0:T(8,128)(2,1)S(1)} %copy-done), channel_id=1, source_target_pairs={{0,80},{16,96},{32,112},{48,0},{64,16},{80,32},{96,48},{112,64},{1... | collective-permute-start | bytes 393224 | tf_op jit(solution)/shard_map/ppermute | solution.py:101
  58.7 20.5 %copy-start.6 = (bf16[32,16,128]{2,1,0:T(8,128)(2,1)}, bf16[32,16,128]{2,1,0:T(8,128)(2,1)S(1)}, u32[]{:S(2)}) copy-start(bf16[32,16,128]{2,1,0:T(8,128)(2,1)S(1)} %collective-permute-done.1) | copy-start | bytes 393220
  58.7 20.6 %collective-permute-start.6 = (bf16[32,16,128]{2,1,0:T(8,128)(2,1)S(1)}, bf16[32,16,128]{2,1,0:T(8,128)(2,1)S(1)}, u32[]{:S(2)}, u32[]{:S(2)}) collective-permute-start(bf16[32,16,128]{2,1,0:T(8,128)(2,1)S(1)} %copy-done), channel_id=1, source_target_pairs={{0,96},{16,112},{32,0},{48,16},{64,32},{80,48},{96,64},{112,80},{1... | collective-permute-start | bytes 393224 | tf_op jit(solution)/shard_map/ppermute | solution.py:101
  60.4 18.9 %collective-permute-start.7 = (bf16[32,16,128]{2,1,0:T(8,128)(2,1)S(1)}, bf16[32,16,128]{2,1,0:T(8,128)(2,1)S(1)}, u32[]{:S(2)}, u32[]{:S(2)}) collective-permute-start(bf16[32,16,128]{2,1,0:T(8,128)(2,1)S(1)} %copy-done), channel_id=1, source_target_pairs={{0,112},{16,0},{32,16},{48,32},{64,48},{80,64},{96,80},{112,96},{1... | collective-permute-start | bytes 393224 | tf_op jit(solution)/shard_map/ppermute | solution.py:101
  79.2 20.6 %copy-start.18 = (s32[32]{0:T(128)S(1)}, s32[32]{0:T(128)}, u32[]{:S(2)}) copy-start(s32[32]{0:T(128)} %param.17) | copy-start | bytes 388
  79.2 20.5 %copy-start.2 = (bf16[32,16,128]{2,1,0:T(8,128)(2,1)}, bf16[32,16,128]{2,1,0:T(8,128)(2,1)S(1)}, u32[]{:S(2)}) copy-start(bf16[32,16,128]{2,1,0:T(8,128)(2,1)S(1)} %collective-permute-done.3) | copy-start | bytes 393220
  79.3 20.5 %copy-start.4 = (bf16[32,16,128]{2,1,0:T(8,128)(2,1)}, bf16[32,16,128]{2,1,0:T(8,128)(2,1)S(1)}, u32[]{:S(2)}) copy-start(bf16[32,16,128]{2,1,0:T(8,128)(2,1)S(1)} %collective-permute-done.4) | copy-start | bytes 393220
  79.3 20.5 %copy-start.10 = (bf16[32,16,128]{2,1,0:T(8,128)(2,1)}, bf16[32,16,128]{2,1,0:T(8,128)(2,1)S(1)}, u32[]{:S(2)}) copy-start(bf16[32,16,128]{2,1,0:T(8,128)(2,1)S(1)} %collective-permute-done.5) | copy-start | bytes 393220
  138.0 2.7 %collective-permute-start.8 = (bf16[64,4,16,128]{3,2,1,0:T(8,128)(2,1)S(1)}, bf16[64,4,16,128]{3,2,1,0:T(8,128)(2,1)S(1)}, u32[]{:S(2)}, u32[]{:S(2)}) collective-permute-start(bf16[64,4,16,128]{3,2,1,0:T(8,128)(2,1)S(1)} %all_to_all.52), channel_id=1, source_target_pairs={{0,1},{1,0},{2,3},{3,2},{4,5},{5,4},{6,7},{7,6},{8,9},{9,8},{10,11... | collective-permute-start | bytes 3145736 | tf_op jit(solution)/shard_map/ppermute | solution.py:76
  189.6 25.1 %copy-start.3 = (bf16[32,16,128]{2,1,0:T(8,128)(2,1)S(1)}, bf16[32,16,128]{2,1,0:T(8,128)(2,1)}, u32[]{:S(2)}) copy-start(bf16[32,16,128]{2,1,0:T(8,128)(2,1)} %copy-done.2) | copy-start | bytes 393220
  189.6 25.1 %copy-start.5 = (bf16[32,16,128]{2,1,0:T(8,128)(2,1)S(1)}, bf16[32,16,128]{2,1,0:T(8,128)(2,1)}, u32[]{:S(2)}) copy-start(bf16[32,16,128]{2,1,0:T(8,128)(2,1)} %copy-done.4) | copy-start | bytes 393220
  190.8 23.9 %copy-start.11 = (bf16[32,16,128]{2,1,0:T(8,128)(2,1)S(1)}, bf16[32,16,128]{2,1,0:T(8,128)(2,1)}, u32[]{:S(2)}) copy-start(bf16[32,16,128]{2,1,0:T(8,128)(2,1)} %copy-done.10) | copy-start | bytes 393220
  190.8 23.9 %copy-start.13 = (bf16[32,16,128]{2,1,0:T(8,128)(2,1)S(1)}, bf16[32,16,128]{2,1,0:T(8,128)(2,1)}, u32[]{:S(2)}) copy-start(bf16[32,16,128]{2,1,0:T(8,128)(2,1)} %copy-done.12) | copy-start | bytes 393220
  190.8 24.0 %copy-start.15 = (bf16[32,16,128]{2,1,0:T(8,128)(2,1)S(1)}, bf16[32,16,128]{2,1,0:T(8,128)(2,1)}, u32[]{:S(2)}) copy-start(bf16[32,16,128]{2,1,0:T(8,128)(2,1)} %copy-done.14) | copy-start | bytes 393220
  190.8 23.8 %all-to-all-start.7 = ((bf16[64,4,16,128]{3,2,1,0:T(8,128)(2,1)}), bf16[64,4,16,128]{3,2,1,0:T(8,128)(2,1)S(1)}, u32[]{:S(2)}, u32[]{:S(2)}) async-start(bf16[64,4,16,128]{3,2,1,0:T(8,128)(2,1)} %broadcast_in_dim.20), calls=%async_computation.7 | async-start | bytes 2097152 | tf_op jit(solution)/shard_map/all_to_all | solution.py:75
  214.6 2.8 %collective-permute-start.9 = (bf16[64,4,16,128]{3,2,1,0:T(8,128)(2,1)S(1)}, bf16[64,4,16,128]{3,2,1,0:T(8,128)(2,1)}, u32[]{:S(2)}, u32[]{:S(2)}) collective-permute-start(bf16[64,4,16,128]{3,2,1,0:T(8,128)(2,1)S(1)} %all-to-all-done.7), channel_id=1, source_target_pairs={{0,1},{1,0},{2,3},{3,2},{4,5},{5,4},{6,7},{7,6},{8,9},{9,8},{10,11... | collective-permute-start | bytes 3145736 | tf_op jit(solution)/shard_map/ppermute | solution.py:76
  (7 other events, 114.0 us)

commit v7 on v6

--- a/solution.py
+++ b/solution.py
@@ -95,11 +95,7 @@
     )
     nlive = jnp.clip(counts - rank * slot_dev, 0, slot_dev).astype(jnp.int32)
     local_links = (links + ncol_all // 2 * lax.axis_index("core")) % ncol_all
-    blocks = [integrals]
-    for k in range(1, col_size):
-        ring = [(i, (i + k) % col_size) for i in range(col_size)]
-        blocks.append(lax.ppermute(integrals, "col", ring))
-    owner_of = (rank - jnp.arange(col_size)) % col_size
+    blocks = lax.all_gather(integrals, "col")
     full_energy = pno_energy.reshape(pair_dev, col_size, 1, row_count, 1)
     denom_full = full_energy + pno_energy[:, None, None, None, :] + shift[:, None, None, None, None]
     for sweep in range(SWEEPS):
@@ -107,7 +103,7 @@
         partial = couple(intersections, colamp, local_links, nlive, col_size)
         if sweep == 0:
             partial, blocks = lax.optimization_barrier((partial, blocks))
-            k_full = jnp.take(jnp.stack(blocks), owner_of, axis=0).astype(jnp.float32)
+            k_full = blocks.astype(jnp.float32)
             weight = k_full / jnp.swapaxes(denom_full[:, :, 0], 0, 1)
         if sweep < SWEEPS - 1:
             parts = lax.all_to_all(partial, "col", 0, 0, tiled=True)

time: 257 us -> 273 us (1.062)
  waiting for transfers between devices: 22.7 us -> 43 us
  between operations: 1.25 us -> 14.4 us
  starting transfers between devices: 21.8 us -> 9.24 us
    all_gather x0 -> x1, waiting for transfers between devices: none -> 17 us  [per_device(): blocks = lax.all_gather(integrals, 'col')]
    ppermute x7 -> x0, starting transfers between devices: 16.5 us -> none  [per_device(): blocks.append(lax.ppermute(integrals, 'col', ring))]
    all_to_all x1, starting transfers between devices: 5.26 us -> 9.19 us  [column_amplitudes(): got = lax.all_to_all(sent, ('ph', 'col'), 0, 0, tiled=True)]
    all_to_all x2, blocking collectives: 50.9 us -> 47.2 us  [column_amplitudes(): got = lax.all_to_all(sent, ('ph', 'col'), 0, 0, tiled=True)]
    ppermute x3, waiting for transfers between devices: 4.52 us -> 7.59 us  [column_amplitudes(): other = lax.ppermute(got, 'core', [(0, 1), (1, 0)])]
  transfers between devices with their start and end apart: 11 -> 5, of which waited for: 3 -> 5; matrix products, arithmetic and copies ran while one was open for 1% -> 0% of each run, Pallas kernels for 5% -> 5%
where the time goes in v7:
time: 273 us
  blocking collectives  154 us (56%)
  waiting for transfers between devices  43 us (16%)
  Pallas kernels  38.8 us (14%)
  between operations  14.4 us (5%)
  starting transfers between devices  9.24 us (3%)
  local copies, waits for them, and re-layouts  6 us (2%)
  other arithmetic  5.9 us (2%)
    all_to_all x2, blocking collectives, column_amplitudes(): got = lax.all_to_all(sent, ('ph', 'col'), 0, 0, tiled=True)  47.2 us
    all_to_all x3, blocking collectives, column_amplitudes(): parts = lax.all_to_all(contrib, ('core', 'ph'), 0, 0, tiled=True)  47 us
    pallas_call x3, Pallas kernels, couple(): pl.pallas_call(functools.partial(couple_kernel, slot_dev), grid_spec=grid...  38.8 us
    all_to_all x2, blocking collectives, per_device(): parts = lax.all_to_all(partial, 'col', 0, 0, tiled=True)  38.7 us
    all_to_all x1, blocking collectives, per_device(): lax.all_to_all(jnp.concatenate([partial, extra], axis=1), 'col', 0, 0, ti...  20.7 us
    all_to_all x1, waiting for transfers between devices, column_amplitudes(): got = lax.all_to_all(sent, ('ph', 'col'), 0, 0, tiled=True)  17.8 us
    all_gather x1, waiting for transfers between devices, per_device(): blocks = lax.all_gather(integrals, 'col')  17 us
    all_to_all x1, starting transfers between devices, column_amplitudes(): got = lax.all_to_all(sent, ('ph', 'col'), 0, 0, tiled=True)  9.19 us
  transfers between devices with their start and end apart: 5, of which 5 were waited for; matrix products, arithmetic and copies ran while one was open for 0% of the time, Pallas kernels for 5%

profile of v7, /device:TPU:0, one launch (start us, length us, event | category | flops | bytes accessed | tf_op | source)
XLA Modules:
  0.0 272.7 jit_solution(4017476712344024877)
XLA Ops:
  7.2 0.8 constant_dynamic-slice_fusion
  8.0 1.1 fusion.1
  9.1 1.1 fusion.12
  10.6 16.8 %all_to_all.48 = f32[16,4,2048]{2,1,0:T(4,128)S(1)} all-to-all(f32[16,4,2048]{2,1,0:T(4,128)S(1)} %copy.17), channel_id=1, replica_groups=mesh['col'=8,'ph'=8,'core'=2] {'core','ph'}, dimensions={0} | all-to-all | bytes 1048576 | tf_op jit(solution)/shard_map/all_to_all | solution.py:70
  27.5 1.3 broadcast_in_dim.8
  28.8 9.2 %all-to-all-start.1 = ((bf16[64,4,16,128]{3,2,1,0:T(8,128)(2,1)}), bf16[64,4,16,128]{3,2,1,0:T(8,128)(2,1)S(1)}, u32[]{:S(2)}, u32[]{:S(2)}) async-start(bf16[64,4,16,128]{3,2,1,0:T(8,128)(2,1)} %broadcast_in_dim.8), calls=%async_computation.1 | async-start | bytes 2097152 | tf_op jit(solution)/shard_map/all_to_all | solution.py:75
  38.0 0.7 all-gather.3.cloned.1.call-update
  38.7 17.8 %all-to-all-done.1 = bf16[64,4,16,128]{3,2,1,0:T(8,128)(2,1)S(1)} async-done(((bf16[64,4,16,128]{3,2,1,0:T(8,128)(2,1)}), bf16[64,4,16,128]{3,2,1,0:T(8,128)(2,1)S(1)}, u32[]{:S(2)}, u32[]{:S(2)}) %all-to-all-start.1) | async-done | bytes 1048608 | tf_op jit(solution)/shard_map/all_to_all | solution.py:75
  56.7 2.5 collective-permute-done
  59.9 12.9 %shard_map.86 = bf16[8,32,16,128]{3,2,1,0:T(8,128)(2,1)S(1)} custom-call(s32[512]{0:T(512)S(1)} %reshape.202.links_ref, s32[32]{0:T(128)S(1)} %subtract_clamp_fusion.nlive_ref, bf16[32,16,128,128]{3,2,1,0:T(8,128)(2,1)} %tiles_ref.5, bf16[64,128,128]{2,1,0:T(8,128)(2,1)S(1)} %bitcast.48), custom_call_target="tpu_custom_call" | custom-call | flops 4294967296 | bytes 19922944 | tf_op jit(solution)/shard_map/pallas_call | solution.py:50
  72.9 17.0 %all-gather.3.cloned.1.call-done = bf16[256,16,128]{2,1,0:T(8,128)(2,1)} async-done(((bf16[32,16,128]{2,1,0:T(8,128)(2,1)}), bf16[256,16,128]{2,1,0:T(8,128)(2,1)}) %all-gather.3.cloned.1.call-update) | async-done | bytes 1048592 | tf_op jit(solution)/shard_map/all_gather | solution.py:98
  89.9 18.8 %all_to_all.49 = bf16[8,32,16,128]{3,2,1,0:T(8,128)(2,1)S(1)} all-to-all(bf16[8,32,16,128]{3,2,1,0:T(8,128)(2,1)S(1)} %shard_map.86), channel_id=1, replica_groups=mesh['col'=8,'ph'=8,'core'=2] {'col'}, dimensions={0} | all-to-all | bytes 2097152 | tf_op jit(solution)/shard_map/all_to_all | solution.py:109
  109.9 16.1 %all_to_all.50 = f32[16,4,2048]{2,1,0:T(4,128)S(1)} all-to-all(f32[16,4,2048]{2,1,0:T(4,128)S(1)} %copy.19), channel_id=1, replica_groups=mesh['col'=8,'ph'=8,'core'=2] {'core','ph'}, dimensions={0} | all-to-all | bytes 1048576 | tf_op jit(solution)/shard_map/all_to_all | solution.py:70
  126.3 23.7 %all_to_all.51 = bf16[64,4,16,128]{3,2,1,0:T(8,128)(2,1)S(1)} all-to-all(bf16[64,4,16,128]{3,2,1,0:T(8,128)(2,1)S(1)} %broadcast_in_dim.9), channel_id=1, replica_groups=mesh['col'=8,'ph'=8,'core'=2] {'ph','col'}, dimensions={0} | all-to-all | bytes 2097152 | tf_op jit(solution)/shard_map/all_to_all | solution.py:75
  150.1 2.7 collective-permute-done.1
  153.5 12.9 %shard_map.87 = bf16[8,32,16,128]{3,2,1,0:T(8,128)(2,1)S(1)} custom-call(s32[512]{0:T(512)S(1)} %reshape.202.links_ref, s32[32]{0:T(128)S(1)} %subtract_clamp_fusion.nlive_ref, bf16[32,16,128,128]{3,2,1,0:T(8,128)(2,1)} %tiles_ref.5, bf16[64,128,128]{2,1,0:T(8,128)(2,1)S(1)} %bitcast.49), custom_call_target="tpu_custom_call" | custom-call | flops 4294967296 | bytes 19922944 | tf_op jit(solution)/shard_map/pallas_call | solution.py:50
  166.4 19.9 %all_to_all.52 = bf16[8,32,16,128]{3,2,1,0:T(8,128)(2,1)S(1)} all-to-all(bf16[8,32,16,128]{3,2,1,0:T(8,128)(2,1)S(1)} %shard_map.87), channel_id=1, replica_groups=mesh['col'=8,'ph'=8,'core'=2] {'col'}, dimensions={0} | all-to-all | bytes 2097152 | tf_op jit(solution)/shard_map/all_to_all | solution.py:109
  187.5 14.0 %all_to_all.53 = f32[16,4,2048]{2,1,0:T(4,128)S(1)} all-to-all(f32[16,4,2048]{2,1,0:T(4,128)S(1)} %copy.21), channel_id=1, replica_groups=mesh['col'=8,'ph'=8,'core'=2] {'core','ph'}, dimensions={0} | all-to-all | bytes 1048576 | tf_op jit(solution)/shard_map/all_to_all | solution.py:70
  201.9 23.5 %all_to_all.54 = bf16[64,4,16,128]{3,2,1,0:T(8,128)(2,1)S(1)} all-to-all(bf16[64,4,16,128]{3,2,1,0:T(8,128)(2,1)S(1)} %broadcast_in_dim.10), channel_id=1, replica_groups=mesh['col'=8,'ph'=8,'core'=2] {'ph','col'}, dimensions={0} | all-to-all | bytes 2097152 | tf_op jit(solution)/shard_map/all_to_all | solution.py:75
  225.5 2.5 collective-permute-done.2
  228.8 12.9 %shard_map.88 = bf16[8,32,16,128]{3,2,1,0:T(8,128)(2,1)S(1)} custom-call(s32[512]{0:T(512)S(1)} %reshape.202.links_ref, s32[32]{0:T(128)S(1)} %subtract_clamp_fusion.nlive_ref, bf16[32,16,128,128]{3,2,1,0:T(8,128)(2,1)} %tiles_ref.5, bf16[64,128,128]{2,1,0:T(8,128)(2,1)S(1)} %bitcast.47), custom_call_target="tpu_custom_call" | custom-call | flops 4294967296 | bytes 19922944 | tf_op jit(solution)/shard_map/pallas_call | solution.py:50
  241.7 1.5 fusion
  243.5 20.7 %all_to_all.55 = bf16[8,33,16,128]{3,2,1,0:T(8,128)(2,1)S(1)} all-to-all(bf16[8,33,16,128]{3,2,1,0:T(8,128)(2,1)S(1)} %pad_maximum_fusion), channel_id=1, replica_groups=mesh['col'=8,'ph'=8,'core'=2] {'col'}, dimensions={0} | all-to-all | bytes 2162688 | tf_op jit(solution)/shard_map/all_to_all | solution.py:118
  264.5 0.9 fusion.7
  (61 shorter events, 7.3 us)
Async XLA Ops:
  27.4 29.1 %copy-start.4 = (s32[32,16]{0,1:T(8,128)S(1)}, s32[32,16]{0,1:T(8,128)}, u32[]{:S(2)}) copy-start(s32[32,16]{0,1:T(8,128)} %param.15) | copy-start | bytes 6148
  27.4 29.3 %copy-start.6 = (s32[32]{0:T(128)S(1)}, s32[32]{0:T(128)}, u32[]{:S(2)}) copy-start(s32[32]{0:T(128)} %param.16) | copy-start | bytes 388
  28.8 27.7 %all-to-all-start.1 = ((bf16[64,4,16,128]{3,2,1,0:T(8,128)(2,1)}), bf16[64,4,16,128]{3,2,1,0:T(8,128)(2,1)S(1)}, u32[]{:S(2)}, u32[]{:S(2)}) async-start(bf16[64,4,16,128]{3,2,1,0:T(8,128)(2,1)} %broadcast_in_dim.8), calls=%async_computation.1 | async-start | bytes 2097152 | tf_op jit(solution)/shard_map/all_to_all | solution.py:75
  38.0 51.9 %all-gather.3.cloned.1.call-start = ((), (), s32[]{:S(2)}) async-start(), calls=%async_computation.9 | async-start | bytes 1179648 | tf_op jit(solution)/shard_map/all_gather | solution.py:98
  56.5 2.7 collective-permute-start
  72.9 36.0 %copy-start = (bf16[32,16,128]{2,1,0:T(8,128)(2,1)S(1)}, bf16[32,16,128]{2,1,0:T(8,128)(2,1)}, u32[]{:S(2)}) copy-start(bf16[32,16,128]{2,1,0:T(8,128)(2,1)} %param.11) | copy-start | bytes 393220
  72.9 36.0 %copy-start.2 = (f32[32,128]{1,0:T(8,128)S(1)}, f32[32,128]{1,0:T(8,128)}, u32[]{:S(2)}) copy-start(f32[32,128]{1,0:T(8,128)} %param.12) | copy-start | bytes 49156
  72.9 36.0 %copy-start.3 = (f32[32]{0:T(128)S(1)}, f32[32]{0:T(128)}, u32[]{:S(2)}) copy-start(f32[32]{0:T(128)} %param.13) | copy-start | bytes 388
  89.9 19.2 %copy-start.5 = (s32[32]{0:T(128)S(1)}, s32[32]{0:T(128)}, u32[]{:S(2)}) copy-start(s32[32]{0:T(128)} %param.17) | copy-start | bytes 388
  150.1 2.7 collective-permute-start.1
  225.3 2.7 collective-permute-start.2
  228.8 12.9 %copy-start.1 = (bf16[256,16,128]{2,1,0:T(8,128)(2,1)S(1)}, bf16[256,16,128]{2,1,0:T(8,128)(2,1)}, u32[]{:S(2)}) copy-start(bf16[256,16,128]{2,1,0:T(8,128)(2,1)} %all-gather.3.cloned.1.call-done) | copy-start | bytes 3145732
Sparse Core Ops, SparseCore 0:
  41.1 48.6 all-gather.2

commit v8 on v7

--- a/solution.py
+++ b/solution.py
@@ -95,17 +95,18 @@
     )
     nlive = jnp.clip(counts - rank * slot_dev, 0, slot_dev).astype(jnp.int32)
     local_links = (links + ncol_all // 2 * lax.axis_index("core")) % ncol_all
-    blocks = lax.all_gather(integrals, "col")
     full_energy = pno_energy.reshape(pair_dev, col_size, 1, row_count, 1)
     denom_full = full_energy + pno_energy[:, None, None, None, :] + shift[:, None, None, None, None]
     for sweep in range(SWEEPS):
         colamp = column_amplitudes(amplitudes, one_hot, pair_size, col_size)
         partial = couple(intersections, colamp, local_links, nlive, col_size)
         if sweep == 0:
-            partial, blocks = lax.optimization_barrier((partial, blocks))
-            k_full = blocks.astype(jnp.float32)
+            sent = jnp.concatenate([partial, jnp.broadcast_to(integrals, partial.shape)], axis=1)
+            parts = lax.all_to_all(sent, "col", 0, 0, tiled=True)
+            coupled = jnp.sum(parts[:, :pair_dev].astype(jnp.float32), axis=0)
+            k_full = parts[:, pair_dev:].astype(jnp.float32)
             weight = k_full / jnp.swapaxes(denom_full[:, :, 0], 0, 1)
-        if sweep < SWEEPS - 1:
+        elif sweep < SWEEPS - 1:
             parts = lax.all_to_all(partial, "col", 0, 0, tiled=True)
             coupled = jnp.sum(parts.astype(jnp.float32), axis=0)
         else:

time: 273 us -> 254 us (0.930)
  blocking collectives: 154 us -> 191 us
  waiting for transfers between devices: 43 us -> 7.72 us
  between operations: 14.4 us -> 0.95 us
  starting transfers between devices: 9.24 us -> 0.01 us
    all_to_all x0 -> x1, blocking collectives: none -> 31.1 us  [per_device(): parts = lax.all_to_all(sent, 'col', 0, 0, tiled=True)]
    all_to_all x2 -> x3, blocking collectives: 47.2 us -> 74.5 us  [column_amplitudes(): got = lax.all_to_all(sent, ('ph', 'col'), 0, 0, tiled=True)]
    all_to_all x2 -> x1, blocking collectives: 38.7 us -> 19.9 us  [per_device(): parts = lax.all_to_all(partial, 'col', 0, 0, tiled=True)]
    all_to_all x1 -> x0, waiting for transfers between devices: 17.8 us -> none  [column_amplitudes(): got = lax.all_to_all(sent, ('ph', 'col'), 0, 0, tiled=True)]
    all_gather x1 -> x0, waiting for transfers between devices: 17 us -> none  [per_device(): blocks = lax.all_gather(integrals, 'col')]
    all_to_all x1 -> x0, starting transfers between devices: 9.19 us -> none  [column_amplitudes(): got = lax.all_to_all(sent, ('ph', 'col'), 0, 0, tiled=True)]
  transfers between devices with their start and end apart: 5 -> 3, of which waited for: 5 -> 3; matrix products, arithmetic and copies ran while one was open for 0% -> 0% of each run, Pallas kernels for 5% -> 0%
where the time goes in v8:
time: 254 us; the launch traced here: 253 us
  blocking collectives  191 us (75%)
  Pallas kernels  38.8 us (15%)
  waiting for transfers between devices  7.72 us (3%)
  other arithmetic  7.32 us (3%)
  local copies, waits for them, and re-layouts  5.33 us (2%)
    all_to_all x3, blocking collectives, column_amplitudes(): got = lax.all_to_all(sent, ('ph', 'col'), 0, 0, tiled=True)  74.5 us
    all_to_all x3, blocking collectives, column_amplitudes(): parts = lax.all_to_all(contrib, ('core', 'ph'), 0, 0, tiled=True)  44.9 us
    pallas_call x3, Pallas kernels, couple(): pl.pallas_call(functools.partial(couple_kernel, slot_dev), grid_spec=grid...  38.8 us
    all_to_all x1, blocking collectives, per_device(): parts = lax.all_to_all(sent, 'col', 0, 0, tiled=True)  31.1 us
    all_to_all x1, blocking collectives, per_device(): lax.all_to_all(jnp.concatenate([partial, extra], axis=1), 'col', 0, 0, ti...  20.7 us
    all_to_all x1, blocking collectives, per_device(): parts = lax.all_to_all(partial, 'col', 0, 0, tiled=True)  19.9 us
    ppermute x3, waiting for transfers between devices, column_amplitudes(): other = lax.ppermute(got, 'core', [(0, 1), (1, 0)])  7.72 us
  transfers between devices with their start and end apart: 3, of which 3 were waited for; matrix products, arithmetic and copies ran while one was open for 0% of the time, Pallas kernels for 0%

profile of v8, /device:TPU:0, one launch (start us, length us, event | category | flops | bytes accessed | tf_op | source)
XLA Modules:
  0.0 253.0 jit_solution(5540684948486814408)
XLA Ops:
  0.6 0.8 constant_dynamic-slice_fusion
  1.4 1.1 fusion.1
  2.6 1.1 fusion.12
  4.0 16.8 %all_to_all.48 = f32[16,4,2048]{2,1,0:T(4,128)S(1)} all-to-all(f32[16,4,2048]{2,1,0:T(4,128)S(1)} %copy.17), channel_id=1, replica_groups=mesh['col'=8,'ph'=8,'core'=2] {'core','ph'}, dimensions={0} | all-to-all | bytes 1048576 | tf_op jit(solution)/shard_map/all_to_all | solution.py:70
  21.2 27.5 %all_to_all.49 = bf16[64,4,16,128]{3,2,1,0:T(8,128)(2,1)S(1)} all-to-all(bf16[64,4,16,128]{3,2,1,0:T(8,128)(2,1)S(1)} %broadcast_in_dim.10), channel_id=1, replica_groups=mesh['col'=8,'ph'=8,'core'=2] {'ph','col'}, dimensions={0} | all-to-all | bytes 2097152 | tf_op jit(solution)/shard_map/all_to_all | solution.py:75
  48.9 2.5 collective-permute-done
  51.6 0.6 copy.18
  52.2 12.9 %shard_map.86 = bf16[8,32,16,128]{3,2,1,0:T(8,128)(2,1)S(1)} custom-call(s32[512]{0:T(512)S(1)} %reshape.202.links_ref, s32[32]{0:T(128)S(1)} %subtract_clamp_fusion.nlive_ref, bf16[32,16,128,128]{3,2,1,0:T(8,128)(2,1)} %tiles_ref.5, bf16[64,128,128]{2,1,0:T(8,128)(2,1)S(1)} %bitcast.47), custom_call_target="tpu_custom_call" | custom-call | flops 4294967296 | bytes 19922944 | tf_op jit(solution)/shard_map/pallas_call | solution.py:50
  65.5 31.1 %all_to_all.50 = bf16[8,64,16,128]{3,2,1,0:T(8,128)(2,1)S(1)} all-to-all(bf16[8,64,16,128]{3,2,1,0:T(8,128)(2,1)S(1)} %pad_maximum_fusion), channel_id=1, replica_groups=mesh['col'=8,'ph'=8,'core'=2] {'col'}, dimensions={0} | all-to-all | bytes 4194304 | tf_op jit(solution)/shard_map/all_to_all | solution.py:105
  98.0 14.0 %all_to_all.51 = f32[16,4,2048]{2,1,0:T(4,128)S(1)} all-to-all(f32[16,4,2048]{2,1,0:T(4,128)S(1)} %copy.19), channel_id=1, replica_groups=mesh['col'=8,'ph'=8,'core'=2] {'core','ph'}, dimensions={0} | all-to-all | bytes 1048576 | tf_op jit(solution)/shard_map/all_to_all | solution.py:70
  112.4 23.5 %all_to_all.52 = bf16[64,4,16,128]{3,2,1,0:T(8,128)(2,1)S(1)} all-to-all(bf16[64,4,16,128]{3,2,1,0:T(8,128)(2,1)S(1)} %broadcast_in_dim.12), channel_id=1, replica_groups=mesh['col'=8,'ph'=8,'core'=2] {'ph','col'}, dimensions={0} | all-to-all | bytes 2097152 | tf_op jit(solution)/shard_map/all_to_all | solution.py:75
  135.9 2.7 %collective-permute-done.1 = bf16[64,4,16,128]{3,2,1,0:T(8,128)(2,1)S(1)} collective-permute-done((bf16[64,4,16,128]{3,2,1,0:T(8,128)(2,1)S(1)}, bf16[64,4,16,128]{3,2,1,0:T(8,128)(2,1)S(1)}, u32[]{:S(2)}, u32[]{:S(2)}) %collective-permute-start.1) | collective-permute-done | bytes 1048608 | tf_op jit(solution)/shard_map/ppermute | solution.py:76
  138.7 0.6 copy.20
  139.3 12.9 %shard_map.87 = bf16[8,32,16,128]{3,2,1,0:T(8,128)(2,1)S(1)} custom-call(s32[512]{0:T(512)S(1)} %reshape.202.links_ref, s32[32]{0:T(128)S(1)} %subtract_clamp_fusion.nlive_ref, bf16[32,16,128,128]{3,2,1,0:T(8,128)(2,1)} %tiles_ref.5, bf16[64,128,128]{2,1,0:T(8,128)(2,1)S(1)} %bitcast.48), custom_call_target="tpu_custom_call" | custom-call | flops 4294967296 | bytes 19922944 | tf_op jit(solution)/shard_map/pallas_call | solution.py:50
  152.2 19.9 %all_to_all.53 = bf16[8,32,16,128]{3,2,1,0:T(8,128)(2,1)S(1)} all-to-all(bf16[8,32,16,128]{3,2,1,0:T(8,128)(2,1)S(1)} %shard_map.87), channel_id=1, replica_groups=mesh['col'=8,'ph'=8,'core'=2] {'col'}, dimensions={0} | all-to-all | bytes 2097152 | tf_op jit(solution)/shard_map/all_to_all | solution.py:110
  173.2 14.0 %all_to_all.54 = f32[16,4,2048]{2,1,0:T(4,128)S(1)} all-to-all(f32[16,4,2048]{2,1,0:T(4,128)S(1)} %copy.21), channel_id=1, replica_groups=mesh['col'=8,'ph'=8,'core'=2] {'core','ph'}, dimensions={0} | all-to-all | bytes 1048576 | tf_op jit(solution)/shard_map/all_to_all | solution.py:70
  187.6 23.5 %all_to_all.55 = bf16[64,4,16,128]{3,2,1,0:T(8,128)(2,1)S(1)} all-to-all(bf16[64,4,16,128]{3,2,1,0:T(8,128)(2,1)S(1)} %broadcast_in_dim.13), channel_id=1, replica_groups=mesh['col'=8,'ph'=8,'core'=2] {'ph','col'}, dimensions={0} | all-to-all | bytes 2097152 | tf_op jit(solution)/shard_map/all_to_all | solution.py:75
  211.3 2.6 %collective-permute-done.2 = bf16[64,4,16,128]{3,2,1,0:T(8,128)(2,1)} collective-permute-done((bf16[64,4,16,128]{3,2,1,0:T(8,128)(2,1)S(1)}, bf16[64,4,16,128]{3,2,1,0:T(8,128)(2,1)}, u32[]{:S(2)}, u32[]{:S(2)}) %collective-permute-start.2) | collective-permute-done | bytes 1048608 | tf_op jit(solution)/shard_map/ppermute | solution.py:76
  213.9 1.4 maximum_bitcast_fusion.2
  215.3 0.6 copy.22
  215.9 12.9 %shard_map.88 = bf16[8,32,16,128]{3,2,1,0:T(8,128)(2,1)S(1)} custom-call(s32[512]{0:T(512)S(1)} %reshape.202.links_ref, s32[32]{0:T(128)S(1)} %subtract_clamp_fusion.nlive_ref, bf16[32,16,128,128]{3,2,1,0:T(8,128)(2,1)} %tiles_ref.5, bf16[64,128,128]{2,1,0:T(8,128)(2,1)S(1)} %bitcast.46), custom_call_target="tpu_custom_call" | custom-call | flops 4294967296 | bytes 19922944 | tf_op jit(solution)/shard_map/pallas_call | solution.py:50
  228.8 1.5 fusion
  230.6 20.7 %all_to_all.56 = bf16[8,33,16,128]{3,2,1,0:T(8,128)(2,1)S(1)} all-to-all(bf16[8,33,16,128]{3,2,1,0:T(8,128)(2,1)S(1)} %pad_maximum_fusion.1), channel_id=1, replica_groups=mesh['col'=8,'ph'=8,'core'=2] {'col'}, dimensions={0} | all-to-all | bytes 2162688 | tf_op jit(solution)/shard_map/all_to_all | solution.py:119
  251.6 0.9 fusion.7
  (57 shorter events, 6.1 us)
Async XLA Ops:
  20.8 27.9 %copy-start.3 = (s32[32,16]{0,1:T(8,128)S(1)}, s32[32,16]{0,1:T(8,128)}, u32[]{:S(2)}) copy-start(s32[32,16]{0,1:T(8,128)} %param.15) | copy-start | bytes 6148
  20.8 28.1 %copy-start.5 = (s32[32]{0:T(128)S(1)}, s32[32]{0:T(128)}, u32[]{:S(2)}) copy-start(s32[32]{0:T(128)} %param.16) | copy-start | bytes 388
  48.7 2.7 %collective-permute-start = (bf16[64,4,16,128]{3,2,1,0:T(8,128)(2,1)S(1)}, bf16[64,4,16,128]{3,2,1,0:T(8,128)(2,1)S(1)}, u32[]{:S(2)}, u32[]{:S(2)}) collective-permute-start(bf16[64,4,16,128]{3,2,1,0:T(8,128)(2,1)S(1)} %all_to_all.49), channel_id=1, source_target_pairs={{0,1},{1,0},{2,3},{3,2},{4,5},{5,4},{6,7},{7,6},{8,9},{9,8},{10,11... | collective-permute-start | bytes 3145736 | tf_op jit(solution)/shard_map/ppermute | solution.py:76
  52.1 12.9 %copy-start = (bf16[32,16,128]{2,1,0:T(8,128)(2,1)S(1)}, bf16[32,16,128]{2,1,0:T(8,128)(2,1)}, u32[]{:S(2)}) copy-start(bf16[32,16,128]{2,1,0:T(8,128)(2,1)} %param.11) | copy-start | bytes 393220
  65.4 31.3 %copy-start.1 = (f32[32,128]{1,0:T(8,128)S(1)}, f32[32,128]{1,0:T(8,128)}, u32[]{:S(2)}) copy-start(f32[32,128]{1,0:T(8,128)} %param.12) | copy-start | bytes 49156
  65.4 31.3 %copy-start.2 = (f32[32]{0:T(128)S(1)}, f32[32]{0:T(128)}, u32[]{:S(2)}) copy-start(f32[32]{0:T(128)} %param.13) | copy-start | bytes 388
  96.6 0.7 copy-start.4
  135.8 2.7 %collective-permute-start.1 = (bf16[64,4,16,128]{3,2,1,0:T(8,128)(2,1)S(1)}, bf16[64,4,16,128]{3,2,1,0:T(8,128)(2,1)S(1)}, u32[]{:S(2)}, u32[]{:S(2)}) collective-permute-start(bf16[64,4,16,128]{3,2,1,0:T(8,128)(2,1)S(1)} %all_to_all.52), channel_id=1, source_target_pairs={{0,1},{1,0},{2,3},{3,2},{4,5},{5,4},{6,7},{7,6},{8,9},{9,8},{10,11... | collective-permute-start | bytes 3145736 | tf_op jit(solution)/shard_map/ppermute | solution.py:76
  211.1 2.8 %collective-permute-start.2 = (bf16[64,4,16,128]{3,2,1,0:T(8,128)(2,1)S(1)}, bf16[64,4,16,128]{3,2,1,0:T(8,128)(2,1)}, u32[]{:S(2)}, u32[]{:S(2)}) collective-permute-start(bf16[64,4,16,128]{3,2,1,0:T(8,128)(2,1)S(1)} %all_to_all.55), channel_id=1, source_target_pairs={{0,1},{1,0},{2,3},{3,2},{4,5},{5,4},{6,7},{7,6},{8,9},{9,8},{10,11... | collective-permute-start | bytes 3145736 | tf_op jit(solution)/shard_map/ppermute | solution.py:76

commit v9 on v6

--- a/solution.py
+++ b/solution.py
@@ -50,11 +50,11 @@
     return pl.pallas_call(
         functools.partial(couple_kernel, slot_dev),
         grid_spec=grid_spec,
-        out_shape=jax.ShapeDtypeStruct((col_size, pair_dev, rows, width), jnp.bfloat16),
+        out_shape=jax.ShapeDtypeStruct((col_size, pair_dev, rows, width), jnp.float32),
         compiler_params=pltpu.CompilerParams(vmem_limit_bytes=48 * 1024 * 1024),
         cost_estimate=pl.CostEstimate(
             flops=flops,
-            bytes_accessed=tiles.size * 2 + colamp.size * 2 + pair_dev * width * width * 2,
+            bytes_accessed=tiles.size * 2 + colamp.size * 2 + pair_dev * width * width * 4,
             transcendentals=0,
         ),
     )(links.reshape(-1), nlive, tiles, colamp)
@@ -111,18 +111,15 @@
             weight = k_full / jnp.swapaxes(denom_full[:, :, 0], 0, 1)
         if sweep < SWEEPS - 1:
             parts = lax.all_to_all(partial, "col", 0, 0, tiled=True)
-            coupled = jnp.sum(parts.astype(jnp.float32), axis=0)
+            coupled = jnp.sum(parts, axis=0)
         else:
-            share = -jnp.sum(weight * partial.astype(jnp.float32), axis=(0, 2, 3))
-            high = share.astype(jnp.bfloat16)
-            low = (share - high.astype(jnp.float32)).astype(jnp.bfloat16)
-            extra = jnp.zeros((row_count, partial.shape[-1]), jnp.bfloat16)
-            extra = extra.at[0, :pair_dev].set(high).at[1, :pair_dev].set(low)
+            share = -jnp.sum(weight * partial, axis=(0, 2, 3))
+            extra = jnp.zeros((row_count, partial.shape[-1]), jnp.float32)
+            extra = extra.at[0, :pair_dev].set(share)
             extra = jnp.broadcast_to(extra, (col_size, 1) + extra.shape)
             parts = lax.all_to_all(jnp.concatenate([partial, extra], axis=1), "col", 0, 0, tiled=True)
-            parts = parts.astype(jnp.float32)
             coupled = jnp.sum(parts[:, :pair_dev], axis=0)
-            shares = parts[:, pair_dev, 0, :pair_dev] + parts[:, pair_dev, 1, :pair_dev]
+            shares = parts[:, pair_dev, 0, :pair_dev]
         amplitudes = -(kfloat + coupled) / denom
     base = -jnp.sum(weight * k_full, axis=(0, 2, 3))
     pair_energy = base + jnp.sum(shares, axis=0)

time: 257 us -> 292 us (1.14)
  blocking collectives: 156 us -> 190 us
    all_to_all x2, blocking collectives: 39.8 us -> 62.3 us  [per_device(): parts = lax.all_to_all(partial, 'col', 0, 0, tiled=True)]
    all_to_all x1, blocking collectives: 20.7 us -> 32.2 us  [per_device(): lax.all_to_all(jnp.concatenate([partial, extra], axis=1), 'col', 0, 0, ti...]
  transfers between devices with their start and end apart: 11 -> 11, of which waited for: 3 -> 3; matrix products, arithmetic and copies ran while one was open for 1% -> 1% of each run, Pallas kernels for 5% -> 4%
where the time goes in v9:
time: 292 us; the launch traced here: 291 us
  blocking collectives  190 us (65%)
  Pallas kernels  38.8 us (13%)
  waiting for transfers between devices  22.7 us (8%)
  starting transfers between devices  21.8 us (7%)
  local copies, waits for them, and re-layouts  7.87 us (3%)
  other arithmetic  6.97 us (2%)
    all_to_all x2, blocking collectives, per_device(): parts = lax.all_to_all(partial, 'col', 0, 0, tiled=True)  62.3 us
    all_to_all x2, blocking collectives, column_amplitudes(): got = lax.all_to_all(sent, ('ph', 'col'), 0, 0, tiled=True)  50.9 us
    all_to_all x3, blocking collectives, column_amplitudes(): parts = lax.all_to_all(contrib, ('core', 'ph'), 0, 0, tiled=True)  44.6 us
    pallas_call x3, Pallas kernels, couple(): pl.pallas_call(functools.partial(couple_kernel, slot_dev), grid_spec=grid...  38.8 us
    all_to_all x1, blocking collectives, per_device(): lax.all_to_all(jnp.concatenate([partial, extra], axis=1), 'col', 0, 0, ti...  32.2 us
    all_to_all x1, waiting for transfers between devices, column_amplitudes(): got = lax.all_to_all(sent, ('ph', 'col'), 0, 0, tiled=True)  18.2 us
    ppermute x7, starting transfers between devices, per_device(): blocks.append(lax.ppermute(integrals, 'col', ring))  16.5 us
  transfers between devices with their start and end apart: 11, of which 3 were waited for; matrix products, arithmetic and copies ran while one was open for 1% of the time, Pallas kernels for 4%

profile of v9, /device:TPU:0, one launch (start us, length us, event | category | flops | bytes accessed | tf_op | source)
XLA Modules:
  0.0 291.2 jit_solution(17940439675345421374)
XLA Ops:
  1.4 1.1 fusion.1
  4.0 16.8 %all_to_all.48 = f32[16,4,2048]{2,1,0:T(4,128)S(1)} all-to-all(f32[16,4,2048]{2,1,0:T(4,128)S(1)} %copy.17), channel_id=1, replica_groups=mesh['col'=8,'ph'=8,'core'=2] {'core','ph'}, dimensions={0} | all-to-all | bytes 1048576 | tf_op jit(solution)/shard_map/all_to_all | solution.py:70
  21.2 27.5 %all_to_all.49 = bf16[64,4,16,128]{3,2,1,0:T(8,128)(2,1)S(1)} all-to-all(bf16[64,4,16,128]{3,2,1,0:T(8,128)(2,1)S(1)} %broadcast_in_dim.18), channel_id=1, replica_groups=mesh['col'=8,'ph'=8,'core'=2] {'ph','col'}, dimensions={0} | all-to-all | bytes 2097152 | tf_op jit(solution)/shard_map/all_to_all | solution.py:75
  49.9 3.5 %collective-permute-start.3 = (bf16[32,16,128]{2,1,0:T(8,128)(2,1)S(1)}, bf16[32,16,128]{2,1,0:T(8,128)(2,1)S(1)}, u32[]{:S(2)}, u32[]{:S(2)}) collective-permute-start(bf16[32,16,128]{2,1,0:T(8,128)(2,1)S(1)} %copy-done), channel_id=1, source_target_pairs={{0,48},{16,64},{32,80},{48,96},{64,112},{80,0},{96,16},{112,32},{1... | collective-permute-start | bytes 393224 | tf_op jit(solution)/shard_map/ppermute | solution.py:101
  53.4 3.0 %collective-permute-start.4 = (bf16[32,16,128]{2,1,0:T(8,128)(2,1)S(1)}, bf16[32,16,128]{2,1,0:T(8,128)(2,1)S(1)}, u32[]{:S(2)}, u32[]{:S(2)}) collective-permute-start(bf16[32,16,128]{2,1,0:T(8,128)(2,1)S(1)} %copy-done), channel_id=1, source_target_pairs={{0,64},{16,80},{32,96},{48,112},{64,0},{80,16},{96,32},{112,48},{1... | collective-permute-start | bytes 393224 | tf_op jit(solution)/shard_map/ppermute | solution.py:101
  56.6 1.3 collective-permute-start.5
  58.7 1.7 collective-permute-start.6
  60.4 5.9 %collective-permute-start.7 = (bf16[32,16,128]{2,1,0:T(8,128)(2,1)S(1)}, bf16[32,16,128]{2,1,0:T(8,128)(2,1)S(1)}, u32[]{:S(2)}, u32[]{:S(2)}) collective-permute-start(bf16[32,16,128]{2,1,0:T(8,128)(2,1)S(1)} %copy-done), channel_id=1, source_target_pairs={{0,112},{16,0},{32,16},{48,32},{64,48},{80,64},{96,80},{112,96},{1... | collective-permute-start | bytes 393224 | tf_op jit(solution)/shard_map/ppermute | solution.py:101
  66.3 12.9 %shard_map.86 = f32[8,32,16,128]{3,2,1,0:T(8,128)S(1)} custom-call(s32[512]{0:T(512)S(1)} %reshape.217.links_ref, s32[32]{0:T(128)S(1)} %subtract_clamp_fusion.nlive_ref, bf16[32,16,128,128]{3,2,1,0:T(8,128)(2,1)} %tiles_ref.5, bf16[64,128,128]{2,1,0:T(8,128)(2,1)S(1)} %bitcast.59), custom_call_target="tpu_custom_call" | custom-call | flops 4294967296 | bytes 20971520 | tf_op jit(solution)/shard_map/pallas_call | solution.py:50
  79.9 31.2 %all_to_all.50 = f32[8,32,16,128]{3,2,1,0:T(8,128)S(1)} all-to-all(f32[8,32,16,128]{3,2,1,0:T(8,128)S(1)} %shard_map.86), channel_id=1, replica_groups=mesh['col'=8,'ph'=8,'core'=2] {'col'}, dimensions={0} | all-to-all | bytes 4194304 | tf_op jit(solution)/shard_map/all_to_all | solution.py:113
  112.9 13.7 %all_to_all.51 = f32[16,4,2048]{2,1,0:T(4,128)S(1)} all-to-all(f32[16,4,2048]{2,1,0:T(4,128)S(1)} %copy.19), channel_id=1, replica_groups=mesh['col'=8,'ph'=8,'core'=2] {'core','ph'}, dimensions={0} | all-to-all | bytes 1048576 | tf_op jit(solution)/shard_map/all_to_all | solution.py:70
  127.0 23.4 %all_to_all.52 = bf16[64,4,16,128]{3,2,1,0:T(8,128)(2,1)S(1)} all-to-all(bf16[64,4,16,128]{3,2,1,0:T(8,128)(2,1)S(1)} %broadcast_in_dim.19), channel_id=1, replica_groups=mesh['col'=8,'ph'=8,'core'=2] {'ph','col'}, dimensions={0} | all-to-all | bytes 2097152 | tf_op jit(solution)/shard_map/all_to_all | solution.py:75
  150.4 2.7 collective-permute-done.8
  153.8 12.9 %shard_map.87 = f32[8,32,16,128]{3,2,1,0:T(8,128)S(1)} custom-call(s32[512]{0:T(512)S(1)} %reshape.217.links_ref, s32[32]{0:T(128)S(1)} %subtract_clamp_fusion.nlive_ref, bf16[32,16,128,128]{3,2,1,0:T(8,128)(2,1)} %tiles_ref.5, bf16[64,128,128]{2,1,0:T(8,128)(2,1)S(1)} %bitcast.61), custom_call_target="tpu_custom_call" | custom-call | flops 4294967296 | bytes 20971520 | tf_op jit(solution)/shard_map/pallas_call | solution.py:50
  166.7 31.1 %all_to_all.53 = f32[8,32,16,128]{3,2,1,0:T(8,128)S(1)} all-to-all(f32[8,32,16,128]{3,2,1,0:T(8,128)S(1)} %shard_map.87), channel_id=1, replica_groups=mesh['col'=8,'ph'=8,'core'=2] {'col'}, dimensions={0} | all-to-all | bytes 4194304 | tf_op jit(solution)/shard_map/all_to_all | solution.py:113
  199.0 14.0 %all_to_all.54 = f32[16,4,2048]{2,1,0:T(4,128)S(1)} all-to-all(f32[16,4,2048]{2,1,0:T(4,128)S(1)} %copy.21), channel_id=1, replica_groups=mesh['col'=8,'ph'=8,'core'=2] {'core','ph'}, dimensions={0} | all-to-all | bytes 1048576 | tf_op jit(solution)/shard_map/all_to_all | solution.py:70
  213.2 1.2 broadcast_in_dim.20
  214.4 5.3 %all-to-all-start.7 = ((bf16[64,4,16,128]{3,2,1,0:T(8,128)(2,1)}), bf16[64,4,16,128]{3,2,1,0:T(8,128)(2,1)S(1)}, u32[]{:S(2)}, u32[]{:S(2)}) async-start(bf16[64,4,16,128]{3,2,1,0:T(8,128)(2,1)} %broadcast_in_dim.20), calls=%async_computation.7 | async-start | bytes 2097152 | tf_op jit(solution)/shard_map/all_to_all | solution.py:75
  220.0 18.2 %all-to-all-done.7 = bf16[64,4,16,128]{3,2,1,0:T(8,128)(2,1)S(1)} async-done(((bf16[64,4,16,128]{3,2,1,0:T(8,128)(2,1)}), bf16[64,4,16,128]{3,2,1,0:T(8,128)(2,1)S(1)}, u32[]{:S(2)}, u32[]{:S(2)}) %all-to-all-start.7) | async-done | bytes 1048608 | tf_op jit(solution)/shard_map/all_to_all | solution.py:75
  239.2 1.9 collective-permute-done.9
  241.0 1.4 maximum_bitcast_fusion.2
  243.0 12.9 %shard_map.88 = f32[8,32,16,128]{3,2,1,0:T(8,128)S(1)} custom-call(s32[512]{0:T(512)S(1)} %reshape.217.links_ref, s32[32]{0:T(128)S(1)} %subtract_clamp_fusion.nlive_ref, bf16[32,16,128,128]{3,2,1,0:T(8,128)(2,1)} %tiles_ref.5, bf16[64,128,128]{2,1,0:T(8,128)(2,1)S(1)} %bitcast.60), custom_call_target="tpu_custom_call" | custom-call | flops 4294967296 | bytes 20971520 | tf_op jit(solution)/shard_map/pallas_call | solution.py:50
  256.0 1.4 fusion
  257.5 32.2 %all_to_all.55 = f32[8,33,16,128]{3,2,1,0:T(8,128)S(1)} all-to-all(f32[8,33,16,128]{3,2,1,0:T(8,128)S(1)} %pad_maximum_fusion), channel_id=1, replica_groups=mesh['col'=8,'ph'=8,'core'=2] {'col'}, dimensions={0} | all-to-all | bytes 4325376 | tf_op jit(solution)/shard_map/all_to_all | solution.py:120
  (107 shorter events, 12.8 us)
Async XLA Ops:
  20.8 27.9 %copy-start = (bf16[32,16,128]{2,1,0:T(8,128)(2,1)S(1)}, bf16[32,16,128]{2,1,0:T(8,128)(2,1)}, u32[]{:S(2)}) copy-start(bf16[32,16,128]{2,1,0:T(8,128)(2,1)} %param.9) | copy-start | bytes 393220
  20.8 35.6 %copy-start.17 = (s32[32,16]{0,1:T(8,128)S(1)}, s32[32,16]{0,1:T(8,128)}, u32[]{:S(2)}) copy-start(s32[32,16]{0,1:T(8,128)} %param.13) | copy-start | bytes 6148
  20.8 35.8 %copy-start.19 = (s32[32]{0:T(128)S(1)}, s32[32]{0:T(128)}, u32[]{:S(2)}) copy-start(s32[32]{0:T(128)} %param.14) | copy-start | bytes 388
  48.7 7.9 %collective-permute-start = (bf16[64,4,16,128]{3,2,1,0:T(8,128)(2,1)S(1)}, bf16[64,4,16,128]{3,2,1,0:T(8,128)(2,1)S(1)}, u32[]{:S(2)}, u32[]{:S(2)}) collective-permute-start(bf16[64,4,16,128]{3,2,1,0:T(8,128)(2,1)S(1)} %all_to_all.49), channel_id=1, source_target_pairs={{0,1},{1,0},{2,3},{3,2},{4,5},{5,4},{6,7},{7,6},{8,9},{9,8},{10,11... | collective-permute-start | bytes 3145736 | tf_op jit(solution)/shard_map/ppermute | solution.py:76
  48.7 9.9 %collective-permute-start.1 = (bf16[32,16,128]{2,1,0:T(8,128)(2,1)S(1)}, bf16[32,16,128]{2,1,0:T(8,128)(2,1)S(1)}, u32[]{:S(2)}, u32[]{:S(2)}) collective-permute-start(bf16[32,16,128]{2,1,0:T(8,128)(2,1)S(1)} %copy-done), channel_id=1, source_target_pairs={{0,16},{16,32},{32,48},{48,64},{64,80},{80,96},{96,112},{112,0},{1... | collective-permute-start | bytes 393224 | tf_op jit(solution)/shard_map/ppermute | solution.py:101
  49.4 11.0 %collective-permute-start.2 = (bf16[32,16,128]{2,1,0:T(8,128)(2,1)S(1)}, bf16[32,16,128]{2,1,0:T(8,128)(2,1)S(1)}, u32[]{:S(2)}, u32[]{:S(2)}) collective-permute-start(bf16[32,16,128]{2,1,0:T(8,128)(2,1)S(1)} %copy-done), channel_id=1, source_target_pairs={{0,32},{16,48},{32,64},{48,80},{64,96},{80,112},{96,0},{112,16},{1... | collective-permute-start | bytes 393224 | tf_op jit(solution)/shard_map/ppermute | solution.py:101
  49.9 29.3 %collective-permute-start.3 = (bf16[32,16,128]{2,1,0:T(8,128)(2,1)S(1)}, bf16[32,16,128]{2,1,0:T(8,128)(2,1)S(1)}, u32[]{:S(2)}, u32[]{:S(2)}) collective-permute-start(bf16[32,16,128]{2,1,0:T(8,128)(2,1)S(1)} %copy-done), channel_id=1, source_target_pairs={{0,48},{16,64},{32,80},{48,96},{64,112},{80,0},{96,16},{112,32},{1... | collective-permute-start | bytes 393224 | tf_op jit(solution)/shard_map/ppermute | solution.py:101
  53.4 25.8 %collective-permute-start.4 = (bf16[32,16,128]{2,1,0:T(8,128)(2,1)S(1)}, bf16[32,16,128]{2,1,0:T(8,128)(2,1)S(1)}, u32[]{:S(2)}, u32[]{:S(2)}) collective-permute-start(bf16[32,16,128]{2,1,0:T(8,128)(2,1)S(1)} %copy-done), channel_id=1, source_target_pairs={{0,64},{16,80},{32,96},{48,112},{64,0},{80,16},{96,32},{112,48},{1... | collective-permute-start | bytes 393224 | tf_op jit(solution)/shard_map/ppermute | solution.py:101
  56.6 22.7 %collective-permute-start.5 = (bf16[32,16,128]{2,1,0:T(8,128)(2,1)S(1)}, bf16[32,16,128]{2,1,0:T(8,128)(2,1)S(1)}, u32[]{:S(2)}, u32[]{:S(2)}) collective-permute-start(bf16[32,16,128]{2,1,0:T(8,128)(2,1)S(1)} %copy-done), channel_id=1, source_target_pairs={{0,80},{16,96},{32,112},{48,0},{64,16},{80,32},{96,48},{112,64},{1... | collective-permute-start | bytes 393224 | tf_op jit(solution)/shard_map/ppermute | solution.py:101
  58.7 20.5 %copy-start.6 = (bf16[32,16,128]{2,1,0:T(8,128)(2,1)}, bf16[32,16,128]{2,1,0:T(8,128)(2,1)S(1)}, u32[]{:S(2)}) copy-start(bf16[32,16,128]{2,1,0:T(8,128)(2,1)S(1)} %collective-permute-done.1) | copy-start | bytes 393220
  58.7 20.6 %collective-permute-start.6 = (bf16[32,16,128]{2,1,0:T(8,128)(2,1)S(1)}, bf16[32,16,128]{2,1,0:T(8,128)(2,1)S(1)}, u32[]{:S(2)}, u32[]{:S(2)}) collective-permute-start(bf16[32,16,128]{2,1,0:T(8,128)(2,1)S(1)} %copy-done), channel_id=1, source_target_pairs={{0,96},{16,112},{32,0},{48,16},{64,32},{80,48},{96,64},{112,80},{1... | collective-permute-start | bytes 393224 | tf_op jit(solution)/shard_map/ppermute | solution.py:101
  60.4 18.8 %copy-start.8 = (bf16[32,16,128]{2,1,0:T(8,128)(2,1)}, bf16[32,16,128]{2,1,0:T(8,128)(2,1)S(1)}, u32[]{:S(2)}) copy-start(bf16[32,16,128]{2,1,0:T(8,128)(2,1)S(1)} %collective-permute-done.2) | copy-start | bytes 393220
  60.4 18.9 %collective-permute-start.7 = (bf16[32,16,128]{2,1,0:T(8,128)(2,1)S(1)}, bf16[32,16,128]{2,1,0:T(8,128)(2,1)S(1)}, u32[]{:S(2)}, u32[]{:S(2)}) collective-permute-start(bf16[32,16,128]{2,1,0:T(8,128)(2,1)S(1)} %copy-done), channel_id=1, source_target_pairs={{0,112},{16,0},{32,16},{48,32},{64,48},{80,64},{96,80},{112,96},{1... | collective-permute-start | bytes 393224 | tf_op jit(solution)/shard_map/ppermute | solution.py:101
  79.3 31.9 %copy-start.10 = (bf16[32,16,128]{2,1,0:T(8,128)(2,1)}, bf16[32,16,128]{2,1,0:T(8,128)(2,1)S(1)}, u32[]{:S(2)}) copy-start(bf16[32,16,128]{2,1,0:T(8,128)(2,1)S(1)} %collective-permute-done.5) | copy-start | bytes 393220
  79.3 31.9 %copy-start.12 = (bf16[32,16,128]{2,1,0:T(8,128)(2,1)}, bf16[32,16,128]{2,1,0:T(8,128)(2,1)S(1)}, u32[]{:S(2)}) copy-start(bf16[32,16,128]{2,1,0:T(8,128)(2,1)S(1)} %collective-permute-done.6) | copy-start | bytes 393220
  79.9 31.2 %copy-start.14 = (bf16[32,16,128]{2,1,0:T(8,128)(2,1)}, bf16[32,16,128]{2,1,0:T(8,128)(2,1)S(1)}, u32[]{:S(2)}) copy-start(bf16[32,16,128]{2,1,0:T(8,128)(2,1)S(1)} %collective-permute-done.7) | copy-start | bytes 393220
  150.4 2.7 collective-permute-start.8
  213.2 25.1 %copy-start.3 = (bf16[32,16,128]{2,1,0:T(8,128)(2,1)S(1)}, bf16[32,16,128]{2,1,0:T(8,128)(2,1)}, u32[]{:S(2)}) copy-start(bf16[32,16,128]{2,1,0:T(8,128)(2,1)} %copy-done.2) | copy-start | bytes 393220
  213.2 25.1 %copy-start.5 = (bf16[32,16,128]{2,1,0:T(8,128)(2,1)S(1)}, bf16[32,16,128]{2,1,0:T(8,128)(2,1)}, u32[]{:S(2)}) copy-start(bf16[32,16,128]{2,1,0:T(8,128)(2,1)} %copy-done.4) | copy-start | bytes 393220
  214.4 23.9 %copy-start.11 = (bf16[32,16,128]{2,1,0:T(8,128)(2,1)S(1)}, bf16[32,16,128]{2,1,0:T(8,128)(2,1)}, u32[]{:S(2)}) copy-start(bf16[32,16,128]{2,1,0:T(8,128)(2,1)} %copy-done.10) | copy-start | bytes 393220
  214.4 23.9 %copy-start.13 = (bf16[32,16,128]{2,1,0:T(8,128)(2,1)S(1)}, bf16[32,16,128]{2,1,0:T(8,128)(2,1)}, u32[]{:S(2)}) copy-start(bf16[32,16,128]{2,1,0:T(8,128)(2,1)} %copy-done.12) | copy-start | bytes 393220
  214.4 24.0 %copy-start.15 = (bf16[32,16,128]{2,1,0:T(8,128)(2,1)S(1)}, bf16[32,16,128]{2,1,0:T(8,128)(2,1)}, u32[]{:S(2)}) copy-start(bf16[32,16,128]{2,1,0:T(8,128)(2,1)} %copy-done.14) | copy-start | bytes 393220
  214.4 23.8 %all-to-all-start.7 = ((bf16[64,4,16,128]{3,2,1,0:T(8,128)(2,1)}), bf16[64,4,16,128]{3,2,1,0:T(8,128)(2,1)S(1)}, u32[]{:S(2)}, u32[]{:S(2)}) async-start(bf16[64,4,16,128]{3,2,1,0:T(8,128)(2,1)} %broadcast_in_dim.20), calls=%async_computation.7 | async-start | bytes 2097152 | tf_op jit(solution)/shard_map/all_to_all | solution.py:75
  238.2 2.8 collective-permute-start.9
  (7 other events, 17.5 us)

commit v10 on v9

--- a/solution.py
+++ b/solution.py
@@ -95,11 +95,14 @@
     )
     nlive = jnp.clip(counts - rank * slot_dev, 0, slot_dev).astype(jnp.int32)
     local_links = (links + ncol_all // 2 * lax.axis_index("core")) % ncol_all
-    blocks = [integrals]
-    for k in range(1, col_size):
-        ring = [(i, (i + k) % col_size) for i in range(col_size)]
-        blocks.append(lax.ppermute(integrals, "col", ring))
-    owner_of = (rank - jnp.arange(col_size)) % col_size
+    held = integrals[None]
+    bit = 1
+    while bit < col_size:
+        flip = [(i, i ^ bit) for i in range(col_size)]
+        held = jnp.concatenate([held, lax.ppermute(held, "col", flip)], axis=0)
+        bit *= 2
+    blocks = held
+    owner_of = rank ^ jnp.arange(col_size)
     full_energy = pno_energy.reshape(pair_dev, col_size, 1, row_count, 1)
     denom_full = full_energy + pno_energy[:, None, None, None, :] + shift[:, None, None, None, None]
     for sweep in range(SWEEPS):
@@ -107,7 +110,7 @@
         partial = couple(intersections, colamp, local_links, nlive, col_size)
         if sweep == 0:
             partial, blocks = lax.optimization_barrier((partial, blocks))
-            k_full = jnp.take(jnp.stack(blocks), owner_of, axis=0).astype(jnp.float32)
+            k_full = jnp.take(blocks, owner_of, axis=0).astype(jnp.float32)
             weight = k_full / jnp.swapaxes(denom_full[:, :, 0], 0, 1)
         if sweep < SWEEPS - 1:
             parts = lax.all_to_all(partial, "col", 0, 0, tiled=True)

time: 292 us -> 303 us (1.038)
  waiting for transfers between devices: 22.7 us -> 35.3 us
  starting transfers between devices: 21.8 us -> 15.9 us
    ppermute x7 -> x3, waiting for transfers between devices: 0.02 us -> 30.9 us  [per_device(): held = jnp.concatenate([held, lax.ppermute(held, 'col', flip)], axis=0)]
    all_to_all x1, waiting for transfers between devices: 18.2 us -> 0.01 us  [column_amplitudes(): got = lax.all_to_all(sent, ('ph', 'col'), 0, 0, tiled=True)]
    ppermute x7 -> x3, starting transfers between devices: 16.5 us -> 6.56 us  [per_device(): held = jnp.concatenate([held, lax.ppermute(held, 'col', flip)], axis=0)]
    all_to_all x1, starting transfers between devices: 5.27 us -> 9.32 us  [column_amplitudes(): got = lax.all_to_all(sent, ('ph', 'col'), 0, 0, tiled=True)]
    all_to_all x2, blocking collectives: 50.9 us -> 47.2 us  [column_amplitudes(): got = lax.all_to_all(sent, ('ph', 'col'), 0, 0, tiled=True)]
  transfers between devices with their start and end apart: 11 -> 7, of which waited for: 3 -> 5; matrix products, arithmetic and copies ran while one was open for 1% -> 0% of each run, Pallas kernels for 4% -> 0%
where the time goes in v10:
time: 303 us; the launch traced here: 302 us
  blocking collectives  190 us (63%)
  Pallas kernels  38.9 us (13%)
  waiting for transfers between devices  35.3 us (12%)
  starting transfers between devices  15.9 us (5%)
  other arithmetic  9.89 us (3%)
  local copies, waits for them, and re-layouts  7.62 us (3%)
  matrix products  3.21 us (1%)
    all_to_all x2, blocking collectives, per_device(): parts = lax.all_to_all(partial, 'col', 0, 0, tiled=True)  63.7 us
    all_to_all x2, blocking collectives, column_amplitudes(): got = lax.all_to_all(sent, ('ph', 'col'), 0, 0, tiled=True)  47.2 us
    all_to_all x3, blocking collectives, column_amplitudes(): parts = lax.all_to_all(contrib, ('core', 'ph'), 0, 0, tiled=True)  47.2 us
    pallas_call x3, Pallas kernels, couple(): pl.pallas_call(functools.partial(couple_kernel, slot_dev), grid_spec=grid...  38.9 us
    all_to_all x1, blocking collectives, per_device(): lax.all_to_all(jnp.concatenate([partial, extra], axis=1), 'col', 0, 0, ti...  32.2 us
    ppermute x3, waiting for transfers between devices, per_device(): held = jnp.concatenate([held, lax.ppermute(held, 'col', flip)], axis=0)  30.9 us
    all_to_all x1, starting transfers between devices, column_amplitudes(): got = lax.all_to_all(sent, ('ph', 'col'), 0, 0, tiled=True)  9.32 us
    ppermute x3, starting transfers between devices, per_device(): held = jnp.concatenate([held, lax.ppermute(held, 'col', flip)], axis=0)  6.56 us
  transfers between devices with their start and end apart: 7, of which 5 were waited for; matrix products, arithmetic and copies ran while one was open for 0% of the time, Pallas kernels for 0%

profile of v10, /device:TPU:0, one launch (start us, length us, event | category | flops | bytes accessed | tf_op | source)
XLA Modules:
  0.0 302.0 jit_solution(3101399923964697986)
XLA Ops:
  1.4 1.1 fusion.1
  4.0 16.8 %all_to_all.48 = f32[16,4,2048]{2,1,0:T(4,128)S(1)} all-to-all(f32[16,4,2048]{2,1,0:T(4,128)S(1)} %copy.17), channel_id=1, replica_groups=mesh['col'=8,'ph'=8,'core'=2] {'core','ph'}, dimensions={0} | all-to-all | bytes 1048576 | tf_op jit(solution)/shard_map/all_to_all | solution.py:70
  20.9 1.2 broadcast_in_dim.20
  22.2 9.3 %all-to-all-start.1 = ((bf16[64,4,16,128]{3,2,1,0:T(8,128)(2,1)}), bf16[64,4,16,128]{3,2,1,0:T(8,128)(2,1)S(1)}, u32[]{:S(2)}, u32[]{:S(2)}) async-start(bf16[64,4,16,128]{3,2,1,0:T(8,128)(2,1)} %broadcast_in_dim.20), calls=%async_computation.1 | async-start | bytes 2097152 | tf_op jit(solution)/shard_map/all_to_all | solution.py:75
  31.5 3.2 %collective-permute-start.1 = (bf16[1,32,16,128]{3,2,1,0:T(8,128)(2,1)S(1)}, bf16[1,32,16,128]{3,2,1,0:T(8,128)(2,1)S(1)}, u32[]{:S(2)}, u32[]{:S(2)}) collective-permute-start(bf16[1,32,16,128]{3,2,1,0:T(8,128)(2,1)S(1)} %bitcast.47), channel_id=1, source_target_pairs={{0,16},{16,0},{32,48},{48,32},{64,80},{80,64},{96,112},{112,96},{1... | collective-permute-start | bytes 393224 | tf_op jit(solution)/shard_map/ppermute | solution.py:102
  34.7 14.8 %collective-permute-done.1 = bf16[1,32,16,128]{3,2,1,0:T(8,128)(2,1)S(1)} collective-permute-done((bf16[1,32,16,128]{3,2,1,0:T(8,128)(2,1)S(1)}, bf16[1,32,16,128]{3,2,1,0:T(8,128)(2,1)S(1)}, u32[]{:S(2)}, u32[]{:S(2)}) %collective-permute-start.1) | collective-permute-done | bytes 131104 | tf_op jit(solution)/shard_map/ppermute | solution.py:102
  50.4 5.6 %collective-permute-done.2 = bf16[2,32,16,128]{3,2,1,0:T(8,128)(2,1)S(1)} collective-permute-done((bf16[2,32,16,128]{3,2,1,0:T(8,128)(2,1)S(1)}, bf16[2,32,16,128]{3,2,1,0:T(8,128)(2,1)S(1)}, u32[]{:S(2)}, u32[]{:S(2)}) %collective-permute-start.2) | collective-permute-done | bytes 262176 | tf_op jit(solution)/shard_map/ppermute | solution.py:102
  56.1 2.5 collective-permute-start.3
  58.8 10.4 %collective-permute-done.3 = bf16[4,32,16,128]{3,2,1,0:T(8,128)(2,1)S(1)} collective-permute-done((bf16[4,32,16,128]{3,2,1,0:T(8,128)(2,1)S(1)}, bf16[4,32,16,128]{3,2,1,0:T(8,128)(2,1)S(1)}, u32[]{:S(2)}, u32[]{:S(2)}) %collective-permute-start.3) | collective-permute-done | bytes 524320 | tf_op jit(solution)/shard_map/ppermute | solution.py:102
  69.4 1.4 maximum_bitcast_fusion
  71.3 13.0 %shard_map.86 = f32[8,32,16,128]{3,2,1,0:T(8,128)S(1)} custom-call(s32[512]{0:T(512)S(1)} %reshape.184.links_ref, s32[32]{0:T(128)S(1)} %subtract_clamp_fusion.nlive_ref, bf16[32,16,128,128]{3,2,1,0:T(8,128)(2,1)} %tiles_ref.5, bf16[64,128,128]{2,1,0:T(8,128)(2,1)S(1)} %bitcast.45), custom_call_target="tpu_custom_call" | custom-call | flops 4294967296 | bytes 20971520 | tf_op jit(solution)/shard_map/pallas_call | solution.py:50
  84.3 32.6 %all_to_all.49 = f32[8,32,16,128]{3,2,1,0:T(8,128)S(1)} all-to-all(f32[8,32,16,128]{3,2,1,0:T(8,128)S(1)} %shard_map.86), channel_id=1, replica_groups=mesh['col'=8,'ph'=8,'core'=2] {'col'}, dimensions={0} | all-to-all | bytes 4194304 | tf_op jit(solution)/shard_map/all_to_all | solution.py:116
  120.0 16.4 %all_to_all.50 = f32[16,4,2048]{2,1,0:T(4,128)S(1)} all-to-all(f32[16,4,2048]{2,1,0:T(4,128)S(1)} %copy.19), channel_id=1, replica_groups=mesh['col'=8,'ph'=8,'core'=2] {'core','ph'}, dimensions={0} | all-to-all | bytes 1048576 | tf_op jit(solution)/shard_map/all_to_all | solution.py:70
  136.7 23.7 %all_to_all.51 = bf16[64,4,16,128]{3,2,1,0:T(8,128)(2,1)S(1)} all-to-all(bf16[64,4,16,128]{3,2,1,0:T(8,128)(2,1)S(1)} %broadcast_in_dim.22), channel_id=1, replica_groups=mesh['col'=8,'ph'=8,'core'=2] {'ph','col'}, dimensions={0} | all-to-all | bytes 2097152 | tf_op jit(solution)/shard_map/all_to_all | solution.py:75
  160.4 2.7 collective-permute-done.4
  163.9 13.0 %shard_map.87 = f32[8,32,16,128]{3,2,1,0:T(8,128)S(1)} custom-call(s32[512]{0:T(512)S(1)} %reshape.184.links_ref, s32[32]{0:T(128)S(1)} %subtract_clamp_fusion.nlive_ref, bf16[32,16,128,128]{3,2,1,0:T(8,128)(2,1)} %tiles_ref.5, bf16[64,128,128]{2,1,0:T(8,128)(2,1)S(1)} %bitcast.46), custom_call_target="tpu_custom_call" | custom-call | flops 4294967296 | bytes 20971520 | tf_op jit(solution)/shard_map/pallas_call | solution.py:50
  176.8 31.1 %all_to_all.52 = f32[8,32,16,128]{3,2,1,0:T(8,128)S(1)} all-to-all(f32[8,32,16,128]{3,2,1,0:T(8,128)S(1)} %shard_map.87), channel_id=1, replica_groups=mesh['col'=8,'ph'=8,'core'=2] {'col'}, dimensions={0} | all-to-all | bytes 4194304 | tf_op jit(solution)/shard_map/all_to_all | solution.py:116
  210.5 14.0 %all_to_all.53 = f32[16,4,2048]{2,1,0:T(4,128)S(1)} all-to-all(f32[16,4,2048]{2,1,0:T(4,128)S(1)} %copy.21), channel_id=1, replica_groups=mesh['col'=8,'ph'=8,'core'=2] {'core','ph'}, dimensions={0} | all-to-all | bytes 1048576 | tf_op jit(solution)/shard_map/all_to_all | solution.py:70
  224.9 23.5 %all_to_all.54 = bf16[64,4,16,128]{3,2,1,0:T(8,128)(2,1)S(1)} all-to-all(bf16[64,4,16,128]{3,2,1,0:T(8,128)(2,1)S(1)} %broadcast_in_dim.23), channel_id=1, replica_groups=mesh['col'=8,'ph'=8,'core'=2] {'ph','col'}, dimensions={0} | all-to-all | bytes 2097152 | tf_op jit(solution)/shard_map/all_to_all | solution.py:75
  249.3 1.8 collective-permute-done.5
  251.1 1.4 maximum_bitcast_fusion.2
  253.1 13.0 %shard_map.88 = f32[8,32,16,128]{3,2,1,0:T(8,128)S(1)} custom-call(s32[512]{0:T(512)S(1)} %reshape.184.links_ref, s32[32]{0:T(128)S(1)} %subtract_clamp_fusion.nlive_ref, bf16[32,16,128,128]{3,2,1,0:T(8,128)(2,1)} %tiles_ref.5, bf16[64,128,128]{2,1,0:T(8,128)(2,1)S(1)} %bitcast.44), custom_call_target="tpu_custom_call" | custom-call | flops 4294967296 | bytes 20971520 | tf_op jit(solution)/shard_map/pallas_call | solution.py:50
  266.1 1.4 fusion
  267.7 32.2 %all_to_all.55 = f32[8,33,16,128]{3,2,1,0:T(8,128)S(1)} all-to-all(f32[8,33,16,128]{3,2,1,0:T(8,128)S(1)} %pad_maximum_fusion), channel_id=1, replica_groups=mesh['col'=8,'ph'=8,'core'=2] {'col'}, dimensions={0} | all-to-all | bytes 4325376 | tf_op jit(solution)/shard_map/all_to_all | solution.py:123
  (68 shorter events, 15.0 us)
Async XLA Ops:
  1.4 2.6 copy-start.2
  20.8 10.7 %copy-start = (bf16[32,16,128]{2,1,0:T(8,128)(2,1)S(1)}, bf16[32,16,128]{2,1,0:T(8,128)(2,1)}, u32[]{:S(2)}) copy-start(bf16[32,16,128]{2,1,0:T(8,128)(2,1)} %param.9) | copy-start | bytes 393220
  22.2 36.4 %copy-start.5 = (s32[32,16]{0,1:T(8,128)S(1)}, s32[32,16]{0,1:T(8,128)}, u32[]{:S(2)}) copy-start(s32[32,16]{0,1:T(8,128)} %param.13) | copy-start | bytes 6148
  22.2 36.6 %copy-start.6 = (s32[32]{0:T(128)S(1)}, s32[32]{0:T(128)}, u32[]{:S(2)}) copy-start(s32[32]{0:T(128)} %param.14) | copy-start | bytes 388
  22.2 28.2 %all-to-all-start.1 = ((bf16[64,4,16,128]{3,2,1,0:T(8,128)(2,1)}), bf16[64,4,16,128]{3,2,1,0:T(8,128)(2,1)S(1)}, u32[]{:S(2)}, u32[]{:S(2)}) async-start(bf16[64,4,16,128]{3,2,1,0:T(8,128)(2,1)} %broadcast_in_dim.20), calls=%async_computation.1 | async-start | bytes 2097152 | tf_op jit(solution)/shard_map/all_to_all | solution.py:75
  31.5 18.0 %collective-permute-start.1 = (bf16[1,32,16,128]{3,2,1,0:T(8,128)(2,1)S(1)}, bf16[1,32,16,128]{3,2,1,0:T(8,128)(2,1)S(1)}, u32[]{:S(2)}, u32[]{:S(2)}) collective-permute-start(bf16[1,32,16,128]{3,2,1,0:T(8,128)(2,1)S(1)} %bitcast.47), channel_id=1, source_target_pairs={{0,16},{16,0},{32,48},{48,32},{64,80},{80,64},{96,112},{112,96},{1... | collective-permute-start | bytes 393224 | tf_op jit(solution)/shard_map/ppermute | solution.py:102
  49.5 6.5 %collective-permute-start.2 = (bf16[2,32,16,128]{3,2,1,0:T(8,128)(2,1)S(1)}, bf16[2,32,16,128]{3,2,1,0:T(8,128)(2,1)S(1)}, u32[]{:S(2)}, u32[]{:S(2)}) collective-permute-start(bf16[2,32,16,128]{3,2,1,0:T(8,128)(2,1)S(1)} %pad_maximum_fusion.3), channel_id=1, source_target_pairs={{0,32},{16,48},{32,0},{48,16},{64,96},{80,112},{96,64},{112,80},{1... | collective-permute-start | bytes 786440 | tf_op jit(solution)/shard_map/ppermute | solution.py:102
  50.4 18.9 %collective-permute-start = (bf16[64,4,16,128]{3,2,1,0:T(8,128)(2,1)S(1)}, bf16[64,4,16,128]{3,2,1,0:T(8,128)(2,1)}, u32[]{:S(2)}, u32[]{:S(2)}) collective-permute-start(bf16[64,4,16,128]{3,2,1,0:T(8,128)(2,1)S(1)} %all-to-all-done.1), channel_id=1, source_target_pairs={{0,1},{1,0},{2,3},{3,2},{4,5},{5,4},{6,7},{7,6},{8,9},{9,8},{10,11... | collective-permute-start | bytes 3145736 | tf_op jit(solution)/shard_map/ppermute | solution.py:76
  56.1 13.2 %collective-permute-start.3 = (bf16[4,32,16,128]{3,2,1,0:T(8,128)(2,1)S(1)}, bf16[4,32,16,128]{3,2,1,0:T(8,128)(2,1)S(1)}, u32[]{:S(2)}, u32[]{:S(2)}) collective-permute-start(bf16[4,32,16,128]{3,2,1,0:T(8,128)(2,1)S(1)} %pad_maximum_fusion.2), channel_id=1, source_target_pairs={{0,64},{16,80},{32,96},{48,112},{64,0},{80,16},{96,32},{112,48},{1... | collective-permute-start | bytes 1572872 | tf_op jit(solution)/shard_map/ppermute | solution.py:102
  116.9 0.7 copy-start.4
  160.4 2.7 collective-permute-start.4
  224.5 23.8 %copy-start.1 = (f32[32,128]{1,0:T(8,128)S(1)}, f32[32,128]{1,0:T(8,128)}, u32[]{:S(2)}) copy-start(f32[32,128]{1,0:T(8,128)} %param.10) | copy-start | bytes 49156
  248.3 2.8 collective-permute-start.5
  299.9 0.7 copy-start.3

commit v11 on v9

--- a/solution.py
+++ b/solution.py
@@ -110,8 +110,11 @@
             k_full = jnp.take(jnp.stack(blocks), owner_of, axis=0).astype(jnp.float32)
             weight = k_full / jnp.swapaxes(denom_full[:, :, 0], 0, 1)
         if sweep < SWEEPS - 1:
-            parts = lax.all_to_all(partial, "col", 0, 0, tiled=True)
-            coupled = jnp.sum(parts, axis=0)
+            coupled = jnp.take(partial, rank, axis=0)
+            for k in range(1, col_size):
+                ring = [(i, (i + k) % col_size) for i in range(col_size)]
+                piece = jnp.take(partial, (rank + k) % col_size, axis=0)
+                coupled = coupled + lax.ppermute(piece, "col", ring)
         else:
             share = -jnp.sum(weight * partial, axis=(0, 2, 3))
             extra = jnp.zeros((row_count, partial.shape[-1]), jnp.float32)

time: 292 us -> 302 us (1.034)
  blocking collectives: 190 us -> 131 us
  starting transfers between devices: 21.8 us -> 70.6 us
  waiting for transfers between devices: 22.7 us -> 41.7 us
    all_to_all x2 -> x0, blocking collectives: 62.3 us -> none  [per_device(): parts = lax.all_to_all(partial, 'col', 0, 0, tiled=True)]
    ppermute x0 -> x14, starting transfers between devices: none -> 46.7 us  [per_device(): coupled = coupled + lax.ppermute(piece, 'col', ring)]
    ppermute x0 -> x14, waiting for transfers between devices: none -> 19 us  [per_device(): coupled = coupled + lax.ppermute(piece, 'col', ring)]
    all_to_all x2, blocking collectives: 50.9 us -> 54 us  [column_amplitudes(): got = lax.all_to_all(sent, ('ph', 'col'), 0, 0, tiled=True)]
  transfers between devices with their start and end apart: 11 -> 25, of which waited for: 3 -> 10; matrix products, arithmetic and copies ran while one was open for 1% -> 1% of each run, Pallas kernels for 4% -> 4%
where the time goes in v11:
time: 302 us
  blocking collectives  131 us (43%)
  starting transfers between devices  70.6 us (23%)
  waiting for transfers between devices  41.7 us (14%)
  Pallas kernels  38.8 us (13%)
  other arithmetic  9.18 us (3%)
  local copies, waits for them, and re-layouts  7.38 us (2%)
    all_to_all x2, blocking collectives, column_amplitudes(): got = lax.all_to_all(sent, ('ph', 'col'), 0, 0, tiled=True)  54 us
    ppermute x14, starting transfers between devices, per_device(): coupled = coupled + lax.ppermute(piece, 'col', ring)  46.7 us
    all_to_all x3, blocking collectives, column_amplitudes(): parts = lax.all_to_all(contrib, ('core', 'ph'), 0, 0, tiled=True)  45 us
    pallas_call x3, Pallas kernels, couple(): pl.pallas_call(functools.partial(couple_kernel, slot_dev), grid_spec=grid...  38.8 us
    all_to_all x1, blocking collectives, per_device(): lax.all_to_all(jnp.concatenate([partial, extra], axis=1), 'col', 0, 0, ti...  32.2 us
    ppermute x14, waiting for transfers between devices, per_device(): coupled = coupled + lax.ppermute(piece, 'col', ring)  19 us
    all_to_all x1, waiting for transfers between devices, column_amplitudes(): got = lax.all_to_all(sent, ('ph', 'col'), 0, 0, tiled=True)  18.2 us
    ppermute x7, starting transfers between devices, per_device(): blocks.append(lax.ppermute(integrals, 'col', ring))  16.5 us
  transfers between devices with their start and end apart: 25, of which 10 were waited for; matrix products, arithmetic and copies ran while one was open for 1% of the time, Pallas kernels for 4%

profile of v11, /device:TPU:0, one launch (start us, length us, event | category | flops | bytes accessed | tf_op | source)
XLA Modules:
  0.0 301.9 jit_solution(12761104928868950692)
XLA Ops:
  4.0 16.8 %all_to_all.38 = f32[16,4,2048]{2,1,0:T(4,128)S(1)} all-to-all(f32[16,4,2048]{2,1,0:T(4,128)S(1)} %copy.17), channel_id=1, replica_groups=mesh['col'=8,'ph'=8,'core'=2] {'core','ph'}, dimensions={0} | all-to-all | bytes 1048576 | tf_op jit(solution)/shard_map/all_to_all | solution.py:70
  21.2 27.5 %all_to_all.39 = bf16[64,4,16,128]{3,2,1,0:T(8,128)(2,1)S(1)} all-to-all(bf16[64,4,16,128]{3,2,1,0:T(8,128)(2,1)S(1)} %broadcast_in_dim.27), channel_id=1, replica_groups=mesh['col'=8,'ph'=8,'core'=2] {'ph','col'}, dimensions={0} | all-to-all | bytes 2097152 | tf_op jit(solution)/shard_map/all_to_all | solution.py:75
  49.9 3.5 %collective-permute-start.3 = (bf16[32,16,128]{2,1,0:T(8,128)(2,1)S(1)}, bf16[32,16,128]{2,1,0:T(8,128)(2,1)S(1)}, u32[]{:S(2)}, u32[]{:S(2)}) collective-permute-start(bf16[32,16,128]{2,1,0:T(8,128)(2,1)S(1)} %copy-done), channel_id=1, source_target_pairs={{0,48},{16,64},{32,80},{48,96},{64,112},{80,0},{96,16},{112,32},{1... | collective-permute-start | bytes 393224 | tf_op jit(solution)/shard_map/ppermute | solution.py:101
  53.4 3.0 collective-permute-start.4
  60.4 5.9 %collective-permute-start.7 = (bf16[32,16,128]{2,1,0:T(8,128)(2,1)S(1)}, bf16[32,16,128]{2,1,0:T(8,128)(2,1)S(1)}, u32[]{:S(2)}, u32[]{:S(2)}) collective-permute-start(bf16[32,16,128]{2,1,0:T(8,128)(2,1)S(1)} %copy-done), channel_id=1, source_target_pairs={{0,112},{16,0},{32,16},{48,32},{64,48},{80,64},{96,80},{112,96},{1... | collective-permute-start | bytes 393224 | tf_op jit(solution)/shard_map/ppermute | solution.py:101
  66.3 12.9 %shard_map.86 = f32[8,32,16,128]{3,2,1,0:T(8,128)S(1)} custom-call(s32[512]{0:T(512)S(1)} %reshape.218.links_ref, s32[32]{0:T(128)S(1)} %subtract_clamp_fusion.nlive_ref, bf16[32,16,128,128]{3,2,1,0:T(8,128)(2,1)} %tiles_ref.5, bf16[64,128,128]{2,1,0:T(8,128)(2,1)S(1)} %bitcast.119), custom_call_target="tpu_custom_call" | custom-call | flops 4294967296 | bytes 20971520 | tf_op jit(solution)/shard_map/pallas_call | solution.py:50
  82.4 4.5 %collective-permute-start.12 = (f32[32,16,128]{2,1,0:T(8,128)}, f32[32,16,128]{2,1,0:T(8,128)}, u32[]{:S(2)}, u32[]{:S(2)}) collective-permute-start(f32[32,16,128]{2,1,0:T(8,128)} %get-tuple-element.56), channel_id=1, source_target_pairs={{0,80},{16,96},{32,112},{48,0},{64,16},{80,32},{96,48},{112,64},{1... | collective-permute-start | bytes 786440 | tf_op jit(solution)/shard_map/ppermute | solution.py:117
  86.9 5.1 %collective-permute-start.13 = (f32[32,16,128]{2,1,0:T(8,128)}, f32[32,16,128]{2,1,0:T(8,128)}, u32[]{:S(2)}, u32[]{:S(2)}) collective-permute-start(f32[32,16,128]{2,1,0:T(8,128)} %get-tuple-element.55), channel_id=1, source_target_pairs={{0,96},{16,112},{32,0},{48,16},{64,32},{80,48},{96,64},{112,80},{1... | collective-permute-start | bytes 786440 | tf_op jit(solution)/shard_map/ppermute | solution.py:117
  94.0 11.1 %collective-permute-start.8 = (f32[32,16,128]{2,1,0:T(8,128)S(1)}, f32[32,16,128]{2,1,0:T(8,128)}, u32[]{:S(2)}, u32[]{:S(2)}) collective-permute-start(f32[32,16,128]{2,1,0:T(8,128)S(1)} %get-tuple-element.53), channel_id=1, source_target_pairs={{0,16},{16,32},{32,48},{48,64},{64,80},{80,96},{96,112},{112,0},{1... | collective-permute-start | bytes 786440 | tf_op jit(solution)/shard_map/ppermute | solution.py:117
  105.2 5.5 %collective-permute-done.14 = f32[32,16,128]{2,1,0:T(8,128)} collective-permute-done((f32[32,16,128]{2,1,0:T(8,128)}, f32[32,16,128]{2,1,0:T(8,128)}, u32[]{:S(2)}, u32[]{:S(2)}) %collective-permute-start.14) | collective-permute-done | bytes 262176 | tf_op jit(solution)/shard_map/ppermute | solution.py:117
  115.2 13.7 %all_to_all.40 = f32[16,4,2048]{2,1,0:T(4,128)S(1)} all-to-all(f32[16,4,2048]{2,1,0:T(4,128)S(1)} %copy.19), channel_id=1, replica_groups=mesh['col'=8,'ph'=8,'core'=2] {'core','ph'}, dimensions={0} | all-to-all | bytes 1048576 | tf_op jit(solution)/shard_map/all_to_all | solution.py:70
  129.3 26.4 %all_to_all.41 = bf16[64,4,16,128]{3,2,1,0:T(8,128)(2,1)S(1)} all-to-all(bf16[64,4,16,128]{3,2,1,0:T(8,128)(2,1)S(1)} %broadcast_in_dim.28), channel_id=1, replica_groups=mesh['col'=8,'ph'=8,'core'=2] {'ph','col'}, dimensions={0} | all-to-all | bytes 2097152 | tf_op jit(solution)/shard_map/all_to_all | solution.py:75
  155.7 2.7 collective-permute-done.15
  159.2 12.9 %shard_map.87 = f32[8,32,16,128]{3,2,1,0:T(8,128)S(1)} custom-call(s32[512]{0:T(512)S(1)} %reshape.218.links_ref, s32[32]{0:T(128)S(1)} %subtract_clamp_fusion.nlive_ref, bf16[32,16,128,128]{3,2,1,0:T(8,128)(2,1)} %tiles_ref.5, bf16[64,128,128]{2,1,0:T(8,128)(2,1)S(1)} %bitcast.121), custom_call_target="tpu_custom_call" | custom-call | flops 4294967296 | bytes 20971520 | tf_op jit(solution)/shard_map/pallas_call | solution.py:50
  173.5 3.5 %collective-permute-start.18 = (f32[32,16,128]{2,1,0:T(8,128)S(1)}, f32[32,16,128]{2,1,0:T(8,128)S(1)}, u32[]{:S(2)}, u32[]{:S(2)}) collective-permute-start(f32[32,16,128]{2,1,0:T(8,128)S(1)} %get-tuple-element.51), channel_id=1, source_target_pairs={{0,48},{16,64},{32,80},{48,96},{64,112},{80,0},{96,16},{112,32},{1... | collective-permute-start | bytes 786440 | tf_op jit(solution)/shard_map/ppermute | solution.py:117
  177.1 3.0 collective-permute-start.19
  181.3 3.9 %collective-permute-done.16 = f32[32,16,128]{2,1,0:T(8,128)S(1)} collective-permute-done((f32[32,16,128]{2,1,0:T(8,128)S(1)}, f32[32,16,128]{2,1,0:T(8,128)S(1)}, u32[]{:S(2)}, u32[]{:S(2)}) %collective-permute-start.16) | collective-permute-done | bytes 262176 | tf_op jit(solution)/shard_map/ppermute | solution.py:117
  186.4 14.4 %collective-permute-start.22 = (f32[32,16,128]{2,1,0:T(8,128)S(1)}, f32[32,16,128]{2,1,0:T(8,128)S(1)}, u32[]{:S(2)}, u32[]{:S(2)}) collective-permute-start(f32[32,16,128]{2,1,0:T(8,128)S(1)} %get-tuple-element.47), channel_id=1, source_target_pairs={{0,112},{16,0},{32,16},{48,32},{64,48},{80,64},{96,80},{112,96},{1... | collective-permute-start | bytes 786440 | tf_op jit(solution)/shard_map/ppermute | solution.py:117
  201.9 4.2 %collective-permute-done.22 = f32[32,16,128]{2,1,0:T(8,128)S(1)} collective-permute-done((f32[32,16,128]{2,1,0:T(8,128)S(1)}, f32[32,16,128]{2,1,0:T(8,128)S(1)}, u32[]{:S(2)}, u32[]{:S(2)}) %collective-permute-start.22) | collective-permute-done | bytes 262176 | tf_op jit(solution)/shard_map/ppermute | solution.py:117
  207.1 14.4 %all_to_all.42 = f32[16,4,2048]{2,1,0:T(4,128)S(1)} all-to-all(f32[16,4,2048]{2,1,0:T(4,128)S(1)} %copy.21), channel_id=1, replica_groups=mesh['col'=8,'ph'=8,'core'=2] {'core','ph'}, dimensions={0} | all-to-all | bytes 1048576 | tf_op jit(solution)/shard_map/all_to_all | solution.py:70
  223.0 7.3 %all-to-all-start.5 = ((bf16[64,4,16,128]{3,2,1,0:T(8,128)(2,1)}), bf16[64,4,16,128]{3,2,1,0:T(8,128)(2,1)S(1)}, u32[]{:S(2)}, u32[]{:S(2)}) async-start(bf16[64,4,16,128]{3,2,1,0:T(8,128)(2,1)} %broadcast_in_dim.29), calls=%async_computation.5 | async-start | bytes 2097152 | tf_op jit(solution)/shard_map/all_to_all | solution.py:75
  230.7 18.2 %all-to-all-done.5 = bf16[64,4,16,128]{3,2,1,0:T(8,128)(2,1)S(1)} async-done(((bf16[64,4,16,128]{3,2,1,0:T(8,128)(2,1)}), bf16[64,4,16,128]{3,2,1,0:T(8,128)(2,1)S(1)}, u32[]{:S(2)}, u32[]{:S(2)}) %all-to-all-start.5) | async-done | bytes 1048608 | tf_op jit(solution)/shard_map/all_to_all | solution.py:75
  253.6 12.9 %shard_map.88 = f32[8,32,16,128]{3,2,1,0:T(8,128)S(1)} custom-call(s32[512]{0:T(512)S(1)} %reshape.218.links_ref, s32[32]{0:T(128)S(1)} %subtract_clamp_fusion.nlive_ref, bf16[32,16,128,128]{3,2,1,0:T(8,128)(2,1)} %tiles_ref.5, bf16[64,128,128]{2,1,0:T(8,128)(2,1)S(1)} %bitcast.120), custom_call_target="tpu_custom_call" | custom-call | flops 4294967296 | bytes 20971520 | tf_op jit(solution)/shard_map/pallas_call | solution.py:50
  268.2 32.2 %all_to_all.43 = f32[8,33,16,128]{3,2,1,0:T(8,128)S(1)} all-to-all(f32[8,33,16,128]{3,2,1,0:T(8,128)S(1)} %pad_maximum_fusion), channel_id=1, replica_groups=mesh['col'=8,'ph'=8,'core'=2] {'col'}, dimensions={0} | all-to-all | bytes 4325376 | tf_op jit(solution)/shard_map/all_to_all | solution.py:123
  (133 shorter events, 35.0 us)
Async XLA Ops:
  48.7 7.9 %collective-permute-start = (bf16[64,4,16,128]{3,2,1,0:T(8,128)(2,1)S(1)}, bf16[64,4,16,128]{3,2,1,0:T(8,128)(2,1)S(1)}, u32[]{:S(2)}, u32[]{:S(2)}) collective-permute-start(bf16[64,4,16,128]{3,2,1,0:T(8,128)(2,1)S(1)} %all_to_all.39), channel_id=1, source_target_pairs={{0,1},{1,0},{2,3},{3,2},{4,5},{5,4},{6,7},{7,6},{8,9},{9,8},{10,11... | collective-permute-start | bytes 3145736 | tf_op jit(solution)/shard_map/ppermute | solution.py:76
  48.7 9.9 %collective-permute-start.1 = (bf16[32,16,128]{2,1,0:T(8,128)(2,1)S(1)}, bf16[32,16,128]{2,1,0:T(8,128)(2,1)S(1)}, u32[]{:S(2)}, u32[]{:S(2)}) collective-permute-start(bf16[32,16,128]{2,1,0:T(8,128)(2,1)S(1)} %copy-done), channel_id=1, source_target_pairs={{0,16},{16,32},{32,48},{48,64},{64,80},{80,96},{96,112},{112,0},{1... | collective-permute-start | bytes 393224 | tf_op jit(solution)/shard_map/ppermute | solution.py:101
  49.4 11.0 %collective-permute-start.2 = (bf16[32,16,128]{2,1,0:T(8,128)(2,1)S(1)}, bf16[32,16,128]{2,1,0:T(8,128)(2,1)S(1)}, u32[]{:S(2)}, u32[]{:S(2)}) collective-permute-start(bf16[32,16,128]{2,1,0:T(8,128)(2,1)S(1)} %copy-done), channel_id=1, source_target_pairs={{0,32},{16,48},{32,64},{48,80},{64,96},{80,112},{96,0},{112,16},{1... | collective-permute-start | bytes 393224 | tf_op jit(solution)/shard_map/ppermute | solution.py:101
  49.9 29.3 %collective-permute-start.3 = (bf16[32,16,128]{2,1,0:T(8,128)(2,1)S(1)}, bf16[32,16,128]{2,1,0:T(8,128)(2,1)S(1)}, u32[]{:S(2)}, u32[]{:S(2)}) collective-permute-start(bf16[32,16,128]{2,1,0:T(8,128)(2,1)S(1)} %copy-done), channel_id=1, source_target_pairs={{0,48},{16,64},{32,80},{48,96},{64,112},{80,0},{96,16},{112,32},{1... | collective-permute-start | bytes 393224 | tf_op jit(solution)/shard_map/ppermute | solution.py:101
  53.4 25.9 %collective-permute-start.4 = (bf16[32,16,128]{2,1,0:T(8,128)(2,1)S(1)}, bf16[32,16,128]{2,1,0:T(8,128)(2,1)S(1)}, u32[]{:S(2)}, u32[]{:S(2)}) collective-permute-start(bf16[32,16,128]{2,1,0:T(8,128)(2,1)S(1)} %copy-done), channel_id=1, source_target_pairs={{0,64},{16,80},{32,96},{48,112},{64,0},{80,16},{96,32},{112,48},{1... | collective-permute-start | bytes 393224 | tf_op jit(solution)/shard_map/ppermute | solution.py:101
  56.6 22.7 %collective-permute-start.5 = (bf16[32,16,128]{2,1,0:T(8,128)(2,1)S(1)}, bf16[32,16,128]{2,1,0:T(8,128)(2,1)S(1)}, u32[]{:S(2)}, u32[]{:S(2)}) collective-permute-start(bf16[32,16,128]{2,1,0:T(8,128)(2,1)S(1)} %copy-done), channel_id=1, source_target_pairs={{0,80},{16,96},{32,112},{48,0},{64,16},{80,32},{96,48},{112,64},{1... | collective-permute-start | bytes 393224 | tf_op jit(solution)/shard_map/ppermute | solution.py:101
  58.7 20.6 %collective-permute-start.6 = (bf16[32,16,128]{2,1,0:T(8,128)(2,1)S(1)}, bf16[32,16,128]{2,1,0:T(8,128)(2,1)S(1)}, u32[]{:S(2)}, u32[]{:S(2)}) collective-permute-start(bf16[32,16,128]{2,1,0:T(8,128)(2,1)S(1)} %copy-done), channel_id=1, source_target_pairs={{0,96},{16,112},{32,0},{48,16},{64,32},{80,48},{96,64},{112,80},{1... | collective-permute-start | bytes 393224 | tf_op jit(solution)/shard_map/ppermute | solution.py:101
  60.4 19.5 %collective-permute-start.7 = (bf16[32,16,128]{2,1,0:T(8,128)(2,1)S(1)}, bf16[32,16,128]{2,1,0:T(8,128)(2,1)S(1)}, u32[]{:S(2)}, u32[]{:S(2)}) collective-permute-start(bf16[32,16,128]{2,1,0:T(8,128)(2,1)S(1)} %copy-done), channel_id=1, source_target_pairs={{0,112},{16,0},{32,16},{48,32},{64,48},{80,64},{96,80},{112,96},{1... | collective-permute-start | bytes 393224 | tf_op jit(solution)/shard_map/ppermute | solution.py:101
  80.9 13.2 %collective-permute-start.10 = (f32[32,16,128]{2,1,0:T(8,128)S(1)}, f32[32,16,128]{2,1,0:T(8,128)S(1)}, u32[]{:S(2)}, u32[]{:S(2)}) collective-permute-start(f32[32,16,128]{2,1,0:T(8,128)S(1)} %get-tuple-element.58), channel_id=1, source_target_pairs={{0,48},{16,64},{32,80},{48,96},{64,112},{80,0},{96,16},{112,32},{1... | collective-permute-start | bytes 786440 | tf_op jit(solution)/shard_map/ppermute | solution.py:117
  80.9 24.2 %collective-permute-start.11 = (f32[32,16,128]{2,1,0:T(8,128)S(1)}, f32[32,16,128]{2,1,0:T(8,128)S(1)}, u32[]{:S(2)}, u32[]{:S(2)}) collective-permute-start(f32[32,16,128]{2,1,0:T(8,128)S(1)} %get-tuple-element.57), channel_id=1, source_target_pairs={{0,64},{16,80},{32,96},{48,112},{64,0},{80,16},{96,32},{112,48},{1... | collective-permute-start | bytes 786440 | tf_op jit(solution)/shard_map/ppermute | solution.py:117
  82.4 22.8 %collective-permute-start.12 = (f32[32,16,128]{2,1,0:T(8,128)}, f32[32,16,128]{2,1,0:T(8,128)}, u32[]{:S(2)}, u32[]{:S(2)}) collective-permute-start(f32[32,16,128]{2,1,0:T(8,128)} %get-tuple-element.56), channel_id=1, source_target_pairs={{0,80},{16,96},{32,112},{48,0},{64,16},{80,32},{96,48},{112,64},{1... | collective-permute-start | bytes 786440 | tf_op jit(solution)/shard_map/ppermute | solution.py:117
  86.9 18.3 %collective-permute-start.13 = (f32[32,16,128]{2,1,0:T(8,128)}, f32[32,16,128]{2,1,0:T(8,128)}, u32[]{:S(2)}, u32[]{:S(2)}) collective-permute-start(f32[32,16,128]{2,1,0:T(8,128)} %get-tuple-element.55), channel_id=1, source_target_pairs={{0,96},{16,112},{32,0},{48,16},{64,32},{80,48},{96,64},{112,80},{1... | collective-permute-start | bytes 786440 | tf_op jit(solution)/shard_map/ppermute | solution.py:117
  92.0 18.7 %collective-permute-start.14 = (f32[32,16,128]{2,1,0:T(8,128)}, f32[32,16,128]{2,1,0:T(8,128)}, u32[]{:S(2)}, u32[]{:S(2)}) collective-permute-start(f32[32,16,128]{2,1,0:T(8,128)} %get-tuple-element.54), channel_id=1, source_target_pairs={{0,112},{16,0},{32,16},{48,32},{64,48},{80,64},{96,80},{112,96},{1... | collective-permute-start | bytes 786440 | tf_op jit(solution)/shard_map/ppermute | solution.py:117
  94.0 18.5 %collective-permute-start.8 = (f32[32,16,128]{2,1,0:T(8,128)S(1)}, f32[32,16,128]{2,1,0:T(8,128)}, u32[]{:S(2)}, u32[]{:S(2)}) collective-permute-start(f32[32,16,128]{2,1,0:T(8,128)S(1)} %get-tuple-element.53), channel_id=1, source_target_pairs={{0,16},{16,32},{32,48},{48,64},{64,80},{80,96},{96,112},{112,0},{1... | collective-permute-start | bytes 786440 | tf_op jit(solution)/shard_map/ppermute | solution.py:117
  105.1 7.7 %collective-permute-start.9 = (f32[32,16,128]{2,1,0:T(8,128)S(1)}, f32[32,16,128]{2,1,0:T(8,128)}, u32[]{:S(2)}, u32[]{:S(2)}) collective-permute-start(f32[32,16,128]{2,1,0:T(8,128)S(1)} %get-tuple-element.59), channel_id=1, source_target_pairs={{0,32},{16,48},{32,64},{48,80},{64,96},{80,112},{96,0},{112,16},{1... | collective-permute-start | bytes 786440 | tf_op jit(solution)/shard_map/ppermute | solution.py:117
  172.3 12.8 %collective-permute-start.16 = (f32[32,16,128]{2,1,0:T(8,128)S(1)}, f32[32,16,128]{2,1,0:T(8,128)S(1)}, u32[]{:S(2)}, u32[]{:S(2)}) collective-permute-start(f32[32,16,128]{2,1,0:T(8,128)S(1)} %get-tuple-element.46), channel_id=1, source_target_pairs={{0,16},{16,32},{32,48},{48,64},{64,80},{80,96},{96,112},{112,0},{1... | collective-permute-start | bytes 786440 | tf_op jit(solution)/shard_map/ppermute | solution.py:117
  173.0 13.3 %collective-permute-start.17 = (f32[32,16,128]{2,1,0:T(8,128)S(1)}, f32[32,16,128]{2,1,0:T(8,128)S(1)}, u32[]{:S(2)}, u32[]{:S(2)}) collective-permute-start(f32[32,16,128]{2,1,0:T(8,128)S(1)} %get-tuple-element.52), channel_id=1, source_target_pairs={{0,32},{16,48},{32,64},{48,80},{64,96},{80,112},{96,0},{112,16},{1... | collective-permute-start | bytes 786440 | tf_op jit(solution)/shard_map/ppermute | solution.py:117
  173.5 27.2 %collective-permute-start.18 = (f32[32,16,128]{2,1,0:T(8,128)S(1)}, f32[32,16,128]{2,1,0:T(8,128)S(1)}, u32[]{:S(2)}, u32[]{:S(2)}) collective-permute-start(f32[32,16,128]{2,1,0:T(8,128)S(1)} %get-tuple-element.51), channel_id=1, source_target_pairs={{0,48},{16,64},{32,80},{48,96},{64,112},{80,0},{96,16},{112,32},{1... | collective-permute-start | bytes 786440 | tf_op jit(solution)/shard_map/ppermute | solution.py:117
  177.1 23.7 %collective-permute-start.19 = (f32[32,16,128]{2,1,0:T(8,128)S(1)}, f32[32,16,128]{2,1,0:T(8,128)S(1)}, u32[]{:S(2)}, u32[]{:S(2)}) collective-permute-start(f32[32,16,128]{2,1,0:T(8,128)S(1)} %get-tuple-element.50), channel_id=1, source_target_pairs={{0,64},{16,80},{32,96},{48,112},{64,0},{80,16},{96,32},{112,48},{1... | collective-permute-start | bytes 786440 | tf_op jit(solution)/shard_map/ppermute | solution.py:117
  180.1 21.8 %collective-permute-start.20 = (f32[32,16,128]{2,1,0:T(8,128)S(1)}, f32[32,16,128]{2,1,0:T(8,128)S(1)}, u32[]{:S(2)}, u32[]{:S(2)}) collective-permute-start(f32[32,16,128]{2,1,0:T(8,128)S(1)} %get-tuple-element.49), channel_id=1, source_target_pairs={{0,80},{16,96},{32,112},{48,0},{64,16},{80,32},{96,48},{112,64},{1... | collective-permute-start | bytes 786440 | tf_op jit(solution)/shard_map/ppermute | solution.py:117
  185.1 16.7 %collective-permute-start.21 = (f32[32,16,128]{2,1,0:T(8,128)S(1)}, f32[32,16,128]{2,1,0:T(8,128)S(1)}, u32[]{:S(2)}, u32[]{:S(2)}) collective-permute-start(f32[32,16,128]{2,1,0:T(8,128)S(1)} %get-tuple-element.48), channel_id=1, source_target_pairs={{0,96},{16,112},{32,0},{48,16},{64,32},{80,48},{96,64},{112,80},{1... | collective-permute-start | bytes 786440 | tf_op jit(solution)/shard_map/ppermute | solution.py:117
  186.4 19.7 %collective-permute-start.22 = (f32[32,16,128]{2,1,0:T(8,128)S(1)}, f32[32,16,128]{2,1,0:T(8,128)S(1)}, u32[]{:S(2)}, u32[]{:S(2)}) collective-permute-start(f32[32,16,128]{2,1,0:T(8,128)S(1)} %get-tuple-element.47), channel_id=1, source_target_pairs={{0,112},{16,0},{32,16},{48,32},{64,48},{80,64},{96,80},{112,96},{1... | collective-permute-start | bytes 786440 | tf_op jit(solution)/shard_map/ppermute | solution.py:117
  223.0 25.9 %all-to-all-start.5 = ((bf16[64,4,16,128]{3,2,1,0:T(8,128)(2,1)}), bf16[64,4,16,128]{3,2,1,0:T(8,128)(2,1)S(1)}, u32[]{:S(2)}, u32[]{:S(2)}) async-start(bf16[64,4,16,128]{3,2,1,0:T(8,128)(2,1)} %broadcast_in_dim.29), calls=%async_computation.5 | async-start | bytes 2097152 | tf_op jit(solution)/shard_map/all_to_all | solution.py:75
  248.9 2.8 collective-permute-start.23
  (21 other events, 431.5 us)

commit v12 on v9

--- a/solution.py
+++ b/solution.py
@@ -105,7 +105,7 @@
     for sweep in range(SWEEPS):
         colamp = column_amplitudes(amplitudes, one_hot, pair_size, col_size)
         partial = couple(intersections, colamp, local_links, nlive, col_size)
-        if sweep == 0:
+        if sweep == 1:
             partial, blocks = lax.optimization_barrier((partial, blocks))
             k_full = jnp.take(jnp.stack(blocks), owner_of, axis=0).astype(jnp.float32)
             weight = k_full / jnp.swapaxes(denom_full[:, :, 0], 0, 1)

time: 292 us -> 293 us (level)
  transfers between devices with their start and end apart: 11 -> 11, of which waited for: 3 -> 4; matrix products, arithmetic and copies ran while one was open for 1% -> 1% of each run, Pallas kernels for 4% -> 4%
where the time goes in v12:
time: 293 us; the launch traced here: 292 us
  blocking collectives  190 us (65%)
  Pallas kernels  38.8 us (13%)
  waiting for transfers between devices  21.9 us (7%)
  starting transfers between devices  21.7 us (7%)
  local copies, waits for them, and re-layouts  9.69 us (3%)
  other arithmetic  6.97 us (2%)
    all_to_all x2, blocking collectives, per_device(): parts = lax.all_to_all(partial, 'col', 0, 0, tiled=True)  62.3 us
    all_to_all x2, blocking collectives, column_amplitudes(): got = lax.all_to_all(sent, ('ph', 'col'), 0, 0, tiled=True)  51 us
    all_to_all x3, blocking collectives, column_amplitudes(): parts = lax.all_to_all(contrib, ('core', 'ph'), 0, 0, tiled=True)  44.6 us
    pallas_call x3, Pallas kernels, couple(): pl.pallas_call(functools.partial(couple_kernel, slot_dev), grid_spec=grid...  38.8 us
    all_to_all x1, blocking collectives, per_device(): lax.all_to_all(jnp.concatenate([partial, extra], axis=1), 'col', 0, 0, ti...  32.2 us
    all_to_all x1, waiting for transfers between devices, column_amplitudes(): got = lax.all_to_all(sent, ('ph', 'col'), 0, 0, tiled=True)  18.2 us
    ppermute x7, starting transfers between devices, per_device(): blocks.append(lax.ppermute(integrals, 'col', ring))  16.5 us
  transfers between devices with their start and end apart: 11, of which 4 were waited for; matrix products, arithmetic and copies ran while one was open for 1% of the time, Pallas kernels for 4%

profile of v12, /device:TPU:0, one launch (start us, length us, event | category | flops | bytes accessed | tf_op | source)
XLA Modules:
  0.0 292.1 jit_solution(1221518955439883949)
XLA Ops:
  1.4 1.1 fusion.1
  2.6 1.1 fusion.12
  4.0 16.8 %all_to_all.48 = f32[16,4,2048]{2,1,0:T(4,128)S(1)} all-to-all(f32[16,4,2048]{2,1,0:T(4,128)S(1)} %copy.17), channel_id=1, replica_groups=mesh['col'=8,'ph'=8,'core'=2] {'core','ph'}, dimensions={0} | all-to-all | bytes 1048576 | tf_op jit(solution)/shard_map/all_to_all | solution.py:70
  21.2 27.5 %all_to_all.49 = bf16[64,4,16,128]{3,2,1,0:T(8,128)(2,1)S(1)} all-to-all(bf16[64,4,16,128]{3,2,1,0:T(8,128)(2,1)S(1)} %broadcast_in_dim.15), channel_id=1, replica_groups=mesh['col'=8,'ph'=8,'core'=2] {'ph','col'}, dimensions={0} | all-to-all | bytes 2097152 | tf_op jit(solution)/shard_map/all_to_all | solution.py:75
  48.9 2.5 collective-permute-done
  52.1 12.9 %shard_map.86 = f32[8,32,16,128]{3,2,1,0:T(8,128)S(1)} custom-call(s32[512]{0:T(512)S(1)} %reshape.217.links_ref, s32[32]{0:T(128)S(1)} %subtract_clamp_fusion.nlive_ref, bf16[32,16,128,128]{3,2,1,0:T(8,128)(2,1)} %tiles_ref.5, bf16[64,128,128]{2,1,0:T(8,128)(2,1)S(1)} %bitcast.61), custom_call_target="tpu_custom_call" | custom-call | flops 4294967296 | bytes 20971520 | tf_op jit(solution)/shard_map/pallas_call | solution.py:50
  65.1 31.1 %all_to_all.50 = f32[8,32,16,128]{3,2,1,0:T(8,128)S(1)} all-to-all(f32[8,32,16,128]{3,2,1,0:T(8,128)S(1)} %shard_map.86), channel_id=1, replica_groups=mesh['col'=8,'ph'=8,'core'=2] {'col'}, dimensions={0} | all-to-all | bytes 4194304 | tf_op jit(solution)/shard_map/all_to_all | solution.py:113
  98.1 14.0 %all_to_all.51 = f32[16,4,2048]{2,1,0:T(4,128)S(1)} all-to-all(f32[16,4,2048]{2,1,0:T(4,128)S(1)} %copy.19), channel_id=1, replica_groups=mesh['col'=8,'ph'=8,'core'=2] {'core','ph'}, dimensions={0} | all-to-all | bytes 1048576 | tf_op jit(solution)/shard_map/all_to_all | solution.py:70
  112.5 23.5 %all_to_all.52 = bf16[64,4,16,128]{3,2,1,0:T(8,128)(2,1)S(1)} all-to-all(bf16[64,4,16,128]{3,2,1,0:T(8,128)(2,1)S(1)} %broadcast_in_dim.16), channel_id=1, replica_groups=mesh['col'=8,'ph'=8,'core'=2] {'ph','col'}, dimensions={0} | all-to-all | bytes 2097152 | tf_op jit(solution)/shard_map/all_to_all | solution.py:75
  137.2 3.5 %collective-permute-start.4 = (bf16[32,16,128]{2,1,0:T(8,128)(2,1)S(1)}, bf16[32,16,128]{2,1,0:T(8,128)(2,1)S(1)}, u32[]{:S(2)}, u32[]{:S(2)}) collective-permute-start(bf16[32,16,128]{2,1,0:T(8,128)(2,1)S(1)} %copy-done), channel_id=1, source_target_pairs={{0,48},{16,64},{32,80},{48,96},{64,112},{80,0},{96,16},{112,32},{1... | collective-permute-start | bytes 393224 | tf_op jit(solution)/shard_map/ppermute | solution.py:101
  140.7 3.0 %collective-permute-start.5 = (bf16[32,16,128]{2,1,0:T(8,128)(2,1)S(1)}, bf16[32,16,128]{2,1,0:T(8,128)(2,1)S(1)}, u32[]{:S(2)}, u32[]{:S(2)}) collective-permute-start(bf16[32,16,128]{2,1,0:T(8,128)(2,1)S(1)} %copy-done), channel_id=1, source_target_pairs={{0,64},{16,80},{32,96},{48,112},{64,0},{80,16},{96,32},{112,48},{1... | collective-permute-start | bytes 393224 | tf_op jit(solution)/shard_map/ppermute | solution.py:101
  143.7 1.2 collective-permute-start.6
  145.9 1.5 collective-permute-start.7
  147.4 6.1 %collective-permute-start.8 = (bf16[32,16,128]{2,1,0:T(8,128)(2,1)S(1)}, bf16[32,16,128]{2,1,0:T(8,128)(2,1)}, u32[]{:S(2)}, u32[]{:S(2)}) collective-permute-start(bf16[32,16,128]{2,1,0:T(8,128)(2,1)S(1)} %copy-done), channel_id=1, source_target_pairs={{0,112},{16,0},{32,16},{48,32},{64,48},{80,64},{96,80},{112,96},{1... | collective-permute-start | bytes 393224 | tf_op jit(solution)/shard_map/ppermute | solution.py:101
  153.5 12.9 %shard_map.87 = f32[8,32,16,128]{3,2,1,0:T(8,128)S(1)} custom-call(s32[512]{0:T(512)S(1)} %reshape.217.links_ref, s32[32]{0:T(128)S(1)} %subtract_clamp_fusion.nlive_ref, bf16[32,16,128,128]{3,2,1,0:T(8,128)(2,1)} %tiles_ref.5, bf16[64,128,128]{2,1,0:T(8,128)(2,1)S(1)} %bitcast.59), custom_call_target="tpu_custom_call" | custom-call | flops 4294967296 | bytes 20971520 | tf_op jit(solution)/shard_map/pallas_call | solution.py:50
  167.9 31.2 %all_to_all.53 = f32[8,32,16,128]{3,2,1,0:T(8,128)S(1)} all-to-all(f32[8,32,16,128]{3,2,1,0:T(8,128)S(1)} %shard_map.87), channel_id=1, replica_groups=mesh['col'=8,'ph'=8,'core'=2] {'col'}, dimensions={0} | all-to-all | bytes 4194304 | tf_op jit(solution)/shard_map/all_to_all | solution.py:113
  200.3 13.7 %all_to_all.54 = f32[16,4,2048]{2,1,0:T(4,128)S(1)} all-to-all(f32[16,4,2048]{2,1,0:T(4,128)S(1)} %copy.21), channel_id=1, replica_groups=mesh['col'=8,'ph'=8,'core'=2] {'core','ph'}, dimensions={0} | all-to-all | bytes 1048576 | tf_op jit(solution)/shard_map/all_to_all | solution.py:70
  214.2 1.2 broadcast_in_dim.20
  215.4 5.2 %all-to-all-start.7 = ((bf16[64,4,16,128]{3,2,1,0:T(8,128)(2,1)}), bf16[64,4,16,128]{3,2,1,0:T(8,128)(2,1)S(1)}, u32[]{:S(2)}, u32[]{:S(2)}) async-start(bf16[64,4,16,128]{3,2,1,0:T(8,128)(2,1)} %broadcast_in_dim.20), calls=%async_computation.7 | async-start | bytes 2097152 | tf_op jit(solution)/shard_map/all_to_all | solution.py:75
  220.9 18.2 %all-to-all-done.7 = bf16[64,4,16,128]{3,2,1,0:T(8,128)(2,1)S(1)} async-done(((bf16[64,4,16,128]{3,2,1,0:T(8,128)(2,1)}), bf16[64,4,16,128]{3,2,1,0:T(8,128)(2,1)S(1)}, u32[]{:S(2)}, u32[]{:S(2)}) %all-to-all-start.7) | async-done | bytes 1048608 | tf_op jit(solution)/shard_map/all_to_all | solution.py:75
  241.9 1.4 maximum_bitcast_fusion.2
  243.9 12.9 %shard_map.88 = f32[8,32,16,128]{3,2,1,0:T(8,128)S(1)} custom-call(s32[512]{0:T(512)S(1)} %reshape.217.links_ref, s32[32]{0:T(128)S(1)} %subtract_clamp_fusion.nlive_ref, bf16[32,16,128,128]{3,2,1,0:T(8,128)(2,1)} %tiles_ref.5, bf16[64,128,128]{2,1,0:T(8,128)(2,1)S(1)} %bitcast.60), custom_call_target="tpu_custom_call" | custom-call | flops 4294967296 | bytes 20971520 | tf_op jit(solution)/shard_map/pallas_call | solution.py:50
  256.8 1.4 fusion
  258.4 32.2 %all_to_all.55 = f32[8,33,16,128]{3,2,1,0:T(8,128)S(1)} all-to-all(f32[8,33,16,128]{3,2,1,0:T(8,128)S(1)} %pad_maximum_fusion), channel_id=1, replica_groups=mesh['col'=8,'ph'=8,'core'=2] {'col'}, dimensions={0} | all-to-all | bytes 4325376 | tf_op jit(solution)/shard_map/all_to_all | solution.py:120
  (103 shorter events, 14.8 us)
Async XLA Ops:
  20.8 27.9 %copy-start.15 = (s32[32,16]{0,1:T(8,128)S(1)}, s32[32,16]{0,1:T(8,128)}, u32[]{:S(2)}) copy-start(s32[32,16]{0,1:T(8,128)} %param.13) | copy-start | bytes 6148
  20.8 28.1 %copy-start.17 = (s32[32]{0:T(128)S(1)}, s32[32]{0:T(128)}, u32[]{:S(2)}) copy-start(s32[32]{0:T(128)} %param.14) | copy-start | bytes 388
  48.7 2.7 collective-permute-start
  96.2 0.9 copy-start.14
  96.2 1.1 copy-start.16
  136.0 7.7 %collective-permute-start.1 = (bf16[64,4,16,128]{3,2,1,0:T(8,128)(2,1)S(1)}, bf16[64,4,16,128]{3,2,1,0:T(8,128)(2,1)S(1)}, u32[]{:S(2)}, u32[]{:S(2)}) collective-permute-start(bf16[64,4,16,128]{3,2,1,0:T(8,128)(2,1)S(1)} %all_to_all.52), channel_id=1, source_target_pairs={{0,1},{1,0},{2,3},{3,2},{4,5},{5,4},{6,7},{7,6},{8,9},{9,8},{10,11... | collective-permute-start | bytes 3145736 | tf_op jit(solution)/shard_map/ppermute | solution.py:76
  136.0 9.9 %collective-permute-start.2 = (bf16[32,16,128]{2,1,0:T(8,128)(2,1)S(1)}, bf16[32,16,128]{2,1,0:T(8,128)(2,1)S(1)}, u32[]{:S(2)}, u32[]{:S(2)}) collective-permute-start(bf16[32,16,128]{2,1,0:T(8,128)(2,1)S(1)} %copy-done), channel_id=1, source_target_pairs={{0,16},{16,32},{32,48},{48,64},{64,80},{80,96},{96,112},{112,0},{1... | collective-permute-start | bytes 393224 | tf_op jit(solution)/shard_map/ppermute | solution.py:101
  136.6 10.8 %collective-permute-start.3 = (bf16[32,16,128]{2,1,0:T(8,128)(2,1)S(1)}, bf16[32,16,128]{2,1,0:T(8,128)(2,1)S(1)}, u32[]{:S(2)}, u32[]{:S(2)}) collective-permute-start(bf16[32,16,128]{2,1,0:T(8,128)(2,1)S(1)} %copy-done), channel_id=1, source_target_pairs={{0,32},{16,48},{32,64},{48,80},{64,96},{80,112},{96,0},{112,16},{1... | collective-permute-start | bytes 393224 | tf_op jit(solution)/shard_map/ppermute | solution.py:101
  137.2 29.3 %collective-permute-start.4 = (bf16[32,16,128]{2,1,0:T(8,128)(2,1)S(1)}, bf16[32,16,128]{2,1,0:T(8,128)(2,1)S(1)}, u32[]{:S(2)}, u32[]{:S(2)}) collective-permute-start(bf16[32,16,128]{2,1,0:T(8,128)(2,1)S(1)} %copy-done), channel_id=1, source_target_pairs={{0,48},{16,64},{32,80},{48,96},{64,112},{80,0},{96,16},{112,32},{1... | collective-permute-start | bytes 393224 | tf_op jit(solution)/shard_map/ppermute | solution.py:101
  140.7 25.8 %collective-permute-start.5 = (bf16[32,16,128]{2,1,0:T(8,128)(2,1)S(1)}, bf16[32,16,128]{2,1,0:T(8,128)(2,1)S(1)}, u32[]{:S(2)}, u32[]{:S(2)}) collective-permute-start(bf16[32,16,128]{2,1,0:T(8,128)(2,1)S(1)} %copy-done), channel_id=1, source_target_pairs={{0,64},{16,80},{32,96},{48,112},{64,0},{80,16},{96,32},{112,48},{1... | collective-permute-start | bytes 393224 | tf_op jit(solution)/shard_map/ppermute | solution.py:101
  143.7 22.9 %collective-permute-start.6 = (bf16[32,16,128]{2,1,0:T(8,128)(2,1)S(1)}, bf16[32,16,128]{2,1,0:T(8,128)(2,1)S(1)}, u32[]{:S(2)}, u32[]{:S(2)}) collective-permute-start(bf16[32,16,128]{2,1,0:T(8,128)(2,1)S(1)} %copy-done), channel_id=1, source_target_pairs={{0,80},{16,96},{32,112},{48,0},{64,16},{80,32},{96,48},{112,64},{1... | collective-permute-start | bytes 393224 | tf_op jit(solution)/shard_map/ppermute | solution.py:101
  145.9 20.6 %copy-start.8 = (bf16[32,16,128]{2,1,0:T(8,128)(2,1)}, bf16[32,16,128]{2,1,0:T(8,128)(2,1)S(1)}, u32[]{:S(2)}) copy-start(bf16[32,16,128]{2,1,0:T(8,128)(2,1)S(1)} %collective-permute-done.2) | copy-start | bytes 393220
  145.9 20.7 %collective-permute-start.7 = (bf16[32,16,128]{2,1,0:T(8,128)(2,1)S(1)}, bf16[32,16,128]{2,1,0:T(8,128)(2,1)S(1)}, u32[]{:S(2)}, u32[]{:S(2)}) collective-permute-start(bf16[32,16,128]{2,1,0:T(8,128)(2,1)S(1)} %copy-done), channel_id=1, source_target_pairs={{0,96},{16,112},{32,0},{48,16},{64,32},{80,48},{96,64},{112,80},{1... | collective-permute-start | bytes 393224 | tf_op jit(solution)/shard_map/ppermute | solution.py:101
  147.4 19.1 %copy-start.10 = (bf16[32,16,128]{2,1,0:T(8,128)(2,1)}, bf16[32,16,128]{2,1,0:T(8,128)(2,1)S(1)}, u32[]{:S(2)}) copy-start(bf16[32,16,128]{2,1,0:T(8,128)(2,1)S(1)} %collective-permute-done.3) | copy-start | bytes 393220
  147.4 20.5 %collective-permute-start.8 = (bf16[32,16,128]{2,1,0:T(8,128)(2,1)S(1)}, bf16[32,16,128]{2,1,0:T(8,128)(2,1)}, u32[]{:S(2)}, u32[]{:S(2)}) collective-permute-start(bf16[32,16,128]{2,1,0:T(8,128)(2,1)S(1)} %copy-done), channel_id=1, source_target_pairs={{0,112},{16,0},{32,16},{48,32},{64,48},{80,64},{96,80},{112,96},{1... | collective-permute-start | bytes 393224 | tf_op jit(solution)/shard_map/ppermute | solution.py:101
  166.5 32.6 %copy-start.2 = (bf16[32,16,128]{2,1,0:T(8,128)(2,1)}, bf16[32,16,128]{2,1,0:T(8,128)(2,1)S(1)}, u32[]{:S(2)}) copy-start(bf16[32,16,128]{2,1,0:T(8,128)(2,1)S(1)} %collective-permute-done.4) | copy-start | bytes 393220
  214.0 6.8 %copy-start.9 = (bf16[32,16,128]{2,1,0:T(8,128)(2,1)S(1)}, bf16[32,16,128]{2,1,0:T(8,128)(2,1)}, u32[]{:S(2)}) copy-start(bf16[32,16,128]{2,1,0:T(8,128)(2,1)} %copy-done.8) | copy-start | bytes 393220
  214.1 6.7 %copy-start.11 = (bf16[32,16,128]{2,1,0:T(8,128)(2,1)S(1)}, bf16[32,16,128]{2,1,0:T(8,128)(2,1)}, u32[]{:S(2)}) copy-start(bf16[32,16,128]{2,1,0:T(8,128)(2,1)} %copy-done.10) | copy-start | bytes 393220
  214.1 25.0 %copy-start.3 = (bf16[32,16,128]{2,1,0:T(8,128)(2,1)S(1)}, bf16[32,16,128]{2,1,0:T(8,128)(2,1)}, u32[]{:S(2)}) copy-start(bf16[32,16,128]{2,1,0:T(8,128)(2,1)} %copy-done.2) | copy-start | bytes 393220
  214.2 25.0 %copy-start.5 = (bf16[32,16,128]{2,1,0:T(8,128)(2,1)S(1)}, bf16[32,16,128]{2,1,0:T(8,128)(2,1)}, u32[]{:S(2)}) copy-start(bf16[32,16,128]{2,1,0:T(8,128)(2,1)} %copy-done.4) | copy-start | bytes 393220
  215.4 23.8 %copy-start.7 = (bf16[32,16,128]{2,1,0:T(8,128)(2,1)S(1)}, bf16[32,16,128]{2,1,0:T(8,128)(2,1)}, u32[]{:S(2)}) copy-start(bf16[32,16,128]{2,1,0:T(8,128)(2,1)} %copy-done.6) | copy-start | bytes 393220
  215.4 23.8 %copy-start.13 = (bf16[32,16,128]{2,1,0:T(8,128)(2,1)S(1)}, bf16[32,16,128]{2,1,0:T(8,128)(2,1)}, u32[]{:S(2)}) copy-start(bf16[32,16,128]{2,1,0:T(8,128)(2,1)} %copy-done.12) | copy-start | bytes 393220
  215.4 23.7 %all-to-all-start.7 = ((bf16[64,4,16,128]{3,2,1,0:T(8,128)(2,1)}), bf16[64,4,16,128]{3,2,1,0:T(8,128)(2,1)S(1)}, u32[]{:S(2)}, u32[]{:S(2)}) async-start(bf16[64,4,16,128]{3,2,1,0:T(8,128)(2,1)} %broadcast_in_dim.20), calls=%async_computation.7 | async-start | bytes 2097152 | tf_op jit(solution)/shard_map/all_to_all | solution.py:75
  239.1 2.8 collective-permute-start.9
  (5 other events, 3.9 us)
